TPU v7x, 768 devices: a whole 4x8x12 slice. The times are simulated.
768 devices in a mesh: sample: 32 (over z_lo, y), sect: 8 (over x, core), dom: 3 (over z_hi).
Axes of the slice: x: 4, y: 8, z: 12 (z_hi: 3, z_lo: 4; z = z_hi * 4 + z_lo), core: 2. Of those that a mesh axis runs over, the one named last changes fastest.
Arguments:
- features: bfloat16 [96, 512, 512], P(('sample', 'dom'), 'sect'), may hold values from -6 to 6
- weight: bfloat16 [4608, 512], P('sample', 'sect'), may hold values from -0.09375 to 0.09375
- style: float32 [96, 512], P(('sample', 'dom')), may hold values from 0.3 to 3
- bias: float32 [512], P('sect'), may hold values from -3 to 3
- adjoint: bfloat16 [96, 512, 512], P(('sample', 'dom'), 'sect'), may hold values from -6 to 6
Outputs:
- styled: bfloat16 [96, 512, 512], P(('sample', 'dom'), 'sect')
- grad_weight: float32 [4608, 512], P(('sample', 'dom'), 'sect')
- grad_features: bfloat16 [96, 512, 512], P(('sample', 'dom'), 'sect')
All inputs are finite; a program needn't handle non-finite values.
Results may differ from a plain program's by a relative error of at most 0.0049.
Values may be sent and summed in bfloat16 or wider, within the bound.
No kernel may reach another device: no remote copies, remote signals or barrier semaphores. Data moves between devices by JAX's collectives and lax.ppermute only.
A program may use at most 32 MiB of HBM per device.

v0:
```python
import jax
import jax.numpy as jnp
from jax import lax
from jax.sharding import PartitionSpec as P

WIDTH = 64
ROWS = 8


OFFSETS = [(-1, -1), (-1, 0), (-1, 1), (0, -1), (0, 0), (0, 1), (1, -1), (1, 0), (1, 1)]
EPSILON = 1e-08


def moved(array, row_step, col_step):
    count = array.shape[0]
    depth = array.shape[1]
    grid = array.reshape(count, depth, ROWS, WIDTH)
    padded = jnp.pad(grid, ((0, 0), (0, 0), (1, 1), (1, 1)))
    part = padded[:, :, 1 + row_step : 1 + row_step + ROWS, 1 + col_step : 1 + col_step + WIDTH]
    return part.reshape(count, depth, ROWS * WIDTH)


def per_device(features, weight, style, bias, adjoint):
    local_ch = features.shape[1]
    sect_count = lax.axis_size("sect")
    sect_place = lax.axis_index("sect")
    channels = local_ch * sect_count
    samples = features.shape[0]
    pixels = features.shape[2]
    own_style = lax.dynamic_slice_in_dim(style, sect_place * local_ch, local_ch, 1)
    local_mod = (features.astype(jnp.float32) * own_style[:, :, None]).astype(jnp.bfloat16)
    modulated = lax.all_gather(local_mod, "sect", axis=1, tiled=True)
    full_weight = lax.all_gather(weight, "sample", axis=0, tiled=True)
    kernel = full_weight.reshape(9, channels, local_ch)
    kernel_f = kernel.astype(jnp.float32)
    shifts = [moved(modulated, row_step, col_step) for row_step, col_step in OFFSETS]
    conv_out = jnp.zeros(features.shape, jnp.float32)
    for index in range(9):
        conv_out = conv_out + jnp.einsum(
            "nip,io->nop", shifts[index], kernel[index], preferred_element_type=jnp.float32
        )
    kernel_sq = jnp.sum(kernel_f * kernel_f, axis=0)
    style_sq = style * style
    energy = jnp.dot(style_sq, kernel_sq, precision=lax.Precision.HIGHEST) + EPSILON
    demod = lax.rsqrt(energy)
    styled = (conv_out * demod[:, :, None] + bias[None, :, None]).astype(jnp.bfloat16)
    adjoint_f = adjoint.astype(jnp.float32)
    scaled_adjoint = (adjoint_f * demod[:, :, None]).astype(jnp.bfloat16)
    demod_grad = jnp.sum(adjoint_f * conv_out, axis=2)
    energy_grad = -0.5 * demod_grad * demod * demod * demod
    coupling = jnp.dot(style_sq.T, energy_grad, precision=lax.Precision.HIGHEST)
    grads = []
    for index in range(9):
        grads.append(
            jnp.einsum(
                "nip,nop->io", shifts[index], scaled_adjoint, preferred_element_type=jnp.float32
            )
            + 2.0 * kernel_f[index] * coupling
        )
    grad_terms = jnp.concatenate(grads, axis=0)
    grad_weight = lax.psum_scatter(grad_terms, ("sample", "dom"), scatter_dimension=0, tiled=True)
    back = jnp.zeros((samples, channels, pixels), jnp.float32)
    for index in range(9):
        row_step, col_step = OFFSETS[index]
        partial_back = jnp.einsum(
            "nop,io->nip", scaled_adjoint, kernel[index], preferred_element_type=jnp.float32
        )
        back = back + moved(partial_back, -row_step, -col_step)
    summed = lax.psum_scatter(back, "sect", scatter_dimension=1, tiled=True)
    grad_features = (summed * own_style[:, :, None]).astype(jnp.bfloat16)
    return (styled, grad_weight, grad_features)


def solution(mesh):
    in_specs = (
        P(("sample", "dom"), "sect", None),
        P("sample", "sect"),
        P(("sample", "dom"), None),
        P("sect"),
        P(("sample", "dom"), "sect", None),
    )
    out_specs = (
        P(("sample", "dom"), "sect", None),
        P(("sample", "dom"), "sect"),
        P(("sample", "dom"), "sect", None),
    )
    return jax.shard_map(
        per_device, mesh=mesh, in_specs=in_specs, out_specs=out_specs, check_vma=False
    )
```

profile of v0, /device:TPU:68, one launch (start us, length us, event | category | flops | bytes accessed | tf_op | source)
XLA Modules:
  0.0 761.4 jit_solution(10721364764257090956)
XLA Ops:
  8.8 0.9 multiply_convert_fusion
  9.7 11.9 %all_gather.6 = bf16[1,512,512]{2,1,0:T(8,128)(2,1)S(1)} all-gather(bf16[1,64,512]{2,1,0:T(8,128)(2,1)S(1)} %multiply_convert_fusion), channel_id=1, replica_groups=mesh['sample'=32,'sect'=8,'dom'=3] {'sect'}, dimensions={1}, use_global_device_ids=true | all-gather | bytes 589824 | tf_op jit(solution)/shard_map/all_gather | solution.py:32
  21.8 1.7 pad_slice_fusion.8
  23.5 72.3 %all-gather = bf16[32,144,64]{1,2,0:T(8,128)(2,1)S(1)} all-gather(bf16[1,144,64]{1,2,0:T(8,128)(2,1)S(1)} %bitcast.212), channel_id=1, replica_groups=mesh['sample'=32,'sect'=8,'dom'=3] {'sample'}, dimensions={0}, use_global_device_ids=true | all-gather | bytes 608256 | tf_op jit(solution)/shard_map/all_gather | solution.py:33
  95.8 1.6 copy.45
  97.4 2.6 reshape.342
  100.0 1.1 convert_multiply_fusion
  101.4 0.9 fusion.55
  102.4 0.9 fusion.58
  103.3 0.9 fusion.69
  104.2 1.5 mul.145
  106.6 1.4 convolution_add_fusion.13
  108.0 1.3 convolution_add_fusion.12
  114.6 2.0 copy.54
  117.6 0.9 fusion.13
  121.3 0.9 fusion.17
  122.2 0.9 fusion.9
  123.1 0.9 fusion.8
  124.1 0.9 fusion.7
  125.0 0.9 fusion.6
  125.9 2.9 copy.57
  128.8 1.3 dynamic-slice
  131.4 74.4 %all-reduce.12.cloned.1.call-done = f32[1,512,512]{2,0,1:T(1,128)} async-done(((f32[1,512,512]{2,0,1:T(1,128)}), f32[1,512,512]{2,0,1:T(1,128)}) %all-reduce.12.cloned.1.call-update) | async-done | bytes 1048592
  207.4 546.5 %reduce-scatter.4.cloned.1.call-done = f32[48,64]{1,0:T(8,128)} async-done(((f32[4608,64]{1,0:T(8,128)}), f32[48,64]{1,0:T(8,128)}) %reduce-scatter.4.cloned.1.call-update) | async-done | bytes 12304
  (73 shorter events, 13.3 us)
Async XLA Ops:
  8.0 197.8 %all-reduce.12.cloned.1.call-start = ((), (), s32[]{:S(2)}) async-start(), calls=%async_computation.2 | async-start | bytes 2097152
  21.8 1.7 copy-start.15
  23.5 77.6 %copy-start.2 = (bf16[1,512,8,64]{1,3,2,0:T(8,128)(2,1)}, bf16[1,512,8,64]{1,3,2,0:T(8,128)(2,1)S(1)}, u32[]{:S(2)}) copy-start(bf16[1,512,8,64]{1,3,2,0:T(8,128)(2,1)S(1)} %get-tuple-element.21) | copy-start | bytes 1572868
  23.5 77.9 %copy-start.4 = (bf16[1,512,8,64]{1,3,2,0:T(8,128)(2,1)}, bf16[1,512,8,64]{1,3,2,0:T(8,128)(2,1)S(1)}, u32[]{:S(2)}) copy-start(bf16[1,512,8,64]{1,3,2,0:T(8,128)(2,1)S(1)} %get-tuple-element.20) | copy-start | bytes 1572868
  23.5 78.9 %copy-start.6 = (bf16[1,512,8,64]{1,3,2,0:T(8,128)(2,1)}, bf16[1,512,8,64]{1,3,2,0:T(8,128)(2,1)S(1)}, u32[]{:S(2)}) copy-start(bf16[1,512,8,64]{1,3,2,0:T(8,128)(2,1)S(1)} %get-tuple-element.19) | copy-start | bytes 1572868
  23.5 79.8 %copy-start.11 = (bf16[1,512,8,64]{1,3,2,0:T(8,128)(2,1)}, bf16[1,512,8,64]{1,3,2,0:T(8,128)(2,1)S(1)}, u32[]{:S(2)}) copy-start(bf16[1,512,8,64]{1,3,2,0:T(8,128)(2,1)S(1)} %get-tuple-element.22) | copy-start | bytes 1572868
  105.7 0.7 copy-start.16
  106.4 3.0 copy-start.8
  106.6 3.1 copy-start.13
  106.6 3.1 copy-start.14
  109.4 1.0 copy-start.1
  109.7 1.0 copy-start
  116.6 1.0 copy-start.12
  116.6 1.9 copy-start.10
  116.6 637.3 %reduce-scatter.4.cloned.1.call-start = ((), (), s32[]{:S(2)}) async-start(), calls=%async_computation.1 | async-start | bytes 2383872
  116.7 2.7 copy-start.9
  119.4 2.8 copy-start.7
  120.3 2.8 copy-start.5
  121.3 2.8 copy-start.3
  128.8 2.0 copy-start.17
Sparse Core Ops, SparseCore 0:
  116.7 89.0 all-reduce.11
Sparse Core Ops, SparseCore 1:
  128.9 625.0 reduce-scatter.3
where the time goes:
time: 762 us; the launch traced here: 761 us
  waiting for transfers between devices  621 us (81%)
  blocking collectives  84.2 us (11%)
  local copies, waits for them, and re-layouts  17.6 us (2%)
  matrix products  17.6 us (2%)
  between operations  16.4 us (2%)
    unnamed x4, waiting for transfers between devices  621 us
    all_gather x1, blocking collectives, per_device(): full_weight = lax.all_gather(weight, 'sample', axis=0, tiled=True)  72.3 us
  transfers between devices with their start and end apart: 2, of which 2 were waited for; matrix products, arithmetic and copies ran while one was open for 2% of the time, Pallas kernels for 0%

commit v1 on v0

--- a/solution.py
+++ b/solution.py
@@ -20,6 +20,19 @@
     return part.reshape(count, depth, ROWS * WIDTH)
 
 
+def gather_by_exchange(block, axis, count):
+    copies = jnp.broadcast_to(block[None], (count,) + block.shape)
+    return lax.all_to_all(copies, axis, 0, 0, tiled=True)
+
+
+def sum_by_exchange(terms, axes):
+    count = 1
+    for axis in (axes if isinstance(axes, tuple) else (axes,)):
+        count *= lax.axis_size(axis)
+    blocks = terms.reshape((count, terms.shape[0] // count) + terms.shape[1:])
+    return jnp.sum(lax.all_to_all(blocks, axes, 0, 0, tiled=True), axis=0)
+
+
 def per_device(features, weight, style, bias, adjoint):
     local_ch = features.shape[1]
     sect_count = lax.axis_size("sect")
@@ -29,8 +42,10 @@
     pixels = features.shape[2]
     own_style = lax.dynamic_slice_in_dim(style, sect_place * local_ch, local_ch, 1)
     local_mod = (features.astype(jnp.float32) * own_style[:, :, None]).astype(jnp.bfloat16)
-    modulated = lax.all_gather(local_mod, "sect", axis=1, tiled=True)
-    full_weight = lax.all_gather(weight, "sample", axis=0, tiled=True)
+    gathered = gather_by_exchange(local_mod, "sect", sect_count)
+    modulated = jnp.swapaxes(gathered, 0, 1).reshape(samples, channels, pixels)
+    sample_count = lax.axis_size("sample")
+    full_weight = gather_by_exchange(weight, "sample", sample_count).reshape(-1, local_ch)
     kernel = full_weight.reshape(9, channels, local_ch)
     kernel_f = kernel.astype(jnp.float32)
     shifts = [moved(modulated, row_step, col_step) for row_step, col_step in OFFSETS]
@@ -58,7 +73,7 @@
             + 2.0 * kernel_f[index] * coupling
         )
     grad_terms = jnp.concatenate(grads, axis=0)
-    grad_weight = lax.psum_scatter(grad_terms, ("sample", "dom"), scatter_dimension=0, tiled=True)
+    grad_weight = sum_by_exchange(grad_terms, ("sample", "dom"))
     back = jnp.zeros((samples, channels, pixels), jnp.float32)
     for index in range(9):
         row_step, col_step = OFFSETS[index]
@@ -66,7 +81,8 @@
             "nop,io->nip", scaled_adjoint, kernel[index], preferred_element_type=jnp.float32
         )
         back = back + moved(partial_back, -row_step, -col_step)
-    summed = lax.psum_scatter(back, "sect", scatter_dimension=1, tiled=True)
+    by_owner = jnp.swapaxes(back.reshape(samples, sect_count, local_ch, pixels), 0, 1)
+    summed = sum_by_exchange(by_owner.reshape(sect_count * samples, local_ch, pixels), "sect").reshape(samples, local_ch, pixels)
     grad_features = (summed * own_style[:, :, None]).astype(jnp.bfloat16)
     return (styled, grad_weight, grad_features)
 

time: 762 us -> 196 us (0.26)
  the two profiles are of different devices: /device:TPU:68 before, /device:TPU:48 now
where the time goes in v1:
time: 196 us; the launch traced here: 194 us
  local copies, waits for them, and re-layouts  57.8 us (29%)
  waiting for transfers between devices  52.1 us (27%)
  starting transfers between devices  33.7 us (17%)
  matrix products  23.2 us (12%)
  blocking collectives  14.5 us (7%)
  other arithmetic  12.2 us (6%)
    all_to_all x2, waiting for transfers between devices, sum_by_exchange(): return jnp.sum(lax.all_to_all(blocks, axes, 0, 0, tiled=True), axis=0)  49.5 us
    slice x13, local copies, waits for them, and re-layouts, moved(): padded[:, :, 1 + row_step:1 + row_step + ROWS, 1 + col_step:1 + col_step...  29.5 us
    all_to_all x2, starting transfers between devices, sum_by_exchange(): return jnp.sum(lax.all_to_all(blocks, axes, 0, 0, tiled=True), axis=0)  20.9 us
    all_to_all x1, blocking collectives, gather_by_exchange(): return lax.all_to_all(copies, axis, 0, 0, tiled=True)  14.5 us
    all_to_all x1, starting transfers between devices, gather_by_exchange(): return lax.all_to_all(copies, axis, 0, 0, tiled=True)  12.8 us
    dot_general x9, matrix products, per_device(): jnp.einsum('nop,io->nip', scaled_adjoint, kernel[index], preferred_elemen...  12 us
    reshape x4, local copies, waits for them, and re-layouts, moved(): return part.reshape(count, depth, ROWS * WIDTH)  10.4 us
    dot_general x9, matrix products, per_device(): jnp.einsum('nip,nop->io', shifts[index], scaled_adjoint, preferred_elemen...  8.56 us
  transfers between devices with their start and end apart: 3, of which 3 were waited for; matrix products, arithmetic and copies ran while one was open for 19% of the time, Pallas kernels for 0%

profile of v1, /device:TPU:48, one launch (start us, length us, event | category | flops | bytes accessed | tf_op | source)
XLA Modules:
  0.0 194.4 jit_solution(2546437010160580824)
XLA Ops:
  2.3 14.5 %all_to_all.20 = bf16[8,1,64,512]{3,2,1,0:T(8,128)(2,1)S(1)} all-to-all(bf16[8,1,64,512]{3,2,1,0:T(8,128)(2,1)S(1)} %broadcast_in_dim.7), channel_id=1, replica_groups=mesh['sample'=32,'sect'=8,'dom'=3] {'sect'}, dimensions={0} | all-to-all | bytes 1048576 | tf_op jit(solution)/shard_map/all_to_all | solution.py:25
  17.9 12.8 %all-to-all-start.1 = ((bf16[32,144,64]{1,2,0:T(8,128)(2,1)}), bf16[32,144,64]{1,2,0:T(8,128)(2,1)}, u32[]{:S(2)}, u32[]{:S(2)}) async-start(bf16[32,144,64]{1,2,0:T(8,128)(2,1)} %broadcast_in_dim.8), calls=%async_computation.1 | async-start | bytes 2097152 | tf_op jit(solution)/shard_map/all_to_all | solution.py:25
  31.2 4.0 %pad_slice_fusion = (bf16[1,512,8,64]{3,2,1,0:T(8,128)(2,1)S(1)}, bf16[1,512,8,64]{3,2,1,0:T(8,128)(2,1)}, bf16[1,512,8,64]{3,2,1,0:T(8,128)(2,1)}, bf16[1,512,8...) fusion(bf16[1,512,8,64]{3,2,1,0:T(8,128)(2,1)S(1)} %reshape_res, ...), kind=kLoop, calls=%fused_computation | loop fusion | bytes 4718592 | tf_op jit(solution)/shard_map/slice | solution.py:19
  39.0 2.7 %copy.91 = bf16[1,512,8,64]{1,3,2,0:T(8,128)(2,1)} copy(bf16[1,512,8,64]{3,2,1,0:T(8,128)(2,1)} %get-tuple-element.12) | data formatting | bytes 1048576 | tf_op jit(solution)/shard_map/slice | solution.py:19
  41.6 2.7 %copy.82 = bf16[1,512,8,64]{1,3,2,0:T(8,128)(2,1)} copy(bf16[1,512,8,64]{3,2,1,0:T(8,128)(2,1)} %get-tuple-element.15) | data formatting | bytes 1048576 | tf_op jit(solution)/shard_map/slice | solution.py:19
  44.3 2.6 %copy.85 = bf16[1,512,8,64]{1,3,2,0:T(8,128)(2,1)} copy(bf16[1,512,8,64]{3,2,1,0:T(8,128)(2,1)} %get-tuple-element.9) | data formatting | bytes 1048576 | tf_op jit(solution)/shard_map/slice | solution.py:19
  46.9 2.6 %copy.87 = bf16[1,512,8,64]{1,3,2,0:T(8,128)(2,1)} copy(bf16[1,512,8,64]{3,2,1,0:T(8,128)(2,1)} %get-tuple-element.10) | data formatting | bytes 1048576 | tf_op jit(solution)/shard_map/slice | solution.py:19
  49.6 2.7 %copy.89 = bf16[1,512,8,64]{1,3,2,0:T(8,128)(2,1)} copy(bf16[1,512,8,64]{3,2,1,0:T(8,128)(2,1)} %get-tuple-element.11) | data formatting | bytes 1048576 | tf_op jit(solution)/shard_map/slice | solution.py:19
  53.8 2.7 %all-to-all-done.1 = bf16[32,144,64]{1,2,0:T(8,128)(2,1)} async-done(((bf16[32,144,64]{1,2,0:T(8,128)(2,1)}), bf16[32,144,64]{1,2,0:T(8,128)(2,1)}, u32[]{:S(2)}, u32[]{:S(2)}) %all-to-all-start.1) | async-done | bytes 589856 | tf_op jit(solution)/shard_map/all_to_all | solution.py:25
  56.5 2.8 %copy.83 = bf16[32,144,64]{1,0,2:T(8,128)(2,1)} copy(bf16[32,144,64]{1,2,0:T(8,128)(2,1)} %all-to-all-done.1) | data formatting | bytes 1179648 | tf_op jit(solution)/shard_map/all_to_all | solution.py:25
  59.3 3.0 %reshape_reshape.3 = bf16[9,512,64]{1,0,2:T(8,128)(2,1)S(1)} reshape(bf16[32,144,64]{1,0,2:T(8,128)(2,1)} %copy.83) | data formatting | bytes 1179648 | tf_op jit(solution)/shard_map/reshape;reshape | solution.py:49
  79.6 2.5 %copy.114 = f32[512,512]{1,0:T(8,128)} copy(f32[512,512]{0,1:T(8,128)} %bitcast.266) | data formatting | bytes 2097152 | tf_op jit(solution)/shard_map/reshape | solution.py:20
  84.4 2.6 %copy.112 = f32[512,512]{1,0:T(8,128)} copy(f32[512,512]{0,1:T(8,128)} %bitcast.267) | data formatting | bytes 2097152 | tf_op jit(solution)/shard_map/reshape | solution.py:20
  89.4 2.6 %copy.110 = f32[512,512]{1,0:T(8,128)} copy(f32[512,512]{0,1:T(8,128)} %bitcast.268) | data formatting | bytes 2097152 | tf_op jit(solution)/shard_map/reshape | solution.py:20
  93.1 2.7 %copy.108 = f32[512,512]{1,0:T(8,128)} copy(f32[512,512]{0,1:T(8,128)} %bitcast.269) | data formatting | bytes 2097152 | tf_op jit(solution)/shard_map/reshape | solution.py:20
  95.8 3.2 %fusion.21 = f32[1,512,8,64]{1,3,2,0:T(8,128)} fusion(f32[1,512,8,64]{1,3,2,0:T(8,128)S(1)} %copy-done.14, f32[1,512,8,64]{1,3,2,0:T(8,128)} %convolution_bitcast_fusion.7, f32[1,512,8,64]{1,3,2,0:T(8,128)} %convolution_bitcast_fusion.6, f32[1,512,8,64]{1,3,2,0:T(8,128)} %convolution_bitcast_fusion.5), kind=kLoop, calls=%fused_computation.62 | loop fusion | flops 786432 | bytes 5242880 | tf_op jit(solution)/shard_map/add | solution.py:83
  99.0 2.6 %copy.106 = f32[512,512]{1,0:T(8,128)} copy(f32[512,512]{0,1:T(8,128)} %bitcast.265) | data formatting | bytes 2097152 | tf_op jit(solution)/shard_map/add | solution.py:83
  101.7 3.7 %fusion.4 = f32[512,512]{1,0:T(8,128)} fusion(f32[512,512]{1,0:T(8,128)S(1)} %copy-done.15, f32[512,512]{1,0:T(8,128)} %copy.112, f32[512,512]{1,0:T(8,128)} %copy.110, f32[512,512]{1,0:T(8,128)} %copy.108, f32[512,512]{1,0:T(8,128)} %copy.106, bf16[1,512,64]{1,0,2:T(2,128)(2,1)S(1)} %copy-done.18, bf16[1,64,512]{2,1,0:T(8,128)(2,1)S(1)} %copy-done, ...), kind=kOutput, calls=%fused_computation.29 | convolution fusion | flops 34963456 | bytes 6422784 | tf_op jit(solution)/shard_map/nop,io->nip/dot_general | solution.py:80
  105.4 3.7 %all-to-all-start.3 = ((f32[8,1,64,512]{3,2,1,0:T(8,128)}), f32[8,1,64,512]{3,2,1,0:T(8,128)S(1)}, u32[]{:S(2)}, u32[]{:S(2)}) async-start(f32[8,1,64,512]{3,2,1,0:T(8,128)} %bitcast.68), calls=%async_computation.3 | async-start | bytes 2097152 | tf_op jit(solution)/shard_map/all_to_all | solution.py:33
  118.2 2.5 %reshape.330 = f32[96,1,3072]{2,1,0:T(1,128)} reshape(f32[96,48,64]{2,1,0:T(8,128)S(1)} %bitcast.246) | data formatting | bytes 2359296
  120.7 4.2 %all-to-all-done.3 = f32[8,1,64,512]{3,2,1,0:T(8,128)S(1)} async-done(((f32[8,1,64,512]{3,2,1,0:T(8,128)}), f32[8,1,64,512]{3,2,1,0:T(8,128)S(1)}, u32[]{:S(2)}, u32[]{:S(2)}) %all-to-all-start.3) | async-done | bytes 1048608 | tf_op jit(solution)/shard_map/all_to_all | solution.py:33
  124.9 17.2 %all-to-all-start.2 = ((f32[96,1,3072]{2,1,0:T(1,128)}), f32[96,1,3072]{2,1,0:T(1,128)S(1)}, u32[]{:S(2)}, u32[]{:S(2)}) async-start(f32[96,1,3072]{2,1,0:T(1,128)} %reshape.330), calls=%async_computation.2 | async-start | bytes 2359296 | tf_op jit(solution)/shard_map/all_to_all | solution.py:33
  143.7 45.2 %all-to-all-done.2 = f32[96,1,3072]{2,1,0:T(1,128)S(1)} async-done(((f32[96,1,3072]{2,1,0:T(1,128)}), f32[96,1,3072]{2,1,0:T(1,128)S(1)}, u32[]{:S(2)}, u32[]{:S(2)}) %all-to-all-start.2) | async-done | bytes 1179680 | tf_op jit(solution)/shard_map/all_to_all | solution.py:33
  189.5 3.4 %reduce.2 = f32[96,3072]{1,0:T(8,128)S(1)} reduce(f32[96,1,3072]{2,1,0:T(1,128)S(1)} %all-to-all-done.2, f32[]{:T(128)} %broadcast.74), dimensions={1}, to_apply=%all_to_all.14.reduce_sub_computation | reduce | bytes 2359300 | tf_op jit(solution)/shard_map/all_to_all | solution.py:33
  (99 shorter events, 44.1 us)
Async XLA Ops:
  0.6 16.2 %copy-start.19 = (bf16[144,64]{0,1:T(8,128)(2,1)S(1)}, bf16[144,64]{0,1:T(8,128)(2,1)}, u32[]{:S(2)}) copy-start(bf16[144,64]{0,1:T(8,128)(2,1)} %param.6) | copy-start | bytes 55300
  17.9 12.8 %copy-start.20 = (f32[1,512]{1,0:T(1,128)S(1)}, f32[1,512]{1,0:T(1,128)}, u32[]{:S(2)}) copy-start(f32[1,512]{1,0:T(1,128)} %param.7) | copy-start | bytes 6148
  17.9 38.6 %all-to-all-start.1 = ((bf16[32,144,64]{1,2,0:T(8,128)(2,1)}), bf16[32,144,64]{1,2,0:T(8,128)(2,1)}, u32[]{:S(2)}, u32[]{:S(2)}) async-start(bf16[32,144,64]{1,2,0:T(8,128)(2,1)} %broadcast_in_dim.8), calls=%async_computation.1 | async-start | bytes 2097152 | tf_op jit(solution)/shard_map/all_to_all | solution.py:25
  63.9 2.6 %copy-start.17 = (bf16[1,512,64]{1,0,2:T(2,128)(2,1)}, bf16[1,512,64]{1,0,2:T(2,128)(2,1)S(1)}, u32[]{:S(2)}) copy-start(bf16[1,512,64]{1,0,2:T(2,128)(2,1)S(1)} %slice.151) | copy-start | bytes 196612
  64.0 1.1 copy-start.9
  64.3 1.3 copy-start.11
  64.8 1.1 copy-start.7
  65.1 1.1 copy-start.5
  66.2 1.1 copy-start.3
  74.0 2.5 %copy-start.22 = (f32[64]{0:T(128)S(1)}, f32[64]{0:T(128)}, u32[]{:S(2)}) copy-start(f32[64]{0:T(128)} %get-tuple-element.17) | copy-start | bytes 772
  74.0 2.6 %copy-start.10 = (bf16[1,512,8,64]{1,3,2,0:T(8,128)(2,1)S(1)}, bf16[1,512,8,64]{1,3,2,0:T(8,128)(2,1)}, u32[]{:S(2)}) copy-start(bf16[1,512,8,64]{1,3,2,0:T(8,128)(2,1)} %copy.82) | copy-start | bytes 1572868
  74.0 2.6 %copy-start.13 = (f32[9,512,64]{1,2,0:T(8,128)S(1)}, f32[9,512,64]{1,2,0:T(8,128)}, u32[]{:S(2)}) copy-start(f32[9,512,64]{1,2,0:T(8,128)} %get-tuple-element.6) | copy-start | bytes 3538948
  75.3 1.6 copy-start.12
  75.3 1.8 copy-start.8
  76.6 1.1 copy-start.6
  78.2 1.4 copy-start.16
  93.1 2.7 %copy-start.14 = (f32[1,512,8,64]{1,3,2,0:T(8,128)S(1)}, f32[1,512,8,64]{1,3,2,0:T(8,128)}, u32[]{:S(2)}) copy-start(f32[1,512,8,64]{1,3,2,0:T(8,128)} %convolution_bitcast_fusion.8) | copy-start | bytes 3145732
  99.0 2.6 %copy-start.15 = (f32[512,512]{1,0:T(8,128)S(1)}, f32[512,512]{1,0:T(8,128)}, u32[]{:S(2)}) copy-start(f32[512,512]{1,0:T(8,128)} %copy.114) | copy-start | bytes 3145732
  99.0 2.6 %copy-start.18 = (bf16[1,512,64]{1,0,2:T(2,128)(2,1)S(1)}, bf16[1,512,64]{1,0,2:T(2,128)(2,1)}, u32[]{:S(2)}) copy-start(bf16[1,512,64]{1,0,2:T(2,128)(2,1)} %copy-done.17) | copy-start | bytes 196612
  105.4 3.7 %copy-start.2 = (bf16[1,512,8,64]{1,3,2,0:T(8,128)(2,1)S(1)}, bf16[1,512,8,64]{1,3,2,0:T(8,128)(2,1)}, u32[]{:S(2)}) copy-start(bf16[1,512,8,64]{1,3,2,0:T(8,128)(2,1)} %copy.91) | copy-start | bytes 1572868
  105.4 19.6 %all-to-all-start.3 = ((f32[8,1,64,512]{3,2,1,0:T(8,128)}), f32[8,1,64,512]{3,2,1,0:T(8,128)S(1)}, u32[]{:S(2)}, u32[]{:S(2)}) async-start(f32[8,1,64,512]{3,2,1,0:T(8,128)} %bitcast.68), calls=%async_computation.3 | async-start | bytes 2097152 | tf_op jit(solution)/shard_map/all_to_all | solution.py:33
  109.1 5.5 %copy-start.4 = (bf16[1,512,8,64]{1,3,2,0:T(8,128)(2,1)S(1)}, bf16[1,512,8,64]{1,3,2,0:T(8,128)(2,1)}, u32[]{:S(2)}) copy-start(bf16[1,512,8,64]{1,3,2,0:T(8,128)(2,1)} %copy.97) | copy-start | bytes 1572868
  120.7 21.5 %copy-start.21 = (f32[64]{0:T(128)S(1)}, f32[64]{0:T(128)}, u32[]{:S(2)}) copy-start(f32[64]{0:T(128)} %param.8) | copy-start | bytes 772
  124.9 64.0 %all-to-all-start.2 = ((f32[96,1,3072]{2,1,0:T(1,128)}), f32[96,1,3072]{2,1,0:T(1,128)S(1)}, u32[]{:S(2)}, u32[]{:S(2)}) async-start(f32[96,1,3072]{2,1,0:T(1,128)} %reshape.330), calls=%async_computation.2 | async-start | bytes 2359296 | tf_op jit(solution)/shard_map/all_to_all | solution.py:33
  (2 other events, 2.1 us)

commit v2 on v1

--- a/solution.py
+++ b/solution.py
@@ -12,12 +12,14 @@
 
 
 def moved(array, row_step, col_step):
-    count = array.shape[0]
-    depth = array.shape[1]
-    grid = array.reshape(count, depth, ROWS, WIDTH)
-    padded = jnp.pad(grid, ((0, 0), (0, 0), (1, 1), (1, 1)))
-    part = padded[:, :, 1 + row_step : 1 + row_step + ROWS, 1 + col_step : 1 + col_step + WIDTH]
-    return part.reshape(count, depth, ROWS * WIDTH)
+    pixels = array.shape[-1]
+    step = row_step * WIDTH + col_step
+    reach = WIDTH + 1
+    padded = jnp.pad(array, [(0, 0)] * (array.ndim - 1) + [(reach, reach)])
+    part = lax.slice_in_dim(padded, reach + step, reach + step + pixels, axis=array.ndim - 1)
+    column = lax.broadcasted_iota(jnp.int32, array.shape, array.ndim - 1) % WIDTH
+    inside = (column + col_step >= 0) & (column + col_step < WIDTH)
+    return jnp.where(inside, part, jnp.zeros_like(part))
 
 
 def gather_by_exchange(block, axis, count):
@@ -48,12 +50,10 @@
     full_weight = gather_by_exchange(weight, "sample", sample_count).reshape(-1, local_ch)
     kernel = full_weight.reshape(9, channels, local_ch)
     kernel_f = kernel.astype(jnp.float32)
-    shifts = [moved(modulated, row_step, col_step) for row_step, col_step in OFFSETS]
-    conv_out = jnp.zeros(features.shape, jnp.float32)
-    for index in range(9):
-        conv_out = conv_out + jnp.einsum(
-            "nip,io->nop", shifts[index], kernel[index], preferred_element_type=jnp.float32
-        )
+    products = jnp.einsum("kio,nip->nkop", kernel, modulated, preferred_element_type=jnp.float32)
+    conv_out = moved(products[:, 0], *OFFSETS[0])
+    for index in range(1, 9):
+        conv_out = conv_out + moved(products[:, index], *OFFSETS[index])
     kernel_sq = jnp.sum(kernel_f * kernel_f, axis=0)
     style_sq = style * style
     energy = jnp.dot(style_sq, kernel_sq, precision=lax.Precision.HIGHEST) + EPSILON
@@ -64,23 +64,13 @@
     demod_grad = jnp.sum(adjoint_f * conv_out, axis=2)
     energy_grad = -0.5 * demod_grad * demod * demod * demod
     coupling = jnp.dot(style_sq.T, energy_grad, precision=lax.Precision.HIGHEST)
-    grads = []
-    for index in range(9):
-        grads.append(
-            jnp.einsum(
-                "nip,nop->io", shifts[index], scaled_adjoint, preferred_element_type=jnp.float32
-            )
-            + 2.0 * kernel_f[index] * coupling
-        )
-    grad_terms = jnp.concatenate(grads, axis=0)
+    back_shifts = jnp.stack(
+        [moved(scaled_adjoint, -row_step, -col_step) for row_step, col_step in OFFSETS], axis=1
+    )
+    grad_main = jnp.einsum("nip,nkop->kio", modulated, back_shifts, preferred_element_type=jnp.float32)
+    grad_terms = (grad_main + 2.0 * kernel_f * coupling[None]).reshape(-1, local_ch)
     grad_weight = sum_by_exchange(grad_terms, ("sample", "dom"))
-    back = jnp.zeros((samples, channels, pixels), jnp.float32)
-    for index in range(9):
-        row_step, col_step = OFFSETS[index]
-        partial_back = jnp.einsum(
-            "nop,io->nip", scaled_adjoint, kernel[index], preferred_element_type=jnp.float32
-        )
-        back = back + moved(partial_back, -row_step, -col_step)
+    back = jnp.einsum("kio,nkop->nip", kernel, back_shifts, preferred_element_type=jnp.float32)
     by_owner = jnp.swapaxes(back.reshape(samples, sect_count, local_ch, pixels), 0, 1)
     summed = sum_by_exchange(by_owner.reshape(sect_count * samples, local_ch, pixels), "sect").reshape(samples, local_ch, pixels)
     grad_features = (summed * own_style[:, :, None]).astype(jnp.bfloat16)

time: 196 us -> 151 us (0.77)
  local copies, waits for them, and re-layouts: 57.8 us -> 10.5 us
  waiting for transfers between devices: 52.1 us -> 88.8 us
  matrix products: 23.2 us -> 2.75 us
  blocking collectives: 14.5 us -> 0 us
  starting transfers between devices: 33.7 us -> 38.2 us
  other arithmetic: 12.2 us -> 9.43 us
    all_to_all x1 -> x2, waiting for transfers between devices: 2.68 us -> 32.8 us  [gather_by_exchange(): return lax.all_to_all(copies, axis, 0, 0, tiled=True)]
    slice x14 -> x0, local copies, waits for them, and re-layouts: 29.7 us -> none  [the longest x13 29.5 us: moved(): padded[:, :, 1 + row_step:1 + row_step + ROWS, 1 + col_step:1 + col_step...]
    dot_general x27 -> x2, matrix products: 23 us -> 2.11 us  [the longest x1 1.61 us: per_device(): jnp.einsum('kio,nkop->nip', kernel, back_shifts, preferred_element_type=j...]
    all_to_all x1 -> x0, blocking collectives: 14.5 us -> none  [gather_by_exchange(): return lax.all_to_all(copies, axis, 0, 0, tiled=True)]
    reshape x5 -> x0, local copies, waits for them, and re-layouts: 12.2 us -> none  [the longest x4 10.4 us: moved(): return part.reshape(count, depth, ROWS * WIDTH)]
    all_to_all x2, waiting for transfers between devices: 49.5 us -> 56 us  [sum_by_exchange(): return jnp.sum(lax.all_to_all(blocks, axes, 0, 0, tiled=True), axis=0)]
    all_to_all x1 -> x2, starting transfers between devices: 12.8 us -> 17 us  [gather_by_exchange(): return lax.all_to_all(copies, axis, 0, 0, tiled=True)]
    add x1 -> x0, other arithmetic: 3.25 us -> none  [per_device(): back = back + moved(partial_back, -row_step, -col_step)]
  transfers between devices with their start and end apart: 3 -> 4, of which waited for: 3 -> 4; matrix products, arithmetic and copies ran while one was open for 19% -> 7% of each run, Pallas kernels for 0% -> 0%
where the time goes in v2:
time: 151 us
  waiting for transfers between devices  88.8 us (59%)
  starting transfers between devices  38.2 us (25%)
  local copies, waits for them, and re-layouts  10.5 us (7%)
  other arithmetic  9.43 us (6%)
  matrix products  2.75 us (2%)
    all_to_all x2, waiting for transfers between devices, sum_by_exchange(): return jnp.sum(lax.all_to_all(blocks, axes, 0, 0, tiled=True), axis=0)  56 us
    all_to_all x2, waiting for transfers between devices, gather_by_exchange(): return lax.all_to_all(copies, axis, 0, 0, tiled=True)  32.8 us
    all_to_all x2, starting transfers between devices, sum_by_exchange(): return jnp.sum(lax.all_to_all(blocks, axes, 0, 0, tiled=True), axis=0)  21.2 us
    all_to_all x2, starting transfers between devices, gather_by_exchange(): return lax.all_to_all(copies, axis, 0, 0, tiled=True)  17 us
    unnamed x12, local copies, waits for them, and re-layouts  3.88 us
    all_to_all x1, other arithmetic, sum_by_exchange(): return jnp.sum(lax.all_to_all(blocks, axes, 0, 0, tiled=True), axis=0)  3.44 us
  transfers between devices with their start and end apart: 4, of which 4 were waited for; matrix products, arithmetic and copies ran while one was open for 7% of the time, Pallas kernels for 0%

profile of v2, /device:TPU:48, one launch (start us, length us, event | category | flops | bytes accessed | tf_op | source)
XLA Modules:
  0.0 150.6 jit_solution(10642242871100351696)
XLA Ops:
  0.6 1.8 %broadcast_in_dim.8 = bf16[32,144,64]{1,2,0:T(8,128)(2,1)} broadcast(bf16[144,64]{0,1:T(8,128)(2,1)} %param.6), dimensions={1,2} | broadcast | bytes 608256 | tf_op jit(solution)/shard_map/broadcast_in_dim | solution.py:26
  2.5 12.7 %all-to-all-start.1 = ((bf16[32,144,64]{1,2,0:T(8,128)(2,1)}), bf16[32,144,64]{1,2,0:T(8,128)(2,1)S(1)}, u32[]{:S(2)}, u32[]{:S(2)}) async-start(bf16[32,144,64]{1,2,0:T(8,128)(2,1)} %broadcast_in_dim.8), calls=%async_computation.1 | async-start | bytes 2097152 | tf_op jit(solution)/shard_map/all_to_all | solution.py:27
  15.4 25.5 %all-to-all-done.1 = bf16[32,144,64]{1,2,0:T(8,128)(2,1)S(1)} async-done(((bf16[32,144,64]{1,2,0:T(8,128)(2,1)}), bf16[32,144,64]{1,2,0:T(8,128)(2,1)S(1)}, u32[]{:S(2)}, u32[]{:S(2)}) %all-to-all-start.1) | async-done | bytes 589856 | tf_op jit(solution)/shard_map/all_to_all | solution.py:27
  40.9 0.8 broadcast_in_dim.7
  41.7 4.3 %all-to-all-start = ((bf16[8,1,64,512]{3,2,1,0:T(8,128)(2,1)}), bf16[8,1,64,512]{3,2,1,0:T(8,128)(2,1)S(1)}, u32[]{:S(2)}, u32[]{:S(2)}) async-start(bf16[8,1,64,512]{3,2,1,0:T(8,128)(2,1)} %broadcast_in_dim.7), calls=%async_computation | async-start | bytes 1048576 | tf_op jit(solution)/shard_map/all_to_all | solution.py:27
  46.1 0.6 copy.13
  46.6 1.8 %reshape_reshape.6 = bf16[9,512,64]{1,0,2:T(8,128)(2,1)S(1)} reshape(bf16[32,144,64]{1,0,2:T(8,128)(2,1)S(1)} %copy.13) | data formatting | bytes 1179648 | tf_op jit(solution)/shard_map/reshape;reshape | solution.py:51
  49.1 7.3 %all-to-all-done = bf16[8,1,64,512]{3,2,1,0:T(8,128)(2,1)S(1)} async-done(((bf16[8,1,64,512]{3,2,1,0:T(8,128)(2,1)}), bf16[8,1,64,512]{3,2,1,0:T(8,128)(2,1)S(1)}, u32[]{:S(2)}, u32[]{:S(2)}) %all-to-all-start) | async-done | bytes 524320 | tf_op jit(solution)/shard_map/all_to_all | solution.py:27
  56.9 0.8 copy-done.1
  57.7 1.1 fusion.12
  59.6 1.6 %fusion.4 = f32[512,512,1]{0,1,2:T(8,128)} fusion(bf16[9,512,64]{1,2,0:T(8,128)(2,1)S(1)} %get-tuple-element.6, bf16[1,9,64,512]{3,2,1,0:T(8,128)(2,1)S(1)} %fusion.58), kind=kOutput, calls=%fused_computation.8 | convolution fusion | flops 301989888 | bytes 2228224 | tf_op jit(solution)/shard_map/kio,nkop->nip/dot_general | solution.py:73
  61.2 4.2 %all-to-all-start.3 = ((f32[8,1,64,512]{3,2,1,0:T(8,128)}), f32[8,1,64,512]{3,2,1,0:T(8,128)}, u32[]{:S(2)}, u32[]{:S(2)}) async-start(f32[8,1,64,512]{3,2,1,0:T(8,128)} %bitcast.39), calls=%async_computation.3 | async-start | bytes 2097152 | tf_op jit(solution)/shard_map/all_to_all | solution.py:35
  66.1 0.9 copy.16
  67.0 2.5 %reshape.417 = f32[96,1,3072]{2,1,0:T(1,128)} reshape(f32[96,48,64]{2,1,0:T(8,128)S(1)} %bitcast.111) | data formatting | bytes 2359296
  69.5 12.0 %all-to-all-done.3 = f32[8,1,64,512]{3,2,1,0:T(8,128)} async-done(((f32[8,1,64,512]{3,2,1,0:T(8,128)}), f32[8,1,64,512]{3,2,1,0:T(8,128)}, u32[]{:S(2)}, u32[]{:S(2)}) %all-to-all-start.3) | async-done | bytes 1048608 | tf_op jit(solution)/shard_map/all_to_all | solution.py:35
  81.4 17.0 %all-to-all-start.2 = ((f32[96,1,3072]{2,1,0:T(1,128)}), f32[96,1,3072]{2,1,0:T(1,128)S(1)}, u32[]{:S(2)}, u32[]{:S(2)}) async-start(f32[96,1,3072]{2,1,0:T(1,128)} %reshape.417), calls=%async_computation.2 | async-start | bytes 2359296 | tf_op jit(solution)/shard_map/all_to_all | solution.py:35
  98.4 0.7 add_convert_fusion
  99.1 1.3 reduce_sum.41
  100.4 0.7 fusion.30
  101.1 44.0 %all-to-all-done.2 = f32[96,1,3072]{2,1,0:T(1,128)S(1)} async-done(((f32[96,1,3072]{2,1,0:T(1,128)}), f32[96,1,3072]{2,1,0:T(1,128)S(1)}, u32[]{:S(2)}, u32[]{:S(2)}) %all-to-all-start.2) | async-done | bytes 1179680 | tf_op jit(solution)/shard_map/all_to_all | solution.py:35
  145.1 0.5 broadcast.518
  145.7 3.4 %reduce.2 = f32[96,3072]{1,0:T(8,128)S(1)} reduce(f32[96,1,3072]{2,1,0:T(1,128)S(1)} %all-to-all-done.2, f32[]{:T(128)} %broadcast.518), dimensions={1}, to_apply=%all_to_all.14.reduce_sub_computation | reduce | bytes 2359300 | tf_op jit(solution)/shard_map/all_to_all | solution.py:35
  149.1 0.6 reshape.418
  149.7 0.8 reduce_sum.40
  (30 shorter events, 2.6 us)
Async XLA Ops:
  2.5 12.7 %copy-start.3 = (f32[1,512]{1,0:T(1,128)S(1)}, f32[1,512]{1,0:T(1,128)}, u32[]{:S(2)}) copy-start(f32[1,512]{1,0:T(1,128)} %param.7) | copy-start | bytes 6148
  2.5 12.8 %copy-start.2 = (bf16[1,64,512]{2,1,0:T(8,128)(2,1)S(1)}, bf16[1,64,512]{2,1,0:T(8,128)(2,1)}, u32[]{:S(2)}) copy-start(bf16[1,64,512]{2,1,0:T(8,128)(2,1)} %param.5) | copy-start | bytes 196612
  2.5 38.4 %all-to-all-start.1 = ((bf16[32,144,64]{1,2,0:T(8,128)(2,1)}), bf16[32,144,64]{1,2,0:T(8,128)(2,1)S(1)}, u32[]{:S(2)}, u32[]{:S(2)}) async-start(bf16[32,144,64]{1,2,0:T(8,128)(2,1)} %broadcast_in_dim.8), calls=%async_computation.1 | async-start | bytes 2097152 | tf_op jit(solution)/shard_map/all_to_all | solution.py:27
  41.7 14.6 %all-to-all-start = ((bf16[8,1,64,512]{3,2,1,0:T(8,128)(2,1)}), bf16[8,1,64,512]{3,2,1,0:T(8,128)(2,1)S(1)}, u32[]{:S(2)}, u32[]{:S(2)}) async-start(bf16[8,1,64,512]{3,2,1,0:T(8,128)(2,1)} %broadcast_in_dim.7), calls=%async_computation | async-start | bytes 1048576 | tf_op jit(solution)/shard_map/all_to_all | solution.py:27
  56.8 0.8 copy-start.1
  61.2 20.2 %all-to-all-start.3 = ((f32[8,1,64,512]{3,2,1,0:T(8,128)}), f32[8,1,64,512]{3,2,1,0:T(8,128)}, u32[]{:S(2)}, u32[]{:S(2)}) async-start(f32[8,1,64,512]{3,2,1,0:T(8,128)} %bitcast.39), calls=%async_computation.3 | async-start | bytes 2097152 | tf_op jit(solution)/shard_map/all_to_all | solution.py:35
  69.4 28.9 %copy-start = (f32[1,64,512]{2,1,0:T(8,128)S(1)}, f32[1,64,512]{2,1,0:T(8,128)}, u32[]{:S(2)}) copy-start(f32[1,64,512]{2,1,0:T(8,128)} %get-tuple-element.4) | copy-start | bytes 393220
  69.4 28.9 %copy-start.4 = (f32[64]{0:T(128)S(1)}, f32[64]{0:T(128)}, u32[]{:S(2)}) copy-start(f32[64]{0:T(128)} %param.8) | copy-start | bytes 772
  81.4 63.7 %all-to-all-start.2 = ((f32[96,1,3072]{2,1,0:T(1,128)}), f32[96,1,3072]{2,1,0:T(1,128)S(1)}, u32[]{:S(2)}, u32[]{:S(2)}) async-start(f32[96,1,3072]{2,1,0:T(1,128)} %reshape.417), calls=%async_computation.2 | async-start | bytes 2359296 | tf_op jit(solution)/shard_map/all_to_all | solution.py:35

commit v3 on v2

--- a/solution.py
+++ b/solution.py
@@ -35,6 +35,31 @@
     return jnp.sum(lax.all_to_all(blocks, axes, 0, 0, tiled=True), axis=0)
 
 
+def gather_by_permutes(block, axis, count):
+    place = lax.axis_index(axis)
+    depth = block.shape[1]
+    whole = jnp.zeros((block.shape[0], depth * count) + block.shape[2:], block.dtype)
+    whole = lax.dynamic_update_slice_in_dim(whole, block, place * depth, 1)
+    for distance in range(1, count):
+        pairs = [(j, (j + distance) % count) for j in range(count)]
+        arrived = lax.ppermute(block, axis, pairs)
+        source = (place + count - distance) % count
+        whole = lax.dynamic_update_slice_in_dim(whole, arrived, source * depth, 1)
+    return whole
+
+
+def sum_by_permutes(whole, axis, count):
+    place = lax.axis_index(axis)
+    depth = whole.shape[1] // count
+    total = lax.dynamic_slice_in_dim(whole, place * depth, depth, 1)
+    for distance in range(1, count):
+        pairs = [(j, (j + distance) % count) for j in range(count)]
+        target = (place + distance) % count
+        part = lax.dynamic_slice_in_dim(whole, target * depth, depth, 1)
+        total = total + lax.ppermute(part, axis, pairs)
+    return total
+
+
 def per_device(features, weight, style, bias, adjoint):
     local_ch = features.shape[1]
     sect_count = lax.axis_size("sect")
@@ -44,8 +69,7 @@
     pixels = features.shape[2]
     own_style = lax.dynamic_slice_in_dim(style, sect_place * local_ch, local_ch, 1)
     local_mod = (features.astype(jnp.float32) * own_style[:, :, None]).astype(jnp.bfloat16)
-    gathered = gather_by_exchange(local_mod, "sect", sect_count)
-    modulated = jnp.swapaxes(gathered, 0, 1).reshape(samples, channels, pixels)
+    modulated = gather_by_permutes(local_mod, "sect", sect_count)
     sample_count = lax.axis_size("sample")
     full_weight = gather_by_exchange(weight, "sample", sample_count).reshape(-1, local_ch)
     kernel = full_weight.reshape(9, channels, local_ch)
@@ -71,8 +95,7 @@
     grad_terms = (grad_main + 2.0 * kernel_f * coupling[None]).reshape(-1, local_ch)
     grad_weight = sum_by_exchange(grad_terms, ("sample", "dom"))
     back = jnp.einsum("kio,nkop->nip", kernel, back_shifts, preferred_element_type=jnp.float32)
-    by_owner = jnp.swapaxes(back.reshape(samples, sect_count, local_ch, pixels), 0, 1)
-    summed = sum_by_exchange(by_owner.reshape(sect_count * samples, local_ch, pixels), "sect").reshape(samples, local_ch, pixels)
+    summed = sum_by_permutes(back, "sect", sect_count)
     grad_features = (summed * own_style[:, :, None]).astype(jnp.bfloat16)
     return (styled, grad_weight, grad_features)
 

time: 151 us -> 145 us (0.960)
  the two profiles are of different devices: /device:TPU:48 before, /device:TPU:50 now
where the time goes in v3:
time: 145 us; the launch traced here: 144 us
  starting transfers between devices  65.8 us (45%)
  waiting for transfers between devices  53.4 us (37%)
  local copies, waits for them, and re-layouts  11.6 us (8%)
  other arithmetic  8.95 us (6%)
  matrix products  2.84 us (2%)
    all_to_all x1, waiting for transfers between devices, sum_by_exchange(): return jnp.sum(lax.all_to_all(blocks, axes, 0, 0, tiled=True), axis=0)  24.4 us
    all_to_all x1, waiting for transfers between devices, gather_by_exchange(): return lax.all_to_all(copies, axis, 0, 0, tiled=True)  21.1 us
    all_to_all x1, starting transfers between devices, sum_by_exchange(): return jnp.sum(lax.all_to_all(blocks, axes, 0, 0, tiled=True), axis=0)  18.5 us
    ppermute x7, starting transfers between devices, gather_by_permutes(): arrived = lax.ppermute(block, axis, pairs)  17.6 us
    ppermute x7, starting transfers between devices, sum_by_permutes(): total = total + lax.ppermute(part, axis, pairs)  17 us
    all_to_all x1, starting transfers between devices, gather_by_exchange(): return lax.all_to_all(copies, axis, 0, 0, tiled=True)  12.7 us
    ppermute x7, waiting for transfers between devices, gather_by_permutes(): arrived = lax.ppermute(block, axis, pairs)  4.56 us
    unnamed x18, local copies, waits for them, and re-layouts  3.94 us
  transfers between devices with their start and end apart: 16, of which 6 were waited for; matrix products, arithmetic and copies ran while one was open for 3% of the time, Pallas kernels for 0%

profile of v3, /device:TPU:50, one launch (start us, length us, event | category | flops | bytes accessed | tf_op | source)
XLA Modules:
  0.0 143.8 jit_solution(14466861328366327759)
XLA Ops:
  2.3 2.4 %collective-permute-start.5 = (bf16[1,64,512]{2,1,0:T(8,128)(2,1)S(1)}, bf16[1,64,512]{2,1,0:T(8,128)(2,1)S(1)}, u32[]{:S(2)}, u32[]{:S(2)}) collective-permute-start(bf16[1,64,512]{2,1,0:T(8,128)(2,1)S(1)} %get-tuple-element.8), channel_id=1, source_target_pairs={{0,18},{3,21},{6,0},{9,3},{12,6},{15,9},{18,12},{21,15},{1,19},{4,... | collective-permute-start | bytes 196616 | tf_op jit(solution)/shard_map/ppermute | solution.py:45
  4.8 3.5 %collective-permute-start.4 = (bf16[1,64,512]{2,1,0:T(8,128)(2,1)S(1)}, bf16[1,64,512]{2,1,0:T(8,128)(2,1)S(1)}, u32[]{:S(2)}, u32[]{:S(2)}) collective-permute-start(bf16[1,64,512]{2,1,0:T(8,128)(2,1)S(1)} %get-tuple-element.8), channel_id=1, source_target_pairs={{0,15},{3,18},{6,21},{9,0},{12,3},{15,6},{18,9},{21,12},{1,16},{4,... | collective-permute-start | bytes 196616 | tf_op jit(solution)/shard_map/ppermute | solution.py:45
  8.3 3.0 %collective-permute-start.3 = (bf16[1,64,512]{2,1,0:T(8,128)(2,1)S(1)}, bf16[1,64,512]{2,1,0:T(8,128)(2,1)S(1)}, u32[]{:S(2)}, u32[]{:S(2)}) collective-permute-start(bf16[1,64,512]{2,1,0:T(8,128)(2,1)S(1)} %get-tuple-element.8), channel_id=1, source_target_pairs={{0,12},{3,15},{6,18},{9,21},{12,0},{15,3},{18,6},{21,9},{1,13},{4,... | collective-permute-start | bytes 196616 | tf_op jit(solution)/shard_map/ppermute | solution.py:45
  11.3 3.7 %collective-permute-start.2 = (bf16[1,64,512]{2,1,0:T(8,128)(2,1)S(1)}, bf16[1,64,512]{2,1,0:T(8,128)(2,1)S(1)}, u32[]{:S(2)}, u32[]{:S(2)}) collective-permute-start(bf16[1,64,512]{2,1,0:T(8,128)(2,1)S(1)} %get-tuple-element.8), channel_id=1, source_target_pairs={{0,9},{3,12},{6,15},{9,18},{12,21},{15,0},{18,3},{21,6},{1,10},{4,... | collective-permute-start | bytes 196616 | tf_op jit(solution)/shard_map/ppermute | solution.py:45
  15.8 1.9 %broadcast_in_dim.2 = bf16[32,144,64]{1,2,0:T(8,128)(2,1)} broadcast(bf16[144,64]{0,1:T(8,128)(2,1)} %param.6), dimensions={1,2} | broadcast | bytes 608256 | tf_op jit(solution)/shard_map/broadcast_in_dim | solution.py:26
  17.7 12.7 %all-to-all-start = ((bf16[32,144,64]{1,2,0:T(8,128)(2,1)}), bf16[32,144,64]{1,2,0:T(8,128)(2,1)S(1)}, u32[]{:S(2)}, u32[]{:S(2)}) async-start(bf16[32,144,64]{1,2,0:T(8,128)(2,1)} %broadcast_in_dim.2), calls=%async_computation | async-start | bytes 2097152 | tf_op jit(solution)/shard_map/all_to_all | solution.py:27
  30.5 3.7 %collective-permute-start.1 = (bf16[1,64,512]{2,1,0:T(8,128)(2,1)S(1)}, bf16[1,64,512]{2,1,0:T(8,128)(2,1)S(1)}, u32[]{:S(2)}, u32[]{:S(2)}) collective-permute-start(bf16[1,64,512]{2,1,0:T(8,128)(2,1)S(1)} %get-tuple-element.8), channel_id=1, source_target_pairs={{0,6},{3,9},{6,12},{9,15},{12,18},{15,21},{18,0},{21,3},{1,7},{4,1... | collective-permute-start | bytes 196616 | tf_op jit(solution)/shard_map/ppermute | solution.py:45
  34.3 2.8 %collective-permute-done.1 = bf16[1,64,512]{2,1,0:T(8,128)(2,1)S(1)} collective-permute-done((bf16[1,64,512]{2,1,0:T(8,128)(2,1)S(1)}, bf16[1,64,512]{2,1,0:T(8,128)(2,1)S(1)}, u32[]{:S(2)}, u32[]{:S(2)}) %collective-permute-start.1) | collective-permute-done | bytes 65568 | tf_op jit(solution)/shard_map/ppermute | solution.py:45
  37.6 1.8 %collective-permute-done.6 = bf16[1,64,512]{2,1,0:T(8,128)(2,1)S(1)} collective-permute-done((bf16[1,64,512]{2,1,0:T(8,128)(2,1)S(1)}, bf16[1,64,512]{2,1,0:T(8,128)(2,1)S(1)}, u32[]{:S(2)}, u32[]{:S(2)}) %collective-permute-start.6) | collective-permute-done | bytes 65568 | tf_op jit(solution)/shard_map/ppermute | solution.py:45
  39.4 21.1 %all-to-all-done = bf16[32,144,64]{1,2,0:T(8,128)(2,1)S(1)} async-done(((bf16[32,144,64]{1,2,0:T(8,128)(2,1)}), bf16[32,144,64]{1,2,0:T(8,128)(2,1)S(1)}, u32[]{:S(2)}, u32[]{:S(2)}) %all-to-all-start) | async-done | bytes 589856 | tf_op jit(solution)/shard_map/all_to_all | solution.py:27
  61.1 1.8 %reshape_reshape.6 = bf16[9,512,64]{1,0,2:T(8,128)(2,1)S(1)} reshape(bf16[32,144,64]{1,0,2:T(8,128)(2,1)S(1)} %copy.13) | data formatting | bytes 1179648 | tf_op jit(solution)/shard_map/reshape;reshape | solution.py:75
  66.9 1.6 %fusion = f32[9,512,64]{1,2,0:T(8,128)} fusion(bf16[9,512,64]{1,2,0:T(8,128)(2,1)S(1)} %get-tuple-element.6, bf16[1,9,64,512]{3,2,1,0:T(8,128)(2,1)S(1)} %fusion.64, f32[512,64]{0,1:T(8,128)S(1)} %multiply_multiply_fusion, bf16[512,512]{1,0:T(8,128)(2,1)S(1)} %bitcast_dynamic-update-slice_fusion.1), kind=kOutput, calls=%fused_computation.3 | convolution fusion | flops 302874624 | bytes 3014656 | tf_op jit(solution)/shard_map/nip,nkop->kio/dot_general | solution.py:94
  68.4 1.8 %copy.16 = f32[9,512,64]{2,1,0:T(8,128)S(1)} copy(f32[9,512,64]{1,2,0:T(8,128)} %fusion) | data formatting | bytes 2359296 | tf_op jit(solution)/shard_map/add | solution.py:95
  70.2 2.5 %reshape.444 = f32[96,1,3072]{2,1,0:T(1,128)} reshape(f32[96,48,64]{2,1,0:T(8,128)S(1)} %bitcast.162) | data formatting | bytes 2359296
  72.8 18.5 %all-to-all-start.1 = ((f32[96,1,3072]{2,1,0:T(1,128)}), f32[96,1,3072]{2,1,0:T(1,128)S(1)}, u32[]{:S(2)}, u32[]{:S(2)}) async-start(f32[96,1,3072]{2,1,0:T(1,128)} %reshape.444), calls=%async_computation.1 | async-start | bytes 2359296 | tf_op jit(solution)/shard_map/all_to_all | solution.py:35
  92.1 1.7 %collective-permute-start.13 = (f32[1,64,512]{2,1,0:T(8,128)S(1)}, f32[1,64,512]{2,1,0:T(8,128)S(1)}, u32[]{:S(2)}, u32[]{:S(2)}) collective-permute-start(f32[1,64,512]{2,1,0:T(8,128)S(1)} %get-tuple-element.18), channel_id=1, source_target_pairs={{0,21},{3,0},{6,3},{9,6},{12,9},{15,12},{18,15},{21,18},{1,22},{4,... | collective-permute-start | bytes 393224 | tf_op jit(solution)/shard_map/ppermute | solution.py:59
  93.8 1.9 %collective-permute-start.12 = (f32[1,64,512]{2,1,0:T(8,128)S(1)}, f32[1,64,512]{2,1,0:T(8,128)S(1)}, u32[]{:S(2)}, u32[]{:S(2)}) collective-permute-start(f32[1,64,512]{2,1,0:T(8,128)S(1)} %get-tuple-element.19), channel_id=1, source_target_pairs={{0,18},{3,21},{6,0},{9,3},{12,6},{15,9},{18,12},{21,15},{1,19},{4,... | collective-permute-start | bytes 393224 | tf_op jit(solution)/shard_map/ppermute | solution.py:59
  95.7 2.5 %collective-permute-start.11 = (f32[1,64,512]{2,1,0:T(8,128)S(1)}, f32[1,64,512]{2,1,0:T(8,128)S(1)}, u32[]{:S(2)}, u32[]{:S(2)}) collective-permute-start(f32[1,64,512]{2,1,0:T(8,128)S(1)} %get-tuple-element.20), channel_id=1, source_target_pairs={{0,15},{3,18},{6,21},{9,0},{12,3},{15,6},{18,9},{21,12},{1,16},{4,... | collective-permute-start | bytes 393224 | tf_op jit(solution)/shard_map/ppermute | solution.py:59
  98.2 4.6 %collective-permute-start.10 = (f32[1,64,512]{2,1,0:T(8,128)S(1)}, f32[1,64,512]{2,1,0:T(8,128)S(1)}, u32[]{:S(2)}, u32[]{:S(2)}) collective-permute-start(f32[1,64,512]{2,1,0:T(8,128)S(1)} %get-tuple-element.21), channel_id=1, source_target_pairs={{0,12},{3,15},{6,18},{9,21},{12,0},{15,3},{18,6},{21,9},{1,13},{4,... | collective-permute-start | bytes 393224 | tf_op jit(solution)/shard_map/ppermute | solution.py:59
  102.8 1.9 %collective-permute-start.9 = (f32[1,64,512]{2,1,0:T(8,128)S(1)}, f32[1,64,512]{2,1,0:T(8,128)S(1)}, u32[]{:S(2)}, u32[]{:S(2)}) collective-permute-start(f32[1,64,512]{2,1,0:T(8,128)S(1)} %get-tuple-element.22), channel_id=1, source_target_pairs={{0,9},{3,12},{6,15},{9,18},{12,21},{15,0},{18,3},{21,6},{1,10},{4,... | collective-permute-start | bytes 393224 | tf_op jit(solution)/shard_map/ppermute | solution.py:59
  104.7 4.4 %collective-permute-start.8 = (f32[1,64,512]{2,1,0:T(8,128)S(1)}, f32[1,64,512]{2,1,0:T(8,128)S(1)}, u32[]{:S(2)}, u32[]{:S(2)}) collective-permute-start(f32[1,64,512]{2,1,0:T(8,128)S(1)} %get-tuple-element.23), channel_id=1, source_target_pairs={{0,6},{3,9},{6,12},{9,15},{12,18},{15,21},{18,0},{21,3},{1,7},{4,1... | collective-permute-start | bytes 393224 | tf_op jit(solution)/shard_map/ppermute | solution.py:59
  110.6 2.7 %collective-permute-done.8 = f32[1,64,512]{2,1,0:T(8,128)S(1)} collective-permute-done((f32[1,64,512]{2,1,0:T(8,128)S(1)}, f32[1,64,512]{2,1,0:T(8,128)S(1)}, u32[]{:S(2)}, u32[]{:S(2)}) %collective-permute-start.8) | collective-permute-done | bytes 131104 | tf_op jit(solution)/shard_map/ppermute | solution.py:59
  114.0 24.4 %all-to-all-done.1 = f32[96,1,3072]{2,1,0:T(1,128)S(1)} async-done(((f32[96,1,3072]{2,1,0:T(1,128)}), f32[96,1,3072]{2,1,0:T(1,128)S(1)}, u32[]{:S(2)}, u32[]{:S(2)}) %all-to-all-start.1) | async-done | bytes 1179680 | tf_op jit(solution)/shard_map/all_to_all | solution.py:35
  138.9 3.4 %reduce.1 = f32[96,3072]{1,0:T(8,128)S(1)} reduce(f32[96,1,3072]{2,1,0:T(1,128)S(1)} %all-to-all-done.1, f32[]{:T(128)} %broadcast.516), dimensions={1}, to_apply=%all_to_all.7.reduce_sub_computation | reduce | bytes 2359300 | tf_op jit(solution)/shard_map/all_to_all | solution.py:35
  (67 shorter events, 12.3 us)
Async XLA Ops:
  1.4 1.0 copy-start.5
  2.3 35.3 %collective-permute-start.5 = (bf16[1,64,512]{2,1,0:T(8,128)(2,1)S(1)}, bf16[1,64,512]{2,1,0:T(8,128)(2,1)S(1)}, u32[]{:S(2)}, u32[]{:S(2)}) collective-permute-start(bf16[1,64,512]{2,1,0:T(8,128)(2,1)S(1)} %get-tuple-element.8), channel_id=1, source_target_pairs={{0,18},{3,21},{6,0},{9,3},{12,6},{15,9},{18,12},{21,15},{1,19},{4,... | collective-permute-start | bytes 196616 | tf_op jit(solution)/shard_map/ppermute | solution.py:45
  4.8 32.8 %collective-permute-start.4 = (bf16[1,64,512]{2,1,0:T(8,128)(2,1)S(1)}, bf16[1,64,512]{2,1,0:T(8,128)(2,1)S(1)}, u32[]{:S(2)}, u32[]{:S(2)}) collective-permute-start(bf16[1,64,512]{2,1,0:T(8,128)(2,1)S(1)} %get-tuple-element.8), channel_id=1, source_target_pairs={{0,15},{3,18},{6,21},{9,0},{12,3},{15,6},{18,9},{21,12},{1,16},{4,... | collective-permute-start | bytes 196616 | tf_op jit(solution)/shard_map/ppermute | solution.py:45
  8.3 29.3 %collective-permute-start.3 = (bf16[1,64,512]{2,1,0:T(8,128)(2,1)S(1)}, bf16[1,64,512]{2,1,0:T(8,128)(2,1)S(1)}, u32[]{:S(2)}, u32[]{:S(2)}) collective-permute-start(bf16[1,64,512]{2,1,0:T(8,128)(2,1)S(1)} %get-tuple-element.8), channel_id=1, source_target_pairs={{0,12},{3,15},{6,18},{9,21},{12,0},{15,3},{18,6},{21,9},{1,13},{4,... | collective-permute-start | bytes 196616 | tf_op jit(solution)/shard_map/ppermute | solution.py:45
  11.3 26.2 %collective-permute-start.2 = (bf16[1,64,512]{2,1,0:T(8,128)(2,1)S(1)}, bf16[1,64,512]{2,1,0:T(8,128)(2,1)S(1)}, u32[]{:S(2)}, u32[]{:S(2)}) collective-permute-start(bf16[1,64,512]{2,1,0:T(8,128)(2,1)S(1)} %get-tuple-element.8), channel_id=1, source_target_pairs={{0,9},{3,12},{6,15},{9,18},{12,21},{15,0},{18,3},{21,6},{1,10},{4,... | collective-permute-start | bytes 196616 | tf_op jit(solution)/shard_map/ppermute | solution.py:45
  15.0 15.5 %collective-permute-start = (bf16[1,64,512]{2,1,0:T(8,128)(2,1)S(1)}, bf16[1,64,512]{2,1,0:T(8,128)(2,1)S(1)}, u32[]{:S(2)}, u32[]{:S(2)}) collective-permute-start(bf16[1,64,512]{2,1,0:T(8,128)(2,1)S(1)} %get-tuple-element.8), channel_id=1, source_target_pairs={{0,3},{3,6},{6,9},{9,12},{12,15},{15,18},{18,21},{21,0},{1,4},{4,7... | collective-permute-start | bytes 196616 | tf_op jit(solution)/shard_map/ppermute | solution.py:45
  17.6 12.8 %copy-start.2 = (f32[1,512]{1,0:T(1,128)S(1)}, f32[1,512]{1,0:T(1,128)}, u32[]{:S(2)}) copy-start(f32[1,512]{1,0:T(1,128)} %param.7) | copy-start | bytes 6148
  17.7 42.8 %all-to-all-start = ((bf16[32,144,64]{1,2,0:T(8,128)(2,1)}), bf16[32,144,64]{1,2,0:T(8,128)(2,1)S(1)}, u32[]{:S(2)}, u32[]{:S(2)}) async-start(bf16[32,144,64]{1,2,0:T(8,128)(2,1)} %broadcast_in_dim.2), calls=%async_computation | async-start | bytes 2097152 | tf_op jit(solution)/shard_map/all_to_all | solution.py:27
  30.5 6.5 %collective-permute-start.1 = (bf16[1,64,512]{2,1,0:T(8,128)(2,1)S(1)}, bf16[1,64,512]{2,1,0:T(8,128)(2,1)S(1)}, u32[]{:S(2)}, u32[]{:S(2)}) collective-permute-start(bf16[1,64,512]{2,1,0:T(8,128)(2,1)S(1)} %get-tuple-element.8), channel_id=1, source_target_pairs={{0,6},{3,9},{6,12},{9,15},{12,18},{15,21},{18,0},{21,3},{1,7},{4,1... | collective-permute-start | bytes 196616 | tf_op jit(solution)/shard_map/ppermute | solution.py:45
  37.1 2.4 %collective-permute-start.6 = (bf16[1,64,512]{2,1,0:T(8,128)(2,1)S(1)}, bf16[1,64,512]{2,1,0:T(8,128)(2,1)S(1)}, u32[]{:S(2)}, u32[]{:S(2)}) collective-permute-start(bf16[1,64,512]{2,1,0:T(8,128)(2,1)S(1)} %get-tuple-element.8), channel_id=1, source_target_pairs={{0,21},{3,0},{6,3},{9,6},{12,9},{15,12},{18,15},{21,18},{1,22},{4,... | collective-permute-start | bytes 196616 | tf_op jit(solution)/shard_map/ppermute | solution.py:45
  63.5 2.5 %copy-start.3 = (f32[64]{0:T(128)}, f32[64]{0:T(128)S(1)}, u32[]{:S(2)}) copy-start(f32[64]{0:T(128)S(1)} %fusion.3) | copy-start | bytes 772
  64.0 0.8 copy-start.1
  72.8 65.7 %all-to-all-start.1 = ((f32[96,1,3072]{2,1,0:T(1,128)}), f32[96,1,3072]{2,1,0:T(1,128)S(1)}, u32[]{:S(2)}, u32[]{:S(2)}) async-start(f32[96,1,3072]{2,1,0:T(1,128)} %reshape.444), calls=%async_computation.1 | async-start | bytes 2359296 | tf_op jit(solution)/shard_map/all_to_all | solution.py:35
  91.9 17.2 %copy-start = (f32[1,64,512]{2,1,0:T(8,128)S(1)}, f32[1,64,512]{2,1,0:T(8,128)}, u32[]{:S(2)}) copy-start(f32[1,64,512]{2,1,0:T(8,128)} %get-tuple-element.4) | copy-start | bytes 393220
  91.9 17.2 %copy-start.4 = (f32[64]{0:T(128)S(1)}, f32[64]{0:T(128)}, u32[]{:S(2)}) copy-start(f32[64]{0:T(128)} %copy-done.3) | copy-start | bytes 772
  91.9 17.2 %copy-start.7 = (f32[64]{0:T(128)S(1)}, f32[64]{0:T(128)}, u32[]{:S(2)}) copy-start(f32[64]{0:T(128)} %param.8) | copy-start | bytes 772
  91.9 21.4 %copy-start.6 = (f32[64]{0:T(128)S(1)}, f32[64]{0:T(128)}, u32[]{:S(2)}) copy-start(f32[64]{0:T(128)} %copy-done.5) | copy-start | bytes 772
  92.0 10.8 %collective-permute-start.7 = (f32[1,64,512]{2,1,0:T(8,128)S(1)}, f32[1,64,512]{2,1,0:T(8,128)S(1)}, u32[]{:S(2)}, u32[]{:S(2)}) collective-permute-start(f32[1,64,512]{2,1,0:T(8,128)S(1)} %get-tuple-element.17), channel_id=1, source_target_pairs={{0,3},{3,6},{6,9},{9,12},{12,15},{15,18},{18,21},{21,0},{1,4},{4,7... | collective-permute-start | bytes 393224 | tf_op jit(solution)/shard_map/ppermute | solution.py:59
  92.1 12.7 %collective-permute-start.13 = (f32[1,64,512]{2,1,0:T(8,128)S(1)}, f32[1,64,512]{2,1,0:T(8,128)S(1)}, u32[]{:S(2)}, u32[]{:S(2)}) collective-permute-start(f32[1,64,512]{2,1,0:T(8,128)S(1)} %get-tuple-element.18), channel_id=1, source_target_pairs={{0,21},{3,0},{6,3},{9,6},{12,9},{15,12},{18,15},{21,18},{1,22},{4,... | collective-permute-start | bytes 393224 | tf_op jit(solution)/shard_map/ppermute | solution.py:59
  93.8 16.1 %collective-permute-start.12 = (f32[1,64,512]{2,1,0:T(8,128)S(1)}, f32[1,64,512]{2,1,0:T(8,128)S(1)}, u32[]{:S(2)}, u32[]{:S(2)}) collective-permute-start(f32[1,64,512]{2,1,0:T(8,128)S(1)} %get-tuple-element.19), channel_id=1, source_target_pairs={{0,18},{3,21},{6,0},{9,3},{12,6},{15,9},{18,12},{21,15},{1,19},{4,... | collective-permute-start | bytes 393224 | tf_op jit(solution)/shard_map/ppermute | solution.py:59
  95.7 14.2 %collective-permute-start.11 = (f32[1,64,512]{2,1,0:T(8,128)S(1)}, f32[1,64,512]{2,1,0:T(8,128)S(1)}, u32[]{:S(2)}, u32[]{:S(2)}) collective-permute-start(f32[1,64,512]{2,1,0:T(8,128)S(1)} %get-tuple-element.20), channel_id=1, source_target_pairs={{0,15},{3,18},{6,21},{9,0},{12,3},{15,6},{18,9},{21,12},{1,16},{4,... | collective-permute-start | bytes 393224 | tf_op jit(solution)/shard_map/ppermute | solution.py:59
  98.2 11.7 %collective-permute-start.10 = (f32[1,64,512]{2,1,0:T(8,128)S(1)}, f32[1,64,512]{2,1,0:T(8,128)S(1)}, u32[]{:S(2)}, u32[]{:S(2)}) collective-permute-start(f32[1,64,512]{2,1,0:T(8,128)S(1)} %get-tuple-element.21), channel_id=1, source_target_pairs={{0,12},{3,15},{6,18},{9,21},{12,0},{15,3},{18,6},{21,9},{1,13},{4,... | collective-permute-start | bytes 393224 | tf_op jit(solution)/shard_map/ppermute | solution.py:59
  102.8 7.8 %collective-permute-start.9 = (f32[1,64,512]{2,1,0:T(8,128)S(1)}, f32[1,64,512]{2,1,0:T(8,128)S(1)}, u32[]{:S(2)}, u32[]{:S(2)}) collective-permute-start(f32[1,64,512]{2,1,0:T(8,128)S(1)} %get-tuple-element.22), channel_id=1, source_target_pairs={{0,9},{3,12},{6,15},{9,18},{12,21},{15,0},{18,3},{21,6},{1,10},{4,... | collective-permute-start | bytes 393224 | tf_op jit(solution)/shard_map/ppermute | solution.py:59
  104.7 8.6 %collective-permute-start.8 = (f32[1,64,512]{2,1,0:T(8,128)S(1)}, f32[1,64,512]{2,1,0:T(8,128)S(1)}, u32[]{:S(2)}, u32[]{:S(2)}) collective-permute-start(f32[1,64,512]{2,1,0:T(8,128)S(1)} %get-tuple-element.23), channel_id=1, source_target_pairs={{0,6},{3,9},{6,12},{9,15},{12,18},{15,21},{18,0},{21,3},{1,7},{4,1... | collective-permute-start | bytes 393224 | tf_op jit(solution)/shard_map/ppermute | solution.py:59

commit v4 on v3

--- a/solution.py
+++ b/solution.py
@@ -1,7 +1,7 @@
 import jax
 import jax.numpy as jnp
 from jax import lax
-from jax.sharding import PartitionSpec as P
+from jax.sharding import Mesh, PartitionSpec as P
 
 WIDTH = 64
 ROWS = 8
@@ -60,6 +60,22 @@
     return total
 
 
+SAMPLE = ("z_hi_half", "z_lo_half", "y_hi", "y_lo")
+NEAR = ("z_lo_half", "y_lo")
+FAR = ("z_hi_half", "y_hi", "dom")
+
+
+def sum_in_two_stages(terms):
+    sizes = {axis: lax.axis_size(axis) for axis in SAMPLE + ("dom",)}
+    owners = terms.reshape([sizes[axis] for axis in SAMPLE + ("dom",)] + [-1, terms.shape[1]])
+    order = SAMPLE + ("dom",)
+    owners = jnp.transpose(owners, [order.index(axis) for axis in NEAR + FAR] + [5, 6])
+    near = sizes[NEAR[0]] * sizes[NEAR[1]]
+    owners = owners.reshape((near, -1) + owners.shape[-2:])
+    partial = jnp.sum(lax.all_to_all(owners, NEAR, 0, 0, tiled=True), axis=0)
+    return jnp.sum(lax.all_to_all(partial, FAR, 0, 0, tiled=True), axis=0)
+
+
 def per_device(features, weight, style, bias, adjoint):
     local_ch = features.shape[1]
     sect_count = lax.axis_size("sect")
@@ -70,8 +86,10 @@
     own_style = lax.dynamic_slice_in_dim(style, sect_place * local_ch, local_ch, 1)
     local_mod = (features.astype(jnp.float32) * own_style[:, :, None]).astype(jnp.bfloat16)
     modulated = gather_by_permutes(local_mod, "sect", sect_count)
-    sample_count = lax.axis_size("sample")
-    full_weight = gather_by_exchange(weight, "sample", sample_count).reshape(-1, local_ch)
+    sample_count = 1
+    for axis in SAMPLE:
+        sample_count *= lax.axis_size(axis)
+    full_weight = gather_by_exchange(weight, SAMPLE, sample_count).reshape(-1, local_ch)
     kernel = full_weight.reshape(9, channels, local_ch)
     kernel_f = kernel.astype(jnp.float32)
     products = jnp.einsum("kio,nip->nkop", kernel, modulated, preferred_element_type=jnp.float32)
@@ -93,7 +111,7 @@
     )
     grad_main = jnp.einsum("nip,nkop->kio", modulated, back_shifts, preferred_element_type=jnp.float32)
     grad_terms = (grad_main + 2.0 * kernel_f * coupling[None]).reshape(-1, local_ch)
-    grad_weight = sum_by_exchange(grad_terms, ("sample", "dom"))
+    grad_weight = sum_in_two_stages(grad_terms)
     back = jnp.einsum("kio,nkop->nip", kernel, back_shifts, preferred_element_type=jnp.float32)
     summed = sum_by_permutes(back, "sect", sect_count)
     grad_features = (summed * own_style[:, :, None]).astype(jnp.bfloat16)
@@ -101,18 +119,24 @@
 
 
 def solution(mesh):
+    z_lo, y = 4, mesh.shape["sample"] // 4
+    fine = Mesh(
+        mesh.devices.reshape((2, z_lo // 2, y // 2, 2) + mesh.devices.shape[1:]),
+        SAMPLE + ("sect", "dom"),
+    )
+    rows = SAMPLE + ("dom",)
     in_specs = (
-        P(("sample", "dom"), "sect", None),
-        P("sample", "sect"),
-        P(("sample", "dom"), None),
+        P(rows, "sect", None),
+        P(SAMPLE, "sect"),
+        P(rows, None),
         P("sect"),
-        P(("sample", "dom"), "sect", None),
+        P(rows, "sect", None),
     )
     out_specs = (
-        P(("sample", "dom"), "sect", None),
-        P(("sample", "dom"), "sect"),
-        P(("sample", "dom"), "sect", None),
+        P(rows, "sect", None),
+        P(rows, "sect"),
+        P(rows, "sect", None),
     )
     return jax.shard_map(
-        per_device, mesh=mesh, in_specs=in_specs, out_specs=out_specs, check_vma=False
+        per_device, mesh=fine, in_specs=in_specs, out_specs=out_specs, check_vma=False
     )

time: 145 us -> 152 us (1.048)
  the two profiles are of different devices: /device:TPU:50 before, /device:TPU:1 now
where the time goes in v4:
time: 152 us; the launch traced here: 151 us
  starting transfers between devices  72 us (47%)
  waiting for transfers between devices  26 us (17%)
  local copies, waits for them, and re-layouts  18.1 us (12%)
  blocking collectives  17.7 us (12%)
  other arithmetic  12.9 us (8%)
  matrix products  2.83 us (2%)
    ppermute x7, starting transfers between devices, gather_by_permutes(): arrived = lax.ppermute(block, axis, pairs)  26.4 us
    ppermute x7, starting transfers between devices, sum_by_permutes(): total = total + lax.ppermute(part, axis, pairs)  24.3 us
    all_to_all x1, blocking collectives, sum_in_two_stages(): partial = jnp.sum(lax.all_to_all(owners, NEAR, 0, 0, tiled=True), axis=0)  17.7 us
    all_to_all x1, starting transfers between devices, sum_in_two_stages(): return jnp.sum(lax.all_to_all(partial, FAR, 0, 0, tiled=True), axis=0)  14.9 us
    all_to_all x1, waiting for transfers between devices, gather_by_exchange(): return lax.all_to_all(copies, axis, 0, 0, tiled=True)  14.8 us
    unnamed x20, local copies, waits for them, and re-layouts  8.75 us
    all_to_all x1, starting transfers between devices, gather_by_exchange(): return lax.all_to_all(copies, axis, 0, 0, tiled=True)  6.46 us
    ppermute x7, waiting for transfers between devices, sum_by_permutes(): total = total + lax.ppermute(part, axis, pairs)  5.69 us
  transfers between devices with their start and end apart: 16, of which 5 were waited for; matrix products, arithmetic and copies ran while one was open for 3% of the time, Pallas kernels for 0%

profile of v4, /device:TPU:1, one launch (start us, length us, event | category | flops | bytes accessed | tf_op | source)
XLA Modules:
  0.0 150.8 jit_solution(6138157220852608641)
XLA Ops:
  2.3 5.2 %collective-permute-start.5 = (bf16[1,64,512]{2,1,0:T(8,128)(2,1)S(1)}, bf16[1,64,512]{2,1,0:T(8,128)(2,1)S(1)}, u32[]{:S(2)}, u32[]{:S(2)}) collective-permute-start(bf16[1,64,512]{2,1,0:T(8,128)(2,1)S(1)} %get-tuple-element.8), channel_id=1, source_target_pairs={{0,18},{3,21},{6,0},{9,3},{12,6},{15,9},{18,12},{21,15},{1,19},{4,... | collective-permute-start | bytes 196616 | tf_op jit(solution)/shard_map/ppermute | solution.py:45
  7.6 3.3 %collective-permute-start.4 = (bf16[1,64,512]{2,1,0:T(8,128)(2,1)S(1)}, bf16[1,64,512]{2,1,0:T(8,128)(2,1)S(1)}, u32[]{:S(2)}, u32[]{:S(2)}) collective-permute-start(bf16[1,64,512]{2,1,0:T(8,128)(2,1)S(1)} %get-tuple-element.8), channel_id=1, source_target_pairs={{0,15},{3,18},{6,21},{9,0},{12,3},{15,6},{18,9},{21,12},{1,16},{4,... | collective-permute-start | bytes 196616 | tf_op jit(solution)/shard_map/ppermute | solution.py:45
  10.9 11.1 %collective-permute-start.3 = (bf16[1,64,512]{2,1,0:T(8,128)(2,1)S(1)}, bf16[1,64,512]{2,1,0:T(8,128)(2,1)S(1)}, u32[]{:S(2)}, u32[]{:S(2)}) collective-permute-start(bf16[1,64,512]{2,1,0:T(8,128)(2,1)S(1)} %get-tuple-element.8), channel_id=1, source_target_pairs={{0,12},{3,15},{6,18},{9,21},{12,0},{15,3},{18,6},{21,9},{1,13},{4,... | collective-permute-start | bytes 196616 | tf_op jit(solution)/shard_map/ppermute | solution.py:45
  22.0 1.9 %collective-permute-start.2 = (bf16[1,64,512]{2,1,0:T(8,128)(2,1)S(1)}, bf16[1,64,512]{2,1,0:T(8,128)(2,1)S(1)}, u32[]{:S(2)}, u32[]{:S(2)}) collective-permute-start(bf16[1,64,512]{2,1,0:T(8,128)(2,1)S(1)} %get-tuple-element.8), channel_id=1, source_target_pairs={{0,9},{3,12},{6,15},{9,18},{12,21},{15,0},{18,3},{21,6},{1,10},{4,... | collective-permute-start | bytes 196616 | tf_op jit(solution)/shard_map/ppermute | solution.py:45
  23.9 1.9 %broadcast_in_dim.2 = bf16[32,144,64]{1,2,0:T(8,128)(2,1)} broadcast(bf16[144,64]{0,1:T(8,128)(2,1)} %param.6), dimensions={1,2} | broadcast | bytes 608256 | tf_op jit(solution)/shard_map/broadcast_in_dim | solution.py:26
  25.8 6.5 %all-to-all-start = ((bf16[32,144,64]{1,2,0:T(8,128)(2,1)}), bf16[32,144,64]{1,2,0:T(8,128)(2,1)S(1)}, u32[]{:S(2)}, u32[]{:S(2)}) async-start(bf16[32,144,64]{1,2,0:T(8,128)(2,1)} %broadcast_in_dim.2), calls=%async_computation | async-start | bytes 2097152 | tf_op jit(solution)/shard_map/all_to_all | solution.py:27
  32.5 3.4 %collective-permute-start.1 = (bf16[1,64,512]{2,1,0:T(8,128)(2,1)S(1)}, bf16[1,64,512]{2,1,0:T(8,128)(2,1)S(1)}, u32[]{:S(2)}, u32[]{:S(2)}) collective-permute-start(bf16[1,64,512]{2,1,0:T(8,128)(2,1)S(1)} %get-tuple-element.8), channel_id=1, source_target_pairs={{0,6},{3,9},{6,12},{9,15},{12,18},{15,21},{18,0},{21,3},{1,7},{4,1... | collective-permute-start | bytes 196616 | tf_op jit(solution)/shard_map/ppermute | solution.py:45
  35.9 3.1 %collective-permute-done.1 = bf16[1,64,512]{2,1,0:T(8,128)(2,1)S(1)} collective-permute-done((bf16[1,64,512]{2,1,0:T(8,128)(2,1)S(1)}, bf16[1,64,512]{2,1,0:T(8,128)(2,1)S(1)}, u32[]{:S(2)}, u32[]{:S(2)}) %collective-permute-start.1) | collective-permute-done | bytes 65568 | tf_op jit(solution)/shard_map/ppermute | solution.py:45
  40.5 2.4 %collective-permute-done.6 = bf16[1,64,512]{2,1,0:T(8,128)(2,1)S(1)} collective-permute-done((bf16[1,64,512]{2,1,0:T(8,128)(2,1)S(1)}, bf16[1,64,512]{2,1,0:T(8,128)(2,1)S(1)}, u32[]{:S(2)}, u32[]{:S(2)}) %collective-permute-start.6) | collective-permute-done | bytes 65568 | tf_op jit(solution)/shard_map/ppermute | solution.py:45
  43.0 14.8 %all-to-all-done = bf16[32,144,64]{1,2,0:T(8,128)(2,1)S(1)} async-done(((bf16[32,144,64]{1,2,0:T(8,128)(2,1)}), bf16[32,144,64]{1,2,0:T(8,128)(2,1)S(1)}, u32[]{:S(2)}, u32[]{:S(2)}) %all-to-all-start) | async-done | bytes 589856 | tf_op jit(solution)/shard_map/all_to_all | solution.py:27
  69.2 3.3 %reshape.448 = f32[4,1,73728]{2,1,0:T(1,128)S(1)} reshape(f32[4,24,48,64]{3,2,1,0:T(8,128)} %bitcast.166) | data formatting | bytes 2359296
  72.5 17.7 %all_to_all.15 = f32[4,1,73728]{2,1,0:T(1,128)S(1)} all-to-all(f32[4,1,73728]{2,1,0:T(1,128)S(1)} %reshape.448), channel_id=1, replica_groups=mesh['z_hi_half'=2,'z_lo_half'=2,'y_hi'=4,'y_lo'=2,'sect'=8,'dom'=3] {'z..., dimensions={0} | all-to-all | bytes 2359296 | tf_op jit(solution)/shard_map/all_to_all | solution.py:75
  90.8 5.1 %reduce.1 = f32[4,73728]{1,0:T(4,128)} reduce(f32[4,1,73728]{2,1,0:T(1,128)S(1)} %all_to_all.15, f32[]{:T(128)} %broadcast.516), dimensions={1}, to_apply=%all_to_all.10.reduce_sub_computation | reduce | bytes 2359300 | tf_op jit(solution)/shard_map/all_to_all | solution.py:75
  95.9 2.4 %reshape.449 = f32[4,24,48,64]{3,2,1,0:T(8,128)S(1)} reshape(f32[4,73728]{1,0:T(4,128)} %reduce.1) | data formatting | bytes 2359296
  99.4 2.1 %reshape.450 = f32[24,1,3072]{2,1,0:T(1,128)} reshape(f32[24,48,64]{2,1,0:T(8,128)} %reduce_sum.38) | data formatting | bytes 589824
  101.5 14.9 %all-to-all-start.2 = ((f32[24,1,3072]{2,1,0:T(1,128)}), f32[24,1,3072]{2,1,0:T(1,128)S(1)}, u32[]{:S(2)}, u32[]{:S(2)}) async-start(f32[24,1,3072]{2,1,0:T(1,128)} %reshape.450), calls=%async_computation.2 | async-start | bytes 589824 | tf_op jit(solution)/shard_map/all_to_all | solution.py:76
  117.2 9.1 %collective-permute-start.7 = (f32[1,64,512]{2,1,0:T(8,128)S(1)}, f32[1,64,512]{2,1,0:T(8,128)S(1)}, u32[]{:S(2)}, u32[]{:S(2)}) collective-permute-start(f32[1,64,512]{2,1,0:T(8,128)S(1)} %get-tuple-element.17), channel_id=1, source_target_pairs={{0,3},{3,6},{6,9},{9,12},{12,15},{15,18},{18,21},{21,0},{1,4},{4,7... | collective-permute-start | bytes 393224 | tf_op jit(solution)/shard_map/ppermute | solution.py:59
  126.3 2.1 %collective-permute-start.12 = (f32[1,64,512]{2,1,0:T(8,128)S(1)}, f32[1,64,512]{2,1,0:T(8,128)S(1)}, u32[]{:S(2)}, u32[]{:S(2)}) collective-permute-start(f32[1,64,512]{2,1,0:T(8,128)S(1)} %get-tuple-element.19), channel_id=1, source_target_pairs={{0,18},{3,21},{6,0},{9,3},{12,6},{15,9},{18,12},{21,15},{1,19},{4,... | collective-permute-start | bytes 393224 | tf_op jit(solution)/shard_map/ppermute | solution.py:59
  128.4 3.5 %collective-permute-start.11 = (f32[1,64,512]{2,1,0:T(8,128)S(1)}, f32[1,64,512]{2,1,0:T(8,128)S(1)}, u32[]{:S(2)}, u32[]{:S(2)}) collective-permute-start(f32[1,64,512]{2,1,0:T(8,128)S(1)} %get-tuple-element.20), channel_id=1, source_target_pairs={{0,15},{3,18},{6,21},{9,0},{12,3},{15,6},{18,9},{21,12},{1,16},{4,... | collective-permute-start | bytes 393224 | tf_op jit(solution)/shard_map/ppermute | solution.py:59
  131.9 3.6 %collective-permute-start.10 = (f32[1,64,512]{2,1,0:T(8,128)S(1)}, f32[1,64,512]{2,1,0:T(8,128)S(1)}, u32[]{:S(2)}, u32[]{:S(2)}) collective-permute-start(f32[1,64,512]{2,1,0:T(8,128)S(1)} %get-tuple-element.21), channel_id=1, source_target_pairs={{0,12},{3,15},{6,18},{9,21},{12,0},{15,3},{18,6},{21,9},{1,13},{4,... | collective-permute-start | bytes 393224 | tf_op jit(solution)/shard_map/ppermute | solution.py:59
  135.6 3.8 %collective-permute-start.9 = (f32[1,64,512]{2,1,0:T(8,128)S(1)}, f32[1,64,512]{2,1,0:T(8,128)S(1)}, u32[]{:S(2)}, u32[]{:S(2)}) collective-permute-start(f32[1,64,512]{2,1,0:T(8,128)S(1)} %get-tuple-element.22), channel_id=1, source_target_pairs={{0,9},{3,12},{6,15},{9,18},{12,21},{15,0},{18,3},{21,6},{1,10},{4,... | collective-permute-start | bytes 393224 | tf_op jit(solution)/shard_map/ppermute | solution.py:59
  139.4 2.1 %collective-permute-start.8 = (f32[1,64,512]{2,1,0:T(8,128)S(1)}, f32[1,64,512]{2,1,0:T(8,128)S(1)}, u32[]{:S(2)}, u32[]{:S(2)}) collective-permute-start(f32[1,64,512]{2,1,0:T(8,128)S(1)} %get-tuple-element.23), channel_id=1, source_target_pairs={{0,6},{3,9},{6,12},{9,15},{12,18},{15,21},{18,0},{21,3},{1,7},{4,1... | collective-permute-start | bytes 393224 | tf_op jit(solution)/shard_map/ppermute | solution.py:59
  142.3 2.2 %collective-permute-done.9 = f32[1,64,512]{2,1,0:T(8,128)S(1)} collective-permute-done((f32[1,64,512]{2,1,0:T(8,128)S(1)}, f32[1,64,512]{2,1,0:T(8,128)S(1)}, u32[]{:S(2)}, u32[]{:S(2)}) %collective-permute-start.9) | collective-permute-done | bytes 131104 | tf_op jit(solution)/shard_map/ppermute | solution.py:59
  144.5 3.5 %collective-permute-done.8 = f32[1,64,512]{2,1,0:T(8,128)S(1)} collective-permute-done((f32[1,64,512]{2,1,0:T(8,128)S(1)}, f32[1,64,512]{2,1,0:T(8,128)S(1)}, u32[]{:S(2)}, u32[]{:S(2)}) %collective-permute-start.8) | collective-permute-done | bytes 131104 | tf_op jit(solution)/shard_map/ppermute | solution.py:59
  (73 shorter events, 20.6 us)
Async XLA Ops:
  1.4 1.0 copy-start.5
  2.3 38.2 %collective-permute-start.5 = (bf16[1,64,512]{2,1,0:T(8,128)(2,1)S(1)}, bf16[1,64,512]{2,1,0:T(8,128)(2,1)S(1)}, u32[]{:S(2)}, u32[]{:S(2)}) collective-permute-start(bf16[1,64,512]{2,1,0:T(8,128)(2,1)S(1)} %get-tuple-element.8), channel_id=1, source_target_pairs={{0,18},{3,21},{6,0},{9,3},{12,6},{15,9},{18,12},{21,15},{1,19},{4,... | collective-permute-start | bytes 196616 | tf_op jit(solution)/shard_map/ppermute | solution.py:45
  7.6 32.9 %collective-permute-start.4 = (bf16[1,64,512]{2,1,0:T(8,128)(2,1)S(1)}, bf16[1,64,512]{2,1,0:T(8,128)(2,1)S(1)}, u32[]{:S(2)}, u32[]{:S(2)}) collective-permute-start(bf16[1,64,512]{2,1,0:T(8,128)(2,1)S(1)} %get-tuple-element.8), channel_id=1, source_target_pairs={{0,15},{3,18},{6,21},{9,0},{12,3},{15,6},{18,9},{21,12},{1,16},{4,... | collective-permute-start | bytes 196616 | tf_op jit(solution)/shard_map/ppermute | solution.py:45
  10.9 29.6 %collective-permute-start.3 = (bf16[1,64,512]{2,1,0:T(8,128)(2,1)S(1)}, bf16[1,64,512]{2,1,0:T(8,128)(2,1)S(1)}, u32[]{:S(2)}, u32[]{:S(2)}) collective-permute-start(bf16[1,64,512]{2,1,0:T(8,128)(2,1)S(1)} %get-tuple-element.8), channel_id=1, source_target_pairs={{0,12},{3,15},{6,18},{9,21},{12,0},{15,3},{18,6},{21,9},{1,13},{4,... | collective-permute-start | bytes 196616 | tf_op jit(solution)/shard_map/ppermute | solution.py:45
  22.0 18.4 %collective-permute-start.2 = (bf16[1,64,512]{2,1,0:T(8,128)(2,1)S(1)}, bf16[1,64,512]{2,1,0:T(8,128)(2,1)S(1)}, u32[]{:S(2)}, u32[]{:S(2)}) collective-permute-start(bf16[1,64,512]{2,1,0:T(8,128)(2,1)S(1)} %get-tuple-element.8), channel_id=1, source_target_pairs={{0,9},{3,12},{6,15},{9,18},{12,21},{15,0},{18,3},{21,6},{1,10},{4,... | collective-permute-start | bytes 196616 | tf_op jit(solution)/shard_map/ppermute | solution.py:45
  23.9 8.5 %collective-permute-start = (bf16[1,64,512]{2,1,0:T(8,128)(2,1)S(1)}, bf16[1,64,512]{2,1,0:T(8,128)(2,1)S(1)}, u32[]{:S(2)}, u32[]{:S(2)}) collective-permute-start(bf16[1,64,512]{2,1,0:T(8,128)(2,1)S(1)} %get-tuple-element.8), channel_id=1, source_target_pairs={{0,3},{3,6},{6,9},{9,12},{12,15},{15,18},{18,21},{21,0},{1,4},{4,7... | collective-permute-start | bytes 196616 | tf_op jit(solution)/shard_map/ppermute | solution.py:45
  25.8 6.6 %copy-start.2 = (f32[1,512]{1,0:T(1,128)S(1)}, f32[1,512]{1,0:T(1,128)}, u32[]{:S(2)}) copy-start(f32[1,512]{1,0:T(1,128)} %param.7) | copy-start | bytes 6148
  25.8 32.0 %all-to-all-start = ((bf16[32,144,64]{1,2,0:T(8,128)(2,1)}), bf16[32,144,64]{1,2,0:T(8,128)(2,1)S(1)}, u32[]{:S(2)}, u32[]{:S(2)}) async-start(bf16[32,144,64]{1,2,0:T(8,128)(2,1)} %broadcast_in_dim.2), calls=%async_computation | async-start | bytes 2097152 | tf_op jit(solution)/shard_map/all_to_all | solution.py:27
  32.5 6.5 %collective-permute-start.1 = (bf16[1,64,512]{2,1,0:T(8,128)(2,1)S(1)}, bf16[1,64,512]{2,1,0:T(8,128)(2,1)S(1)}, u32[]{:S(2)}, u32[]{:S(2)}) collective-permute-start(bf16[1,64,512]{2,1,0:T(8,128)(2,1)S(1)} %get-tuple-element.8), channel_id=1, source_target_pairs={{0,6},{3,9},{6,12},{9,15},{12,18},{15,21},{18,0},{21,3},{1,7},{4,1... | collective-permute-start | bytes 196616 | tf_op jit(solution)/shard_map/ppermute | solution.py:45
  39.0 4.0 %collective-permute-start.6 = (bf16[1,64,512]{2,1,0:T(8,128)(2,1)S(1)}, bf16[1,64,512]{2,1,0:T(8,128)(2,1)S(1)}, u32[]{:S(2)}, u32[]{:S(2)}) collective-permute-start(bf16[1,64,512]{2,1,0:T(8,128)(2,1)S(1)} %get-tuple-element.8), channel_id=1, source_target_pairs={{0,21},{3,0},{6,3},{9,6},{12,9},{15,12},{18,15},{21,18},{1,22},{4,... | collective-permute-start | bytes 196616 | tf_op jit(solution)/shard_map/ppermute | solution.py:45
  60.8 2.5 %copy-start.3 = (f32[64]{0:T(128)}, f32[64]{0:T(128)S(1)}, u32[]{:S(2)}) copy-start(f32[64]{0:T(128)S(1)} %fusion.3) | copy-start | bytes 772
  61.3 0.8 copy-start.1
  101.5 47.1 %all-to-all-start.2 = ((f32[24,1,3072]{2,1,0:T(1,128)}), f32[24,1,3072]{2,1,0:T(1,128)S(1)}, u32[]{:S(2)}, u32[]{:S(2)}) async-start(f32[24,1,3072]{2,1,0:T(1,128)} %reshape.450), calls=%async_computation.2 | async-start | bytes 589824 | tf_op jit(solution)/shard_map/all_to_all | solution.py:76
  117.0 24.5 %copy-start = (f32[1,64,512]{2,1,0:T(8,128)S(1)}, f32[1,64,512]{2,1,0:T(8,128)}, u32[]{:S(2)}) copy-start(f32[1,64,512]{2,1,0:T(8,128)} %get-tuple-element.4) | copy-start | bytes 393220
  117.0 24.5 %copy-start.4 = (f32[64]{0:T(128)S(1)}, f32[64]{0:T(128)}, u32[]{:S(2)}) copy-start(f32[64]{0:T(128)} %copy-done.3) | copy-start | bytes 772
  117.1 24.5 %copy-start.7 = (f32[64]{0:T(128)S(1)}, f32[64]{0:T(128)}, u32[]{:S(2)}) copy-start(f32[64]{0:T(128)} %param.8) | copy-start | bytes 772
  117.1 30.9 %copy-start.6 = (f32[64]{0:T(128)S(1)}, f32[64]{0:T(128)}, u32[]{:S(2)}) copy-start(f32[64]{0:T(128)} %copy-done.5) | copy-start | bytes 772
  117.2 18.4 %collective-permute-start.7 = (f32[1,64,512]{2,1,0:T(8,128)S(1)}, f32[1,64,512]{2,1,0:T(8,128)S(1)}, u32[]{:S(2)}, u32[]{:S(2)}) collective-permute-start(f32[1,64,512]{2,1,0:T(8,128)S(1)} %get-tuple-element.17), channel_id=1, source_target_pairs={{0,3},{3,6},{6,9},{9,12},{12,15},{15,18},{18,21},{21,0},{1,4},{4,7... | collective-permute-start | bytes 393224 | tf_op jit(solution)/shard_map/ppermute | solution.py:59
  126.3 13.1 %collective-permute-start.13 = (f32[1,64,512]{2,1,0:T(8,128)S(1)}, f32[1,64,512]{2,1,0:T(8,128)S(1)}, u32[]{:S(2)}, u32[]{:S(2)}) collective-permute-start(f32[1,64,512]{2,1,0:T(8,128)S(1)} %get-tuple-element.18), channel_id=1, source_target_pairs={{0,21},{3,0},{6,3},{9,6},{12,9},{15,12},{18,15},{21,18},{1,22},{4,... | collective-permute-start | bytes 393224 | tf_op jit(solution)/shard_map/ppermute | solution.py:59
  126.3 16.0 %collective-permute-start.12 = (f32[1,64,512]{2,1,0:T(8,128)S(1)}, f32[1,64,512]{2,1,0:T(8,128)S(1)}, u32[]{:S(2)}, u32[]{:S(2)}) collective-permute-start(f32[1,64,512]{2,1,0:T(8,128)S(1)} %get-tuple-element.19), channel_id=1, source_target_pairs={{0,18},{3,21},{6,0},{9,3},{12,6},{15,9},{18,12},{21,15},{1,19},{4,... | collective-permute-start | bytes 393224 | tf_op jit(solution)/shard_map/ppermute | solution.py:59
  128.4 13.9 %collective-permute-start.11 = (f32[1,64,512]{2,1,0:T(8,128)S(1)}, f32[1,64,512]{2,1,0:T(8,128)S(1)}, u32[]{:S(2)}, u32[]{:S(2)}) collective-permute-start(f32[1,64,512]{2,1,0:T(8,128)S(1)} %get-tuple-element.20), channel_id=1, source_target_pairs={{0,15},{3,18},{6,21},{9,0},{12,3},{15,6},{18,9},{21,12},{1,16},{4,... | collective-permute-start | bytes 393224 | tf_op jit(solution)/shard_map/ppermute | solution.py:59
  131.9 10.3 %collective-permute-start.10 = (f32[1,64,512]{2,1,0:T(8,128)S(1)}, f32[1,64,512]{2,1,0:T(8,128)S(1)}, u32[]{:S(2)}, u32[]{:S(2)}) collective-permute-start(f32[1,64,512]{2,1,0:T(8,128)S(1)} %get-tuple-element.21), channel_id=1, source_target_pairs={{0,12},{3,15},{6,18},{9,21},{12,0},{15,3},{18,6},{21,9},{1,13},{4,... | collective-permute-start | bytes 393224 | tf_op jit(solution)/shard_map/ppermute | solution.py:59
  135.6 8.9 %collective-permute-start.9 = (f32[1,64,512]{2,1,0:T(8,128)S(1)}, f32[1,64,512]{2,1,0:T(8,128)S(1)}, u32[]{:S(2)}, u32[]{:S(2)}) collective-permute-start(f32[1,64,512]{2,1,0:T(8,128)S(1)} %get-tuple-element.22), channel_id=1, source_target_pairs={{0,9},{3,12},{6,15},{9,18},{12,21},{15,0},{18,3},{21,6},{1,10},{4,... | collective-permute-start | bytes 393224 | tf_op jit(solution)/shard_map/ppermute | solution.py:59
  139.4 8.5 %collective-permute-start.8 = (f32[1,64,512]{2,1,0:T(8,128)S(1)}, f32[1,64,512]{2,1,0:T(8,128)S(1)}, u32[]{:S(2)}, u32[]{:S(2)}) collective-permute-start(f32[1,64,512]{2,1,0:T(8,128)S(1)} %get-tuple-element.23), channel_id=1, source_target_pairs={{0,6},{3,9},{6,12},{9,15},{12,18},{15,21},{18,0},{21,3},{1,7},{4,1... | collective-permute-start | bytes 393224 | tf_op jit(solution)/shard_map/ppermute | solution.py:59

commit v5 on v3

--- a/solution.py
+++ b/solution.py
@@ -3,8 +3,8 @@
 from jax import lax
 from jax.sharding import PartitionSpec as P
 
+
 WIDTH = 64
-ROWS = 8
 
 
 OFFSETS = [(-1, -1), (-1, 0), (-1, 1), (0, -1), (0, 0), (0, 1), (1, -1), (1, 0), (1, 1)]
@@ -60,13 +60,11 @@
     return total
 
 
-def per_device(features, weight, style, bias, adjoint):
+def layer(features, weight, style, bias, adjoint):
     local_ch = features.shape[1]
     sect_count = lax.axis_size("sect")
     sect_place = lax.axis_index("sect")
     channels = local_ch * sect_count
-    samples = features.shape[0]
-    pixels = features.shape[2]
     own_style = lax.dynamic_slice_in_dim(style, sect_place * local_ch, local_ch, 1)
     local_mod = (features.astype(jnp.float32) * own_style[:, :, None]).astype(jnp.bfloat16)
     modulated = gather_by_permutes(local_mod, "sect", sect_count)
@@ -113,6 +111,4 @@
         P(("sample", "dom"), "sect"),
         P(("sample", "dom"), "sect", None),
     )
-    return jax.shard_map(
-        per_device, mesh=mesh, in_specs=in_specs, out_specs=out_specs, check_vma=False
-    )
+    return jax.shard_map(layer, mesh=mesh, in_specs=in_specs, out_specs=out_specs, check_vma=False)

time: 145 us -> 145 us (level)
  no operation moved by 1% of the time
where the time goes in v5:
time: 145 us; the launch traced here: 144 us
  starting transfers between devices  65.8 us (45%)
  waiting for transfers between devices  53.4 us (37%)
  local copies, waits for them, and re-layouts  11.6 us (8%)
  other arithmetic  8.95 us (6%)
  matrix products  2.84 us (2%)
    all_to_all x1, waiting for transfers between devices, sum_by_exchange(): return jnp.sum(lax.all_to_all(blocks, axes, 0, 0, tiled=True), axis=0)  24.4 us
    all_to_all x1, waiting for transfers between devices, gather_by_exchange(): return lax.all_to_all(copies, axis, 0, 0, tiled=True)  21.1 us
    all_to_all x1, starting transfers between devices, sum_by_exchange(): return jnp.sum(lax.all_to_all(blocks, axes, 0, 0, tiled=True), axis=0)  18.5 us
    ppermute x7, starting transfers between devices, gather_by_permutes(): arrived = lax.ppermute(block, axis, pairs)  17.6 us
    ppermute x7, starting transfers between devices, sum_by_permutes(): total = total + lax.ppermute(part, axis, pairs)  17 us
    all_to_all x1, starting transfers between devices, gather_by_exchange(): return lax.all_to_all(copies, axis, 0, 0, tiled=True)  12.7 us
    ppermute x7, waiting for transfers between devices, gather_by_permutes(): arrived = lax.ppermute(block, axis, pairs)  4.56 us
    unnamed x18, local copies, waits for them, and re-layouts  3.94 us
  transfers between devices with their start and end apart: 16, of which 6 were waited for; matrix products, arithmetic and copies ran while one was open for 3% of the time, Pallas kernels for 0%

profile of v5, /device:TPU:50, one launch (start us, length us, event | category | flops | bytes accessed | tf_op | source)
XLA Modules:
  0.0 143.8 jit_solution(14466861328366327759)
XLA Ops:
  2.3 2.4 %collective-permute-start.5 = (bf16[1,64,512]{2,1,0:T(8,128)(2,1)S(1)}, bf16[1,64,512]{2,1,0:T(8,128)(2,1)S(1)}, u32[]{:S(2)}, u32[]{:S(2)}) collective-permute-start(bf16[1,64,512]{2,1,0:T(8,128)(2,1)S(1)} %get-tuple-element.8), channel_id=1, source_target_pairs={{0,18},{3,21},{6,0},{9,3},{12,6},{15,9},{18,12},{21,15},{1,19},{4,... | collective-permute-start | bytes 196616 | tf_op jit(solution)/shard_map/ppermute | solution.py:45
  4.8 3.5 %collective-permute-start.4 = (bf16[1,64,512]{2,1,0:T(8,128)(2,1)S(1)}, bf16[1,64,512]{2,1,0:T(8,128)(2,1)S(1)}, u32[]{:S(2)}, u32[]{:S(2)}) collective-permute-start(bf16[1,64,512]{2,1,0:T(8,128)(2,1)S(1)} %get-tuple-element.8), channel_id=1, source_target_pairs={{0,15},{3,18},{6,21},{9,0},{12,3},{15,6},{18,9},{21,12},{1,16},{4,... | collective-permute-start | bytes 196616 | tf_op jit(solution)/shard_map/ppermute | solution.py:45
  8.3 3.0 %collective-permute-start.3 = (bf16[1,64,512]{2,1,0:T(8,128)(2,1)S(1)}, bf16[1,64,512]{2,1,0:T(8,128)(2,1)S(1)}, u32[]{:S(2)}, u32[]{:S(2)}) collective-permute-start(bf16[1,64,512]{2,1,0:T(8,128)(2,1)S(1)} %get-tuple-element.8), channel_id=1, source_target_pairs={{0,12},{3,15},{6,18},{9,21},{12,0},{15,3},{18,6},{21,9},{1,13},{4,... | collective-permute-start | bytes 196616 | tf_op jit(solution)/shard_map/ppermute | solution.py:45
  11.3 3.7 %collective-permute-start.2 = (bf16[1,64,512]{2,1,0:T(8,128)(2,1)S(1)}, bf16[1,64,512]{2,1,0:T(8,128)(2,1)S(1)}, u32[]{:S(2)}, u32[]{:S(2)}) collective-permute-start(bf16[1,64,512]{2,1,0:T(8,128)(2,1)S(1)} %get-tuple-element.8), channel_id=1, source_target_pairs={{0,9},{3,12},{6,15},{9,18},{12,21},{15,0},{18,3},{21,6},{1,10},{4,... | collective-permute-start | bytes 196616 | tf_op jit(solution)/shard_map/ppermute | solution.py:45
  15.8 1.9 %broadcast_in_dim.2 = bf16[32,144,64]{1,2,0:T(8,128)(2,1)} broadcast(bf16[144,64]{0,1:T(8,128)(2,1)} %param.6), dimensions={1,2} | broadcast | bytes 608256 | tf_op jit(solution)/shard_map/broadcast_in_dim | solution.py:26
  17.7 12.7 %all-to-all-start = ((bf16[32,144,64]{1,2,0:T(8,128)(2,1)}), bf16[32,144,64]{1,2,0:T(8,128)(2,1)S(1)}, u32[]{:S(2)}, u32[]{:S(2)}) async-start(bf16[32,144,64]{1,2,0:T(8,128)(2,1)} %broadcast_in_dim.2), calls=%async_computation | async-start | bytes 2097152 | tf_op jit(solution)/shard_map/all_to_all | solution.py:27
  30.5 3.7 %collective-permute-start.1 = (bf16[1,64,512]{2,1,0:T(8,128)(2,1)S(1)}, bf16[1,64,512]{2,1,0:T(8,128)(2,1)S(1)}, u32[]{:S(2)}, u32[]{:S(2)}) collective-permute-start(bf16[1,64,512]{2,1,0:T(8,128)(2,1)S(1)} %get-tuple-element.8), channel_id=1, source_target_pairs={{0,6},{3,9},{6,12},{9,15},{12,18},{15,21},{18,0},{21,3},{1,7},{4,1... | collective-permute-start | bytes 196616 | tf_op jit(solution)/shard_map/ppermute | solution.py:45
  34.3 2.8 %collective-permute-done.1 = bf16[1,64,512]{2,1,0:T(8,128)(2,1)S(1)} collective-permute-done((bf16[1,64,512]{2,1,0:T(8,128)(2,1)S(1)}, bf16[1,64,512]{2,1,0:T(8,128)(2,1)S(1)}, u32[]{:S(2)}, u32[]{:S(2)}) %collective-permute-start.1) | collective-permute-done | bytes 65568 | tf_op jit(solution)/shard_map/ppermute | solution.py:45
  37.6 1.8 %collective-permute-done.6 = bf16[1,64,512]{2,1,0:T(8,128)(2,1)S(1)} collective-permute-done((bf16[1,64,512]{2,1,0:T(8,128)(2,1)S(1)}, bf16[1,64,512]{2,1,0:T(8,128)(2,1)S(1)}, u32[]{:S(2)}, u32[]{:S(2)}) %collective-permute-start.6) | collective-permute-done | bytes 65568 | tf_op jit(solution)/shard_map/ppermute | solution.py:45
  39.4 21.1 %all-to-all-done = bf16[32,144,64]{1,2,0:T(8,128)(2,1)S(1)} async-done(((bf16[32,144,64]{1,2,0:T(8,128)(2,1)}), bf16[32,144,64]{1,2,0:T(8,128)(2,1)S(1)}, u32[]{:S(2)}, u32[]{:S(2)}) %all-to-all-start) | async-done | bytes 589856 | tf_op jit(solution)/shard_map/all_to_all | solution.py:27
  61.1 1.8 %reshape_reshape.6 = bf16[9,512,64]{1,0,2:T(8,128)(2,1)S(1)} reshape(bf16[32,144,64]{1,0,2:T(8,128)(2,1)S(1)} %copy.13) | data formatting | bytes 1179648 | tf_op jit(solution)/shard_map/reshape;reshape | solution.py:73
  66.9 1.6 %fusion = f32[9,512,64]{1,2,0:T(8,128)} fusion(bf16[9,512,64]{1,2,0:T(8,128)(2,1)S(1)} %get-tuple-element.6, bf16[1,9,64,512]{3,2,1,0:T(8,128)(2,1)S(1)} %fusion.64, f32[512,64]{0,1:T(8,128)S(1)} %multiply_multiply_fusion, bf16[512,512]{1,0:T(8,128)(2,1)S(1)} %bitcast_dynamic-update-slice_fusion.1), kind=kOutput, calls=%fused_computation.3 | convolution fusion | flops 302874624 | bytes 3014656 | tf_op jit(solution)/shard_map/nip,nkop->kio/dot_general | solution.py:92
  68.4 1.8 %copy.16 = f32[9,512,64]{2,1,0:T(8,128)S(1)} copy(f32[9,512,64]{1,2,0:T(8,128)} %fusion) | data formatting | bytes 2359296 | tf_op jit(solution)/shard_map/add | solution.py:93
  70.2 2.5 %reshape.444 = f32[96,1,3072]{2,1,0:T(1,128)} reshape(f32[96,48,64]{2,1,0:T(8,128)S(1)} %bitcast.162) | data formatting | bytes 2359296
  72.8 18.5 %all-to-all-start.1 = ((f32[96,1,3072]{2,1,0:T(1,128)}), f32[96,1,3072]{2,1,0:T(1,128)S(1)}, u32[]{:S(2)}, u32[]{:S(2)}) async-start(f32[96,1,3072]{2,1,0:T(1,128)} %reshape.444), calls=%async_computation.1 | async-start | bytes 2359296 | tf_op jit(solution)/shard_map/all_to_all | solution.py:35
  92.1 1.7 %collective-permute-start.13 = (f32[1,64,512]{2,1,0:T(8,128)S(1)}, f32[1,64,512]{2,1,0:T(8,128)S(1)}, u32[]{:S(2)}, u32[]{:S(2)}) collective-permute-start(f32[1,64,512]{2,1,0:T(8,128)S(1)} %get-tuple-element.18), channel_id=1, source_target_pairs={{0,21},{3,0},{6,3},{9,6},{12,9},{15,12},{18,15},{21,18},{1,22},{4,... | collective-permute-start | bytes 393224 | tf_op jit(solution)/shard_map/ppermute | solution.py:59
  93.8 1.9 %collective-permute-start.12 = (f32[1,64,512]{2,1,0:T(8,128)S(1)}, f32[1,64,512]{2,1,0:T(8,128)S(1)}, u32[]{:S(2)}, u32[]{:S(2)}) collective-permute-start(f32[1,64,512]{2,1,0:T(8,128)S(1)} %get-tuple-element.19), channel_id=1, source_target_pairs={{0,18},{3,21},{6,0},{9,3},{12,6},{15,9},{18,12},{21,15},{1,19},{4,... | collective-permute-start | bytes 393224 | tf_op jit(solution)/shard_map/ppermute | solution.py:59
  95.7 2.5 %collective-permute-start.11 = (f32[1,64,512]{2,1,0:T(8,128)S(1)}, f32[1,64,512]{2,1,0:T(8,128)S(1)}, u32[]{:S(2)}, u32[]{:S(2)}) collective-permute-start(f32[1,64,512]{2,1,0:T(8,128)S(1)} %get-tuple-element.20), channel_id=1, source_target_pairs={{0,15},{3,18},{6,21},{9,0},{12,3},{15,6},{18,9},{21,12},{1,16},{4,... | collective-permute-start | bytes 393224 | tf_op jit(solution)/shard_map/ppermute | solution.py:59
  98.2 4.6 %collective-permute-start.10 = (f32[1,64,512]{2,1,0:T(8,128)S(1)}, f32[1,64,512]{2,1,0:T(8,128)S(1)}, u32[]{:S(2)}, u32[]{:S(2)}) collective-permute-start(f32[1,64,512]{2,1,0:T(8,128)S(1)} %get-tuple-element.21), channel_id=1, source_target_pairs={{0,12},{3,15},{6,18},{9,21},{12,0},{15,3},{18,6},{21,9},{1,13},{4,... | collective-permute-start | bytes 393224 | tf_op jit(solution)/shard_map/ppermute | solution.py:59
  102.8 1.9 %collective-permute-start.9 = (f32[1,64,512]{2,1,0:T(8,128)S(1)}, f32[1,64,512]{2,1,0:T(8,128)S(1)}, u32[]{:S(2)}, u32[]{:S(2)}) collective-permute-start(f32[1,64,512]{2,1,0:T(8,128)S(1)} %get-tuple-element.22), channel_id=1, source_target_pairs={{0,9},{3,12},{6,15},{9,18},{12,21},{15,0},{18,3},{21,6},{1,10},{4,... | collective-permute-start | bytes 393224 | tf_op jit(solution)/shard_map/ppermute | solution.py:59
  104.7 4.4 %collective-permute-start.8 = (f32[1,64,512]{2,1,0:T(8,128)S(1)}, f32[1,64,512]{2,1,0:T(8,128)S(1)}, u32[]{:S(2)}, u32[]{:S(2)}) collective-permute-start(f32[1,64,512]{2,1,0:T(8,128)S(1)} %get-tuple-element.23), channel_id=1, source_target_pairs={{0,6},{3,9},{6,12},{9,15},{12,18},{15,21},{18,0},{21,3},{1,7},{4,1... | collective-permute-start | bytes 393224 | tf_op jit(solution)/shard_map/ppermute | solution.py:59
  110.6 2.7 %collective-permute-done.8 = f32[1,64,512]{2,1,0:T(8,128)S(1)} collective-permute-done((f32[1,64,512]{2,1,0:T(8,128)S(1)}, f32[1,64,512]{2,1,0:T(8,128)S(1)}, u32[]{:S(2)}, u32[]{:S(2)}) %collective-permute-start.8) | collective-permute-done | bytes 131104 | tf_op jit(solution)/shard_map/ppermute | solution.py:59
  114.0 24.4 %all-to-all-done.1 = f32[96,1,3072]{2,1,0:T(1,128)S(1)} async-done(((f32[96,1,3072]{2,1,0:T(1,128)}), f32[96,1,3072]{2,1,0:T(1,128)S(1)}, u32[]{:S(2)}, u32[]{:S(2)}) %all-to-all-start.1) | async-done | bytes 1179680 | tf_op jit(solution)/shard_map/all_to_all | solution.py:35
  138.9 3.4 %reduce.1 = f32[96,3072]{1,0:T(8,128)S(1)} reduce(f32[96,1,3072]{2,1,0:T(1,128)S(1)} %all-to-all-done.1, f32[]{:T(128)} %broadcast.516), dimensions={1}, to_apply=%all_to_all.7.reduce_sub_computation | reduce | bytes 2359300 | tf_op jit(solution)/shard_map/all_to_all | solution.py:35
  (67 shorter events, 12.3 us)
Async XLA Ops:
  1.4 1.0 copy-start.5
  2.3 35.3 %collective-permute-start.5 = (bf16[1,64,512]{2,1,0:T(8,128)(2,1)S(1)}, bf16[1,64,512]{2,1,0:T(8,128)(2,1)S(1)}, u32[]{:S(2)}, u32[]{:S(2)}) collective-permute-start(bf16[1,64,512]{2,1,0:T(8,128)(2,1)S(1)} %get-tuple-element.8), channel_id=1, source_target_pairs={{0,18},{3,21},{6,0},{9,3},{12,6},{15,9},{18,12},{21,15},{1,19},{4,... | collective-permute-start | bytes 196616 | tf_op jit(solution)/shard_map/ppermute | solution.py:45
  4.8 32.8 %collective-permute-start.4 = (bf16[1,64,512]{2,1,0:T(8,128)(2,1)S(1)}, bf16[1,64,512]{2,1,0:T(8,128)(2,1)S(1)}, u32[]{:S(2)}, u32[]{:S(2)}) collective-permute-start(bf16[1,64,512]{2,1,0:T(8,128)(2,1)S(1)} %get-tuple-element.8), channel_id=1, source_target_pairs={{0,15},{3,18},{6,21},{9,0},{12,3},{15,6},{18,9},{21,12},{1,16},{4,... | collective-permute-start | bytes 196616 | tf_op jit(solution)/shard_map/ppermute | solution.py:45
  8.3 29.3 %collective-permute-start.3 = (bf16[1,64,512]{2,1,0:T(8,128)(2,1)S(1)}, bf16[1,64,512]{2,1,0:T(8,128)(2,1)S(1)}, u32[]{:S(2)}, u32[]{:S(2)}) collective-permute-start(bf16[1,64,512]{2,1,0:T(8,128)(2,1)S(1)} %get-tuple-element.8), channel_id=1, source_target_pairs={{0,12},{3,15},{6,18},{9,21},{12,0},{15,3},{18,6},{21,9},{1,13},{4,... | collective-permute-start | bytes 196616 | tf_op jit(solution)/shard_map/ppermute | solution.py:45
  11.3 26.2 %collective-permute-start.2 = (bf16[1,64,512]{2,1,0:T(8,128)(2,1)S(1)}, bf16[1,64,512]{2,1,0:T(8,128)(2,1)S(1)}, u32[]{:S(2)}, u32[]{:S(2)}) collective-permute-start(bf16[1,64,512]{2,1,0:T(8,128)(2,1)S(1)} %get-tuple-element.8), channel_id=1, source_target_pairs={{0,9},{3,12},{6,15},{9,18},{12,21},{15,0},{18,3},{21,6},{1,10},{4,... | collective-permute-start | bytes 196616 | tf_op jit(solution)/shard_map/ppermute | solution.py:45
  15.0 15.5 %collective-permute-start = (bf16[1,64,512]{2,1,0:T(8,128)(2,1)S(1)}, bf16[1,64,512]{2,1,0:T(8,128)(2,1)S(1)}, u32[]{:S(2)}, u32[]{:S(2)}) collective-permute-start(bf16[1,64,512]{2,1,0:T(8,128)(2,1)S(1)} %get-tuple-element.8), channel_id=1, source_target_pairs={{0,3},{3,6},{6,9},{9,12},{12,15},{15,18},{18,21},{21,0},{1,4},{4,7... | collective-permute-start | bytes 196616 | tf_op jit(solution)/shard_map/ppermute | solution.py:45
  17.6 12.8 %copy-start.2 = (f32[1,512]{1,0:T(1,128)S(1)}, f32[1,512]{1,0:T(1,128)}, u32[]{:S(2)}) copy-start(f32[1,512]{1,0:T(1,128)} %param.7) | copy-start | bytes 6148
  17.7 42.8 %all-to-all-start = ((bf16[32,144,64]{1,2,0:T(8,128)(2,1)}), bf16[32,144,64]{1,2,0:T(8,128)(2,1)S(1)}, u32[]{:S(2)}, u32[]{:S(2)}) async-start(bf16[32,144,64]{1,2,0:T(8,128)(2,1)} %broadcast_in_dim.2), calls=%async_computation | async-start | bytes 2097152 | tf_op jit(solution)/shard_map/all_to_all | solution.py:27
  30.5 6.5 %collective-permute-start.1 = (bf16[1,64,512]{2,1,0:T(8,128)(2,1)S(1)}, bf16[1,64,512]{2,1,0:T(8,128)(2,1)S(1)}, u32[]{:S(2)}, u32[]{:S(2)}) collective-permute-start(bf16[1,64,512]{2,1,0:T(8,128)(2,1)S(1)} %get-tuple-element.8), channel_id=1, source_target_pairs={{0,6},{3,9},{6,12},{9,15},{12,18},{15,21},{18,0},{21,3},{1,7},{4,1... | collective-permute-start | bytes 196616 | tf_op jit(solution)/shard_map/ppermute | solution.py:45
  37.1 2.4 %collective-permute-start.6 = (bf16[1,64,512]{2,1,0:T(8,128)(2,1)S(1)}, bf16[1,64,512]{2,1,0:T(8,128)(2,1)S(1)}, u32[]{:S(2)}, u32[]{:S(2)}) collective-permute-start(bf16[1,64,512]{2,1,0:T(8,128)(2,1)S(1)} %get-tuple-element.8), channel_id=1, source_target_pairs={{0,21},{3,0},{6,3},{9,6},{12,9},{15,12},{18,15},{21,18},{1,22},{4,... | collective-permute-start | bytes 196616 | tf_op jit(solution)/shard_map/ppermute | solution.py:45
  63.5 2.5 %copy-start.3 = (f32[64]{0:T(128)}, f32[64]{0:T(128)S(1)}, u32[]{:S(2)}) copy-start(f32[64]{0:T(128)S(1)} %fusion.3) | copy-start | bytes 772
  64.0 0.8 copy-start.1
  72.8 65.7 %all-to-all-start.1 = ((f32[96,1,3072]{2,1,0:T(1,128)}), f32[96,1,3072]{2,1,0:T(1,128)S(1)}, u32[]{:S(2)}, u32[]{:S(2)}) async-start(f32[96,1,3072]{2,1,0:T(1,128)} %reshape.444), calls=%async_computation.1 | async-start | bytes 2359296 | tf_op jit(solution)/shard_map/all_to_all | solution.py:35
  91.9 17.2 %copy-start = (f32[1,64,512]{2,1,0:T(8,128)S(1)}, f32[1,64,512]{2,1,0:T(8,128)}, u32[]{:S(2)}) copy-start(f32[1,64,512]{2,1,0:T(8,128)} %get-tuple-element.4) | copy-start | bytes 393220
  91.9 17.2 %copy-start.4 = (f32[64]{0:T(128)S(1)}, f32[64]{0:T(128)}, u32[]{:S(2)}) copy-start(f32[64]{0:T(128)} %copy-done.3) | copy-start | bytes 772
  91.9 17.2 %copy-start.7 = (f32[64]{0:T(128)S(1)}, f32[64]{0:T(128)}, u32[]{:S(2)}) copy-start(f32[64]{0:T(128)} %param.8) | copy-start | bytes 772
  91.9 21.4 %copy-start.6 = (f32[64]{0:T(128)S(1)}, f32[64]{0:T(128)}, u32[]{:S(2)}) copy-start(f32[64]{0:T(128)} %copy-done.5) | copy-start | bytes 772
  92.0 10.8 %collective-permute-start.7 = (f32[1,64,512]{2,1,0:T(8,128)S(1)}, f32[1,64,512]{2,1,0:T(8,128)S(1)}, u32[]{:S(2)}, u32[]{:S(2)}) collective-permute-start(f32[1,64,512]{2,1,0:T(8,128)S(1)} %get-tuple-element.17), channel_id=1, source_target_pairs={{0,3},{3,6},{6,9},{9,12},{12,15},{15,18},{18,21},{21,0},{1,4},{4,7... | collective-permute-start | bytes 393224 | tf_op jit(solution)/shard_map/ppermute | solution.py:59
  92.1 12.7 %collective-permute-start.13 = (f32[1,64,512]{2,1,0:T(8,128)S(1)}, f32[1,64,512]{2,1,0:T(8,128)S(1)}, u32[]{:S(2)}, u32[]{:S(2)}) collective-permute-start(f32[1,64,512]{2,1,0:T(8,128)S(1)} %get-tuple-element.18), channel_id=1, source_target_pairs={{0,21},{3,0},{6,3},{9,6},{12,9},{15,12},{18,15},{21,18},{1,22},{4,... | collective-permute-start | bytes 393224 | tf_op jit(solution)/shard_map/ppermute | solution.py:59
  93.8 16.1 %collective-permute-start.12 = (f32[1,64,512]{2,1,0:T(8,128)S(1)}, f32[1,64,512]{2,1,0:T(8,128)S(1)}, u32[]{:S(2)}, u32[]{:S(2)}) collective-permute-start(f32[1,64,512]{2,1,0:T(8,128)S(1)} %get-tuple-element.19), channel_id=1, source_target_pairs={{0,18},{3,21},{6,0},{9,3},{12,6},{15,9},{18,12},{21,15},{1,19},{4,... | collective-permute-start | bytes 393224 | tf_op jit(solution)/shard_map/ppermute | solution.py:59
  95.7 14.2 %collective-permute-start.11 = (f32[1,64,512]{2,1,0:T(8,128)S(1)}, f32[1,64,512]{2,1,0:T(8,128)S(1)}, u32[]{:S(2)}, u32[]{:S(2)}) collective-permute-start(f32[1,64,512]{2,1,0:T(8,128)S(1)} %get-tuple-element.20), channel_id=1, source_target_pairs={{0,15},{3,18},{6,21},{9,0},{12,3},{15,6},{18,9},{21,12},{1,16},{4,... | collective-permute-start | bytes 393224 | tf_op jit(solution)/shard_map/ppermute | solution.py:59
  98.2 11.7 %collective-permute-start.10 = (f32[1,64,512]{2,1,0:T(8,128)S(1)}, f32[1,64,512]{2,1,0:T(8,128)S(1)}, u32[]{:S(2)}, u32[]{:S(2)}) collective-permute-start(f32[1,64,512]{2,1,0:T(8,128)S(1)} %get-tuple-element.21), channel_id=1, source_target_pairs={{0,12},{3,15},{6,18},{9,21},{12,0},{15,3},{18,6},{21,9},{1,13},{4,... | collective-permute-start | bytes 393224 | tf_op jit(solution)/shard_map/ppermute | solution.py:59
  102.8 7.8 %collective-permute-start.9 = (f32[1,64,512]{2,1,0:T(8,128)S(1)}, f32[1,64,512]{2,1,0:T(8,128)S(1)}, u32[]{:S(2)}, u32[]{:S(2)}) collective-permute-start(f32[1,64,512]{2,1,0:T(8,128)S(1)} %get-tuple-element.22), channel_id=1, source_target_pairs={{0,9},{3,12},{6,15},{9,18},{12,21},{15,0},{18,3},{21,6},{1,10},{4,... | collective-permute-start | bytes 393224 | tf_op jit(solution)/shard_map/ppermute | solution.py:59
  104.7 8.6 %collective-permute-start.8 = (f32[1,64,512]{2,1,0:T(8,128)S(1)}, f32[1,64,512]{2,1,0:T(8,128)S(1)}, u32[]{:S(2)}, u32[]{:S(2)}) collective-permute-start(f32[1,64,512]{2,1,0:T(8,128)S(1)} %get-tuple-element.23), channel_id=1, source_target_pairs={{0,6},{3,9},{6,12},{9,15},{12,18},{15,21},{18,0},{21,3},{1,7},{4,1... | collective-permute-start | bytes 393224 | tf_op jit(solution)/shard_map/ppermute | solution.py:59

commit v6 on v5

--- a/solution.py
+++ b/solution.py
@@ -1,7 +1,7 @@
 import jax
 import jax.numpy as jnp
 from jax import lax
-from jax.sharding import PartitionSpec as P
+from jax.sharding import Mesh, PartitionSpec as P
 
 
 WIDTH = 64
@@ -9,6 +9,7 @@
 
 OFFSETS = [(-1, -1), (-1, 0), (-1, 1), (0, -1), (0, 0), (0, 1), (1, -1), (1, 0), (1, 1)]
 EPSILON = 1e-08
+ROWS_AXES = ("z_lo", "y", "dom")
 
 
 def moved(array, row_step, col_step):
@@ -31,8 +32,10 @@
     count = 1
     for axis in (axes if isinstance(axes, tuple) else (axes,)):
         count *= lax.axis_size(axis)
-    blocks = terms.reshape((count, terms.shape[0] // count) + terms.shape[1:])
-    return jnp.sum(lax.all_to_all(blocks, axes, 0, 0, tiled=True), axis=0)
+    rows = terms.shape[0] // count
+    flat = terms.reshape(count, rows * terms.shape[1])
+    received = lax.all_to_all(flat, axes, 0, 0, tiled=True)
+    return jnp.sum(received, axis=0).reshape(rows, terms.shape[1])
 
 
 def gather_by_permutes(block, axis, count):
@@ -68,8 +71,8 @@
     own_style = lax.dynamic_slice_in_dim(style, sect_place * local_ch, local_ch, 1)
     local_mod = (features.astype(jnp.float32) * own_style[:, :, None]).astype(jnp.bfloat16)
     modulated = gather_by_permutes(local_mod, "sect", sect_count)
-    sample_count = lax.axis_size("sample")
-    full_weight = gather_by_exchange(weight, "sample", sample_count).reshape(-1, local_ch)
+    along_y = gather_by_exchange(weight, "y", lax.axis_size("y"))
+    full_weight = gather_by_exchange(along_y, "z_lo", lax.axis_size("z_lo")).reshape(-1, local_ch)
     kernel = full_weight.reshape(9, channels, local_ch)
     kernel_f = kernel.astype(jnp.float32)
     products = jnp.einsum("kio,nip->nkop", kernel, modulated, preferred_element_type=jnp.float32)
@@ -91,7 +94,7 @@
     )
     grad_main = jnp.einsum("nip,nkop->kio", modulated, back_shifts, preferred_element_type=jnp.float32)
     grad_terms = (grad_main + 2.0 * kernel_f * coupling[None]).reshape(-1, local_ch)
-    grad_weight = sum_by_exchange(grad_terms, ("sample", "dom"))
+    grad_weight = sum_by_exchange(grad_terms, ROWS_AXES)
     back = jnp.einsum("kio,nkop->nip", kernel, back_shifts, preferred_element_type=jnp.float32)
     summed = sum_by_permutes(back, "sect", sect_count)
     grad_features = (summed * own_style[:, :, None]).astype(jnp.bfloat16)
@@ -99,16 +102,21 @@
 
 
 def solution(mesh):
+    z_lo = 4
+    fine = Mesh(
+        mesh.devices.reshape((z_lo, mesh.shape["sample"] // z_lo) + mesh.devices.shape[1:]),
+        ("z_lo", "y", "sect", "dom"),
+    )
     in_specs = (
-        P(("sample", "dom"), "sect", None),
-        P("sample", "sect"),
-        P(("sample", "dom"), None),
+        P(ROWS_AXES, "sect", None),
+        P(("z_lo", "y"), "sect"),
+        P(ROWS_AXES, None),
         P("sect"),
-        P(("sample", "dom"), "sect", None),
+        P(ROWS_AXES, "sect", None),
     )
     out_specs = (
-        P(("sample", "dom"), "sect", None),
-        P(("sample", "dom"), "sect"),
-        P(("sample", "dom"), "sect", None),
+        P(ROWS_AXES, "sect", None),
+        P(ROWS_AXES, "sect"),
+        P(ROWS_AXES, "sect", None),
     )
-    return jax.shard_map(layer, mesh=mesh, in_specs=in_specs, out_specs=out_specs, check_vma=False)
+    return jax.shard_map(layer, mesh=fine, in_specs=in_specs, out_specs=out_specs, check_vma=False)

time: 145 us -> 145 us (level)
  waiting for transfers between devices: 53.4 us -> 59.1 us
  other arithmetic: 8.95 us -> 5.38 us
  starting transfers between devices: 65.8 us -> 63.6 us
    all_to_all x1 -> x2, waiting for transfers between devices: 21.1 us -> 30.4 us  [gather_by_exchange(): return lax.all_to_all(copies, axis, 0, 0, tiled=True)]
    all_to_all x1 -> x0, other arithmetic: 3.44 us -> none  [sum_by_exchange(): return jnp.sum(lax.all_to_all(blocks, axes, 0, 0, tiled=True), axis=0)]
    unnamed x18 -> x16, local copies, waits for them, and re-layouts: 3.94 us -> 0.8 us
    ppermute x7, waiting for transfers between devices: 4.56 us -> 1.78 us  [gather_by_permutes(): arrived = lax.ppermute(block, axis, pairs)]
    ppermute x7, starting transfers between devices: 17.6 us -> 15.3 us  [gather_by_permutes(): arrived = lax.ppermute(block, axis, pairs)]
    all_to_all x1, starting transfers between devices: 18.5 us -> 16.3 us  [sum_by_exchange(): received = lax.all_to_all(flat, axes, 0, 0, tiled=True)]
    all_to_all x1 -> x2, starting transfers between devices: 12.7 us -> 14.9 us  [gather_by_exchange(): return lax.all_to_all(copies, axis, 0, 0, tiled=True)]
    all_to_all x1, local copies, waits for them, and re-layouts: 0.51 us -> 2.5 us  [sum_by_exchange(): received = lax.all_to_all(flat, axes, 0, 0, tiled=True)]
  transfers between devices with their start and end apart: 16 -> 17, of which waited for: 6 -> 6; matrix products, arithmetic and copies ran while one was open for 3% -> 3% of each run, Pallas kernels for 0% -> 0%
where the time goes in v6:
time: 145 us; the launch traced here: 144 us
  starting transfers between devices  63.6 us (44%)
  waiting for transfers between devices  59.1 us (41%)
  local copies, waits for them, and re-layouts  11.5 us (8%)
  other arithmetic  5.38 us (4%)
  matrix products  2.83 us (2%)
    all_to_all x2, waiting for transfers between devices, gather_by_exchange(): return lax.all_to_all(copies, axis, 0, 0, tiled=True)  30.4 us
    all_to_all x1, waiting for transfers between devices, sum_by_exchange(): received = lax.all_to_all(flat, axes, 0, 0, tiled=True)  23.7 us
    ppermute x7, starting transfers between devices, sum_by_permutes(): total = total + lax.ppermute(part, axis, pairs)  17.2 us
    all_to_all x1, starting transfers between devices, sum_by_exchange(): received = lax.all_to_all(flat, axes, 0, 0, tiled=True)  16.3 us
    ppermute x7, starting transfers between devices, gather_by_permutes(): arrived = lax.ppermute(block, axis, pairs)  15.3 us
    all_to_all x2, starting transfers between devices, gather_by_exchange(): return lax.all_to_all(copies, axis, 0, 0, tiled=True)  14.9 us
    ppermute x7, waiting for transfers between devices, sum_by_permutes(): total = total + lax.ppermute(part, axis, pairs)  3.17 us
  transfers between devices with their start and end apart: 17, of which 6 were waited for; matrix products, arithmetic and copies ran while one was open for 3% of the time, Pallas kernels for 0%

profile of v6, /device:TPU:50, one launch (start us, length us, event | category | flops | bytes accessed | tf_op | source)
XLA Modules:
  0.0 143.7 jit_solution(4010391272840425320)
XLA Ops:
  2.4 2.4 %collective-permute-start.5 = (bf16[1,64,512]{2,1,0:T(8,128)(2,1)S(1)}, bf16[1,64,512]{2,1,0:T(8,128)(2,1)S(1)}, u32[]{:S(2)}, u32[]{:S(2)}) collective-permute-start(bf16[1,64,512]{2,1,0:T(8,128)(2,1)S(1)} %get-tuple-element.8), channel_id=1, source_target_pairs={{0,18},{3,21},{6,0},{9,3},{12,6},{15,9},{18,12},{21,15},{1,19},{4,... | collective-permute-start | bytes 196616 | tf_op jit(solution)/shard_map/ppermute | solution.py:48
  4.9 3.5 %collective-permute-start.4 = (bf16[1,64,512]{2,1,0:T(8,128)(2,1)S(1)}, bf16[1,64,512]{2,1,0:T(8,128)(2,1)S(1)}, u32[]{:S(2)}, u32[]{:S(2)}) collective-permute-start(bf16[1,64,512]{2,1,0:T(8,128)(2,1)S(1)} %get-tuple-element.8), channel_id=1, source_target_pairs={{0,15},{3,18},{6,21},{9,0},{12,3},{15,6},{18,9},{21,12},{1,16},{4,... | collective-permute-start | bytes 196616 | tf_op jit(solution)/shard_map/ppermute | solution.py:48
  8.4 3.0 %collective-permute-start.3 = (bf16[1,64,512]{2,1,0:T(8,128)(2,1)S(1)}, bf16[1,64,512]{2,1,0:T(8,128)(2,1)S(1)}, u32[]{:S(2)}, u32[]{:S(2)}) collective-permute-start(bf16[1,64,512]{2,1,0:T(8,128)(2,1)S(1)} %get-tuple-element.8), channel_id=1, source_target_pairs={{0,12},{3,15},{6,18},{9,21},{12,0},{15,3},{18,6},{21,9},{1,13},{4,... | collective-permute-start | bytes 196616 | tf_op jit(solution)/shard_map/ppermute | solution.py:48
  11.4 3.7 %collective-permute-start.2 = (bf16[1,64,512]{2,1,0:T(8,128)(2,1)S(1)}, bf16[1,64,512]{2,1,0:T(8,128)(2,1)S(1)}, u32[]{:S(2)}, u32[]{:S(2)}) collective-permute-start(bf16[1,64,512]{2,1,0:T(8,128)(2,1)S(1)} %get-tuple-element.8), channel_id=1, source_target_pairs={{0,9},{3,12},{6,15},{9,18},{12,21},{15,0},{18,3},{21,6},{1,10},{4,... | collective-permute-start | bytes 196616 | tf_op jit(solution)/shard_map/ppermute | solution.py:48
  15.8 1.5 %broadcast_in_dim.4 = bf16[8,144,64]{1,2,0:T(8,128)(2,1)} broadcast(bf16[144,64]{0,1:T(8,128)(2,1)} %param.6), dimensions={1,2} | broadcast | bytes 165888 | tf_op jit(solution)/shard_map/broadcast_in_dim | solution.py:27
  17.3 10.6 %all-to-all-start = ((bf16[8,144,64]{1,2,0:T(8,128)(2,1)}), bf16[8,144,64]{1,2,0:T(8,128)(2,1)S(1)}, u32[]{:S(2)}, u32[]{:S(2)}) async-start(bf16[8,144,64]{1,2,0:T(8,128)(2,1)} %broadcast_in_dim.4), calls=%async_computation | async-start | bytes 524288 | tf_op jit(solution)/shard_map/all_to_all | solution.py:28
  28.1 1.9 %collective-permute-start.1 = (bf16[1,64,512]{2,1,0:T(8,128)(2,1)S(1)}, bf16[1,64,512]{2,1,0:T(8,128)(2,1)S(1)}, u32[]{:S(2)}, u32[]{:S(2)}) collective-permute-start(bf16[1,64,512]{2,1,0:T(8,128)(2,1)S(1)} %get-tuple-element.8), channel_id=1, source_target_pairs={{0,6},{3,9},{6,12},{9,15},{12,18},{15,21},{18,0},{21,3},{1,7},{4,1... | collective-permute-start | bytes 196616 | tf_op jit(solution)/shard_map/ppermute | solution.py:48
  30.1 6.4 %all-to-all-done = bf16[8,144,64]{1,2,0:T(8,128)(2,1)S(1)} async-done(((bf16[8,144,64]{1,2,0:T(8,128)(2,1)}), bf16[8,144,64]{1,2,0:T(8,128)(2,1)S(1)}, u32[]{:S(2)}, u32[]{:S(2)}) %all-to-all-start) | async-done | bytes 147488 | tf_op jit(solution)/shard_map/all_to_all | solution.py:28
  37.7 4.2 %all-to-all-start.1 = ((bf16[4,8,144,64]{2,1,3,0:T(8,128)(2,1)}), bf16[4,8,144,64]{2,1,3,0:T(8,128)(2,1)S(1)}, u32[]{:S(2)}, u32[]{:S(2)}) async-start(bf16[4,8,144,64]{2,1,3,0:T(8,128)(2,1)} %broadcast_in_dim.5), calls=%async_computation.1 | async-start | bytes 2097152 | tf_op jit(solution)/shard_map/all_to_all | solution.py:28
  42.1 1.8 %collective-permute-done.6 = bf16[1,64,512]{2,1,0:T(8,128)(2,1)S(1)} collective-permute-done((bf16[1,64,512]{2,1,0:T(8,128)(2,1)S(1)}, bf16[1,64,512]{2,1,0:T(8,128)(2,1)S(1)}, u32[]{:S(2)}, u32[]{:S(2)}) %collective-permute-start.6) | collective-permute-done | bytes 65568 | tf_op jit(solution)/shard_map/ppermute | solution.py:48
  43.9 24.1 %all-to-all-done.1 = bf16[4,8,144,64]{2,1,3,0:T(8,128)(2,1)S(1)} async-done(((bf16[4,8,144,64]{2,1,3,0:T(8,128)(2,1)}), bf16[4,8,144,64]{2,1,3,0:T(8,128)(2,1)S(1)}, u32[]{:S(2)}, u32[]{:S(2)}) %all-to-all-start.1) | async-done | bytes 589856 | tf_op jit(solution)/shard_map/all_to_all | solution.py:28
  68.1 1.8 %reshape_reshape.4 = bf16[9,512,64]{1,0,2:T(8,128)(2,1)S(1)} reshape(bf16[4,8,144,64]{2,1,0,3:T(8,128)(2,1)S(1)} %copy.14) | data formatting | bytes 1179648 | tf_op jit(solution)/shard_map/reshape;reshape | solution.py:76
  73.9 1.5 %fusion = f32[9,512,64]{1,2,0:T(8,128)} fusion(bf16[9,512,64]{1,2,0:T(8,128)(2,1)S(1)} %get-tuple-element.6, bf16[1,9,64,512]{3,2,1,0:T(8,128)(2,1)S(1)} %fusion.64, f32[512,64]{0,1:T(8,128)S(1)} %multiply_multiply_fusion, bf16[512,512]{1,0:T(8,128)(2,1)S(1)} %bitcast_dynamic-update-slice_fusion.1), kind=kOutput, calls=%fused_computation.3 | convolution fusion | flops 302874624 | bytes 3014656 | tf_op jit(solution)/shard_map/nip,nkop->kio/dot_general | solution.py:95
  75.4 1.8 %copy.17 = f32[9,512,64]{2,1,0:T(8,128)S(1)} copy(f32[9,512,64]{1,2,0:T(8,128)} %fusion) | data formatting | bytes 2359296 | tf_op jit(solution)/shard_map/add | solution.py:96
  77.2 2.5 %all_to_all.16 = f32[96,1,3072]{2,1,0:T(1,128)} reshape(f32[9,512,64]{2,1,0:T(8,128)S(1)} %copy.17) | data formatting | bytes 2359296 | tf_op jit(solution)/shard_map/all_to_all | solution.py:37
  79.7 16.3 %all-to-all-start.2 = ((f32[96,1,3072]{2,1,0:T(1,128)}), f32[96,1,3072]{2,1,0:T(1,128)S(1)}, u32[]{:S(2)}, u32[]{:S(2)}) async-start(f32[96,1,3072]{2,1,0:T(1,128)} %all_to_all.16), calls=%async_computation.2 | async-start | bytes 2359296 | tf_op jit(solution)/shard_map/all_to_all | solution.py:37
  96.8 1.7 %collective-permute-start.13 = (f32[1,64,512]{2,1,0:T(8,128)S(1)}, f32[1,64,512]{2,1,0:T(8,128)S(1)}, u32[]{:S(2)}, u32[]{:S(2)}) collective-permute-start(f32[1,64,512]{2,1,0:T(8,128)S(1)} %get-tuple-element.18), channel_id=1, source_target_pairs={{0,21},{3,0},{6,3},{9,6},{12,9},{15,12},{18,15},{21,18},{1,22},{4,... | collective-permute-start | bytes 393224 | tf_op jit(solution)/shard_map/ppermute | solution.py:62
  98.5 2.6 %collective-permute-start.12 = (f32[1,64,512]{2,1,0:T(8,128)S(1)}, f32[1,64,512]{2,1,0:T(8,128)S(1)}, u32[]{:S(2)}, u32[]{:S(2)}) collective-permute-start(f32[1,64,512]{2,1,0:T(8,128)S(1)} %get-tuple-element.19), channel_id=1, source_target_pairs={{0,18},{3,21},{6,0},{9,3},{12,6},{15,9},{18,12},{21,15},{1,19},{4,... | collective-permute-start | bytes 393224 | tf_op jit(solution)/shard_map/ppermute | solution.py:62
  101.1 2.1 %collective-permute-start.11 = (f32[1,64,512]{2,1,0:T(8,128)S(1)}, f32[1,64,512]{2,1,0:T(8,128)S(1)}, u32[]{:S(2)}, u32[]{:S(2)}) collective-permute-start(f32[1,64,512]{2,1,0:T(8,128)S(1)} %get-tuple-element.20), channel_id=1, source_target_pairs={{0,15},{3,18},{6,21},{9,0},{12,3},{15,6},{18,9},{21,12},{1,16},{4,... | collective-permute-start | bytes 393224 | tf_op jit(solution)/shard_map/ppermute | solution.py:62
  103.3 4.3 %collective-permute-start.10 = (f32[1,64,512]{2,1,0:T(8,128)S(1)}, f32[1,64,512]{2,1,0:T(8,128)S(1)}, u32[]{:S(2)}, u32[]{:S(2)}) collective-permute-start(f32[1,64,512]{2,1,0:T(8,128)S(1)} %get-tuple-element.21), channel_id=1, source_target_pairs={{0,12},{3,15},{6,18},{9,21},{12,0},{15,3},{18,6},{21,9},{1,13},{4,... | collective-permute-start | bytes 393224 | tf_op jit(solution)/shard_map/ppermute | solution.py:62
  107.5 2.0 %collective-permute-start.9 = (f32[1,64,512]{2,1,0:T(8,128)S(1)}, f32[1,64,512]{2,1,0:T(8,128)S(1)}, u32[]{:S(2)}, u32[]{:S(2)}) collective-permute-start(f32[1,64,512]{2,1,0:T(8,128)S(1)} %get-tuple-element.22), channel_id=1, source_target_pairs={{0,9},{3,12},{6,15},{9,18},{12,21},{15,0},{18,3},{21,6},{1,10},{4,... | collective-permute-start | bytes 393224 | tf_op jit(solution)/shard_map/ppermute | solution.py:62
  109.6 4.4 %collective-permute-start.8 = (f32[1,64,512]{2,1,0:T(8,128)S(1)}, f32[1,64,512]{2,1,0:T(8,128)S(1)}, u32[]{:S(2)}, u32[]{:S(2)}) collective-permute-start(f32[1,64,512]{2,1,0:T(8,128)S(1)} %get-tuple-element.23), channel_id=1, source_target_pairs={{0,6},{3,9},{6,12},{9,15},{12,18},{15,21},{18,0},{21,3},{1,7},{4,1... | collective-permute-start | bytes 393224 | tf_op jit(solution)/shard_map/ppermute | solution.py:62
  115.3 2.6 %collective-permute-done.8 = f32[1,64,512]{2,1,0:T(8,128)S(1)} collective-permute-done((f32[1,64,512]{2,1,0:T(8,128)S(1)}, f32[1,64,512]{2,1,0:T(8,128)S(1)}, u32[]{:S(2)}, u32[]{:S(2)}) %collective-permute-start.8) | collective-permute-done | bytes 131104 | tf_op jit(solution)/shard_map/ppermute | solution.py:62
  118.6 23.7 %all-to-all-done.2 = f32[96,1,3072]{2,1,0:T(1,128)S(1)} async-done(((f32[96,1,3072]{2,1,0:T(1,128)}), f32[96,1,3072]{2,1,0:T(1,128)S(1)}, u32[]{:S(2)}, u32[]{:S(2)}) %all-to-all-start.2) | async-done | bytes 1179680 | tf_op jit(solution)/shard_map/all_to_all | solution.py:37
  (69 shorter events, 11.9 us)
Async XLA Ops:
  0.6 27.4 %copy-start.2 = (f32[1,512]{1,0:T(1,128)S(1)}, f32[1,512]{1,0:T(1,128)}, u32[]{:S(2)}) copy-start(f32[1,512]{1,0:T(1,128)} %param.7) | copy-start | bytes 6148
  1.4 1.0 copy-start.5
  2.4 39.7 %collective-permute-start.5 = (bf16[1,64,512]{2,1,0:T(8,128)(2,1)S(1)}, bf16[1,64,512]{2,1,0:T(8,128)(2,1)S(1)}, u32[]{:S(2)}, u32[]{:S(2)}) collective-permute-start(bf16[1,64,512]{2,1,0:T(8,128)(2,1)S(1)} %get-tuple-element.8), channel_id=1, source_target_pairs={{0,18},{3,21},{6,0},{9,3},{12,6},{15,9},{18,12},{21,15},{1,19},{4,... | collective-permute-start | bytes 196616 | tf_op jit(solution)/shard_map/ppermute | solution.py:48
  4.9 37.2 %collective-permute-start.4 = (bf16[1,64,512]{2,1,0:T(8,128)(2,1)S(1)}, bf16[1,64,512]{2,1,0:T(8,128)(2,1)S(1)}, u32[]{:S(2)}, u32[]{:S(2)}) collective-permute-start(bf16[1,64,512]{2,1,0:T(8,128)(2,1)S(1)} %get-tuple-element.8), channel_id=1, source_target_pairs={{0,15},{3,18},{6,21},{9,0},{12,3},{15,6},{18,9},{21,12},{1,16},{4,... | collective-permute-start | bytes 196616 | tf_op jit(solution)/shard_map/ppermute | solution.py:48
  8.4 33.7 %collective-permute-start.3 = (bf16[1,64,512]{2,1,0:T(8,128)(2,1)S(1)}, bf16[1,64,512]{2,1,0:T(8,128)(2,1)S(1)}, u32[]{:S(2)}, u32[]{:S(2)}) collective-permute-start(bf16[1,64,512]{2,1,0:T(8,128)(2,1)S(1)} %get-tuple-element.8), channel_id=1, source_target_pairs={{0,12},{3,15},{6,18},{9,21},{12,0},{15,3},{18,6},{21,9},{1,13},{4,... | collective-permute-start | bytes 196616 | tf_op jit(solution)/shard_map/ppermute | solution.py:48
  11.4 30.6 %collective-permute-start.2 = (bf16[1,64,512]{2,1,0:T(8,128)(2,1)S(1)}, bf16[1,64,512]{2,1,0:T(8,128)(2,1)S(1)}, u32[]{:S(2)}, u32[]{:S(2)}) collective-permute-start(bf16[1,64,512]{2,1,0:T(8,128)(2,1)S(1)} %get-tuple-element.8), channel_id=1, source_target_pairs={{0,9},{3,12},{6,15},{9,18},{12,21},{15,0},{18,3},{21,6},{1,10},{4,... | collective-permute-start | bytes 196616 | tf_op jit(solution)/shard_map/ppermute | solution.py:48
  15.1 13.0 %collective-permute-start = (bf16[1,64,512]{2,1,0:T(8,128)(2,1)S(1)}, bf16[1,64,512]{2,1,0:T(8,128)(2,1)S(1)}, u32[]{:S(2)}, u32[]{:S(2)}) collective-permute-start(bf16[1,64,512]{2,1,0:T(8,128)(2,1)S(1)} %get-tuple-element.8), channel_id=1, source_target_pairs={{0,3},{3,6},{6,9},{9,12},{12,15},{15,18},{18,21},{21,0},{1,4},{4,7... | collective-permute-start | bytes 196616 | tf_op jit(solution)/shard_map/ppermute | solution.py:48
  17.3 19.2 %all-to-all-start = ((bf16[8,144,64]{1,2,0:T(8,128)(2,1)}), bf16[8,144,64]{1,2,0:T(8,128)(2,1)S(1)}, u32[]{:S(2)}, u32[]{:S(2)}) async-start(bf16[8,144,64]{1,2,0:T(8,128)(2,1)} %broadcast_in_dim.4), calls=%async_computation | async-start | bytes 524288 | tf_op jit(solution)/shard_map/all_to_all | solution.py:28
  28.1 13.8 %collective-permute-start.1 = (bf16[1,64,512]{2,1,0:T(8,128)(2,1)S(1)}, bf16[1,64,512]{2,1,0:T(8,128)(2,1)S(1)}, u32[]{:S(2)}, u32[]{:S(2)}) collective-permute-start(bf16[1,64,512]{2,1,0:T(8,128)(2,1)S(1)} %get-tuple-element.8), channel_id=1, source_target_pairs={{0,6},{3,9},{6,12},{9,15},{12,18},{15,21},{18,0},{21,3},{1,7},{4,1... | collective-permute-start | bytes 196616 | tf_op jit(solution)/shard_map/ppermute | solution.py:48
  37.7 30.2 %all-to-all-start.1 = ((bf16[4,8,144,64]{2,1,3,0:T(8,128)(2,1)}), bf16[4,8,144,64]{2,1,3,0:T(8,128)(2,1)S(1)}, u32[]{:S(2)}, u32[]{:S(2)}) async-start(bf16[4,8,144,64]{2,1,3,0:T(8,128)(2,1)} %broadcast_in_dim.5), calls=%async_computation.1 | async-start | bytes 2097152 | tf_op jit(solution)/shard_map/all_to_all | solution.py:28
  42.0 1.9 %collective-permute-start.6 = (bf16[1,64,512]{2,1,0:T(8,128)(2,1)S(1)}, bf16[1,64,512]{2,1,0:T(8,128)(2,1)S(1)}, u32[]{:S(2)}, u32[]{:S(2)}) collective-permute-start(bf16[1,64,512]{2,1,0:T(8,128)(2,1)S(1)} %get-tuple-element.8), channel_id=1, source_target_pairs={{0,21},{3,0},{6,3},{9,6},{12,9},{15,12},{18,15},{21,18},{1,22},{4,... | collective-permute-start | bytes 196616 | tf_op jit(solution)/shard_map/ppermute | solution.py:48
  70.5 2.5 %copy-start.3 = (f32[64]{0:T(128)}, f32[64]{0:T(128)S(1)}, u32[]{:S(2)}) copy-start(f32[64]{0:T(128)S(1)} %fusion.3) | copy-start | bytes 772
  79.7 62.6 %all-to-all-start.2 = ((f32[96,1,3072]{2,1,0:T(1,128)}), f32[96,1,3072]{2,1,0:T(1,128)S(1)}, u32[]{:S(2)}, u32[]{:S(2)}) async-start(f32[96,1,3072]{2,1,0:T(1,128)} %all_to_all.16), calls=%async_computation.2 | async-start | bytes 2359296 | tf_op jit(solution)/shard_map/all_to_all | solution.py:37
  96.6 17.4 %copy-start = (f32[1,64,512]{2,1,0:T(8,128)S(1)}, f32[1,64,512]{2,1,0:T(8,128)}, u32[]{:S(2)}) copy-start(f32[1,64,512]{2,1,0:T(8,128)} %get-tuple-element.4) | copy-start | bytes 393220
  96.6 17.4 %copy-start.4 = (f32[64]{0:T(128)S(1)}, f32[64]{0:T(128)}, u32[]{:S(2)}) copy-start(f32[64]{0:T(128)} %copy-done.3) | copy-start | bytes 772
  96.7 17.4 %copy-start.7 = (f32[64]{0:T(128)S(1)}, f32[64]{0:T(128)}, u32[]{:S(2)}) copy-start(f32[64]{0:T(128)} %param.8) | copy-start | bytes 772
  96.7 21.3 %copy-start.6 = (f32[64]{0:T(128)S(1)}, f32[64]{0:T(128)}, u32[]{:S(2)}) copy-start(f32[64]{0:T(128)} %copy-done.5) | copy-start | bytes 772
  96.8 10.8 %collective-permute-start.7 = (f32[1,64,512]{2,1,0:T(8,128)S(1)}, f32[1,64,512]{2,1,0:T(8,128)S(1)}, u32[]{:S(2)}, u32[]{:S(2)}) collective-permute-start(f32[1,64,512]{2,1,0:T(8,128)S(1)} %get-tuple-element.17), channel_id=1, source_target_pairs={{0,3},{3,6},{6,9},{9,12},{12,15},{15,18},{18,21},{21,0},{1,4},{4,7... | collective-permute-start | bytes 393224 | tf_op jit(solution)/shard_map/ppermute | solution.py:62
  96.8 12.8 %collective-permute-start.13 = (f32[1,64,512]{2,1,0:T(8,128)S(1)}, f32[1,64,512]{2,1,0:T(8,128)S(1)}, u32[]{:S(2)}, u32[]{:S(2)}) collective-permute-start(f32[1,64,512]{2,1,0:T(8,128)S(1)} %get-tuple-element.18), channel_id=1, source_target_pairs={{0,21},{3,0},{6,3},{9,6},{12,9},{15,12},{18,15},{21,18},{1,22},{4,... | collective-permute-start | bytes 393224 | tf_op jit(solution)/shard_map/ppermute | solution.py:62
  98.5 16.2 %collective-permute-start.12 = (f32[1,64,512]{2,1,0:T(8,128)S(1)}, f32[1,64,512]{2,1,0:T(8,128)S(1)}, u32[]{:S(2)}, u32[]{:S(2)}) collective-permute-start(f32[1,64,512]{2,1,0:T(8,128)S(1)} %get-tuple-element.19), channel_id=1, source_target_pairs={{0,18},{3,21},{6,0},{9,3},{12,6},{15,9},{18,12},{21,15},{1,19},{4,... | collective-permute-start | bytes 393224 | tf_op jit(solution)/shard_map/ppermute | solution.py:62
  101.1 13.6 %collective-permute-start.11 = (f32[1,64,512]{2,1,0:T(8,128)S(1)}, f32[1,64,512]{2,1,0:T(8,128)S(1)}, u32[]{:S(2)}, u32[]{:S(2)}) collective-permute-start(f32[1,64,512]{2,1,0:T(8,128)S(1)} %get-tuple-element.20), channel_id=1, source_target_pairs={{0,15},{3,18},{6,21},{9,0},{12,3},{15,6},{18,9},{21,12},{1,16},{4,... | collective-permute-start | bytes 393224 | tf_op jit(solution)/shard_map/ppermute | solution.py:62
  103.3 11.5 %collective-permute-start.10 = (f32[1,64,512]{2,1,0:T(8,128)S(1)}, f32[1,64,512]{2,1,0:T(8,128)S(1)}, u32[]{:S(2)}, u32[]{:S(2)}) collective-permute-start(f32[1,64,512]{2,1,0:T(8,128)S(1)} %get-tuple-element.21), channel_id=1, source_target_pairs={{0,12},{3,15},{6,18},{9,21},{12,0},{15,3},{18,6},{21,9},{1,13},{4,... | collective-permute-start | bytes 393224 | tf_op jit(solution)/shard_map/ppermute | solution.py:62
  107.5 7.8 %collective-permute-start.9 = (f32[1,64,512]{2,1,0:T(8,128)S(1)}, f32[1,64,512]{2,1,0:T(8,128)S(1)}, u32[]{:S(2)}, u32[]{:S(2)}) collective-permute-start(f32[1,64,512]{2,1,0:T(8,128)S(1)} %get-tuple-element.22), channel_id=1, source_target_pairs={{0,9},{3,12},{6,15},{9,18},{12,21},{15,0},{18,3},{21,6},{1,10},{4,... | collective-permute-start | bytes 393224 | tf_op jit(solution)/shard_map/ppermute | solution.py:62
  109.6 8.3 %collective-permute-start.8 = (f32[1,64,512]{2,1,0:T(8,128)S(1)}, f32[1,64,512]{2,1,0:T(8,128)S(1)}, u32[]{:S(2)}, u32[]{:S(2)}) collective-permute-start(f32[1,64,512]{2,1,0:T(8,128)S(1)} %get-tuple-element.23), channel_id=1, source_target_pairs={{0,6},{3,9},{6,12},{9,15},{12,18},{15,21},{18,0},{21,3},{1,7},{4,1... | collective-permute-start | bytes 393224 | tf_op jit(solution)/shard_map/ppermute | solution.py:62
  (1 other events, 0.8 us)

commit v7 on v6

--- a/solution.py
+++ b/solution.py
@@ -9,7 +9,7 @@
 
 OFFSETS = [(-1, -1), (-1, 0), (-1, 1), (0, -1), (0, 0), (0, 1), (1, -1), (1, 0), (1, 1)]
 EPSILON = 1e-08
-ROWS_AXES = ("z_lo", "y", "dom")
+SECT = ("sect_x", "sect_core")
 
 
 def moved(array, row_step, col_step):
@@ -38,8 +38,7 @@
     return jnp.sum(received, axis=0).reshape(rows, terms.shape[1])
 
 
-def gather_by_permutes(block, axis, count):
-    place = lax.axis_index(axis)
+def gather_by_permutes(block, axis, count, place):
     depth = block.shape[1]
     whole = jnp.zeros((block.shape[0], depth * count) + block.shape[2:], block.dtype)
     whole = lax.dynamic_update_slice_in_dim(whole, block, place * depth, 1)
@@ -51,28 +50,34 @@
     return whole
 
 
-def sum_by_permutes(whole, axis, count):
-    place = lax.axis_index(axis)
-    depth = whole.shape[1] // count
-    total = lax.dynamic_slice_in_dim(whole, place * depth, depth, 1)
-    for distance in range(1, count):
-        pairs = [(j, (j + distance) % count) for j in range(count)]
-        target = (place + distance) % count
-        part = lax.dynamic_slice_in_dim(whole, target * depth, depth, 1)
-        total = total + lax.ppermute(part, axis, pairs)
+def sum_core_then_x(whole):
+    samples, channels, pixels = whole.shape
+    chips, cores = lax.axis_size("sect_x"), lax.axis_size("sect_core")
+    depth = channels // (chips * cores)
+    core = lax.axis_index("sect_core")
+    chip = lax.axis_index("sect_x")
+    grid = whole.reshape(samples, chips, cores, depth, pixels)
+    mine = lax.dynamic_index_in_dim(grid, core, 2, keepdims=False)
+    other = lax.dynamic_index_in_dim(grid, 1 - core, 2, keepdims=False)
+    partial = mine + lax.ppermute(other, "sect_core", [(0, 1), (1, 0)])
+    total = lax.dynamic_index_in_dim(partial, chip, 1, keepdims=False)
+    for distance in range(1, chips):
+        pairs = [(j, (j + distance) % chips) for j in range(chips)]
+        part = lax.dynamic_index_in_dim(partial, (chip + distance) % chips, 1, keepdims=False)
+        total = total + lax.ppermute(part, "sect_x", pairs)
     return total
 
 
 def layer(features, weight, style, bias, adjoint):
     local_ch = features.shape[1]
-    sect_count = lax.axis_size("sect")
-    sect_place = lax.axis_index("sect")
+    sect_count = lax.axis_size(SECT)
+    sect_place = lax.axis_index("sect_x") * lax.axis_size("sect_core") + lax.axis_index("sect_core")
     channels = local_ch * sect_count
     own_style = lax.dynamic_slice_in_dim(style, sect_place * local_ch, local_ch, 1)
     local_mod = (features.astype(jnp.float32) * own_style[:, :, None]).astype(jnp.bfloat16)
-    modulated = gather_by_permutes(local_mod, "sect", sect_count)
-    along_y = gather_by_exchange(weight, "y", lax.axis_size("y"))
-    full_weight = gather_by_exchange(along_y, "z_lo", lax.axis_size("z_lo")).reshape(-1, local_ch)
+    modulated = gather_by_permutes(local_mod, SECT, sect_count, sect_place)
+    sample_count = lax.axis_size("sample")
+    full_weight = gather_by_exchange(weight, "sample", sample_count).reshape(-1, local_ch)
     kernel = full_weight.reshape(9, channels, local_ch)
     kernel_f = kernel.astype(jnp.float32)
     products = jnp.einsum("kio,nip->nkop", kernel, modulated, preferred_element_type=jnp.float32)
@@ -94,29 +99,31 @@
     )
     grad_main = jnp.einsum("nip,nkop->kio", modulated, back_shifts, preferred_element_type=jnp.float32)
     grad_terms = (grad_main + 2.0 * kernel_f * coupling[None]).reshape(-1, local_ch)
-    grad_weight = sum_by_exchange(grad_terms, ROWS_AXES)
+    grad_weight = sum_by_exchange(grad_terms, ("sample", "dom"))
     back = jnp.einsum("kio,nkop->nip", kernel, back_shifts, preferred_element_type=jnp.float32)
-    summed = sum_by_permutes(back, "sect", sect_count)
+    summed = sum_core_then_x(back)
     grad_features = (summed * own_style[:, :, None]).astype(jnp.bfloat16)
     return (styled, grad_weight, grad_features)
 
 
 def solution(mesh):
-    z_lo = 4
+    cores = 2
     fine = Mesh(
-        mesh.devices.reshape((z_lo, mesh.shape["sample"] // z_lo) + mesh.devices.shape[1:]),
-        ("z_lo", "y", "sect", "dom"),
+        mesh.devices.reshape(
+            (mesh.shape["sample"], mesh.shape["sect"] // cores, cores, mesh.shape["dom"])
+        ),
+        ("sample",) + SECT + ("dom",),
     )
     in_specs = (
-        P(ROWS_AXES, "sect", None),
-        P(("z_lo", "y"), "sect"),
-        P(ROWS_AXES, None),
-        P("sect"),
-        P(ROWS_AXES, "sect", None),
+        P(("sample", "dom"), SECT, None),
+        P("sample", SECT),
+        P(("sample", "dom"), None),
+        P(SECT),
+        P(("sample", "dom"), SECT, None),
     )
     out_specs = (
-        P(ROWS_AXES, "sect", None),
-        P(ROWS_AXES, "sect"),
-        P(ROWS_AXES, "sect", None),
+        P(("sample", "dom"), SECT, None),
+        P(("sample", "dom"), SECT),
+        P(("sample", "dom"), SECT, None),
     )
     return jax.shard_map(layer, mesh=fine, in_specs=in_specs, out_specs=out_specs, check_vma=False)

time: 145 us -> 141 us (0.972)
  starting transfers between devices: 63.6 us -> 59.3 us
    all_to_all x2 -> x1, waiting for transfers between devices: 30.4 us -> 21.1 us  [gather_by_exchange(): return lax.all_to_all(copies, axis, 0, 0, tiled=True)]
    ppermute x7 -> x4, starting transfers between devices: 17.2 us -> 10.5 us  [the longest x3 8.62 us: sum_core_then_x(): total = total + lax.ppermute(part, 'sect_x', pairs)]
    all_to_all x1, waiting for transfers between devices: 23.7 us -> 27.6 us  [sum_by_exchange(): received = lax.all_to_all(flat, axes, 0, 0, tiled=True)]
    ppermute x7 -> x4, waiting for transfers between devices: 3.17 us -> 6.63 us  [the longest x3 4.84 us: sum_core_then_x(): total = total + lax.ppermute(part, 'sect_x', pairs)]
    ppermute x7, waiting for transfers between devices: 1.78 us -> 4.56 us  [gather_by_permutes(): arrived = lax.ppermute(block, axis, pairs)]
    ppermute x7, starting transfers between devices: 15.3 us -> 17.6 us  [gather_by_permutes(): arrived = lax.ppermute(block, axis, pairs)]
    all_to_all x1, starting transfers between devices: 16.3 us -> 18.5 us  [sum_by_exchange(): received = lax.all_to_all(flat, axes, 0, 0, tiled=True)]
    all_to_all x2 -> x1, starting transfers between devices: 14.9 us -> 12.7 us  [gather_by_exchange(): return lax.all_to_all(copies, axis, 0, 0, tiled=True)]
  transfers between devices with their start and end apart: 17 -> 13, of which waited for: 6 -> 6; matrix products, arithmetic and copies ran while one was open for 3% -> 3% of each run, Pallas kernels for 0% -> 0%
where the time goes in v7:
time: 141 us; the launch traced here: 140 us
  waiting for transfers between devices  59.8 us (42%)
  starting transfers between devices  59.3 us (42%)
  local copies, waits for them, and re-layouts  11.1 us (8%)
  other arithmetic  5.46 us (4%)
  matrix products  2.84 us (2%)
    all_to_all x1, waiting for transfers between devices, sum_by_exchange(): received = lax.all_to_all(flat, axes, 0, 0, tiled=True)  27.6 us
    all_to_all x1, waiting for transfers between devices, gather_by_exchange(): return lax.all_to_all(copies, axis, 0, 0, tiled=True)  21.1 us
    all_to_all x1, starting transfers between devices, sum_by_exchange(): received = lax.all_to_all(flat, axes, 0, 0, tiled=True)  18.5 us
    ppermute x7, starting transfers between devices, gather_by_permutes(): arrived = lax.ppermute(block, axis, pairs)  17.6 us
    all_to_all x1, starting transfers between devices, gather_by_exchange(): return lax.all_to_all(copies, axis, 0, 0, tiled=True)  12.7 us
    ppermute x3, starting transfers between devices, sum_core_then_x(): total = total + lax.ppermute(part, 'sect_x', pairs)  8.62 us
    ppermute x3, waiting for transfers between devices, sum_core_then_x(): total = total + lax.ppermute(part, 'sect_x', pairs)  4.84 us
    ppermute x7, waiting for transfers between devices, gather_by_permutes(): arrived = lax.ppermute(block, axis, pairs)  4.56 us
  transfers between devices with their start and end apart: 13, of which 6 were waited for; matrix products, arithmetic and copies ran while one was open for 3% of the time, Pallas kernels for 0%

profile of v7, /device:TPU:50, one launch (start us, length us, event | category | flops | bytes accessed | tf_op | source)
XLA Modules:
  0.0 139.8 jit_solution(8009663596130424819)
XLA Ops:
  1.4 0.9 bitcast_dynamic-update-slice_fusion.8
  2.4 2.4 %collective-permute-start.5 = (bf16[1,64,512]{2,1,0:T(8,128)(2,1)S(1)}, bf16[1,64,512]{2,1,0:T(8,128)(2,1)S(1)}, u32[]{:S(2)}, u32[]{:S(2)}) collective-permute-start(bf16[1,64,512]{2,1,0:T(8,128)(2,1)S(1)} %get-tuple-element.8), channel_id=1, source_target_pairs={{0,18},{3,21},{6,0},{9,3},{12,6},{15,9},{18,12},{21,15},{1,19},{4,... | collective-permute-start | bytes 196616 | tf_op jit(solution)/shard_map/ppermute | solution.py:47
  4.8 3.5 %collective-permute-start.4 = (bf16[1,64,512]{2,1,0:T(8,128)(2,1)S(1)}, bf16[1,64,512]{2,1,0:T(8,128)(2,1)S(1)}, u32[]{:S(2)}, u32[]{:S(2)}) collective-permute-start(bf16[1,64,512]{2,1,0:T(8,128)(2,1)S(1)} %get-tuple-element.8), channel_id=1, source_target_pairs={{0,15},{3,18},{6,21},{9,0},{12,3},{15,6},{18,9},{21,12},{1,16},{4,... | collective-permute-start | bytes 196616 | tf_op jit(solution)/shard_map/ppermute | solution.py:47
  8.3 3.0 %collective-permute-start.3 = (bf16[1,64,512]{2,1,0:T(8,128)(2,1)S(1)}, bf16[1,64,512]{2,1,0:T(8,128)(2,1)S(1)}, u32[]{:S(2)}, u32[]{:S(2)}) collective-permute-start(bf16[1,64,512]{2,1,0:T(8,128)(2,1)S(1)} %get-tuple-element.8), channel_id=1, source_target_pairs={{0,12},{3,15},{6,18},{9,21},{12,0},{15,3},{18,6},{21,9},{1,13},{4,... | collective-permute-start | bytes 196616 | tf_op jit(solution)/shard_map/ppermute | solution.py:47
  11.3 3.7 %collective-permute-start.2 = (bf16[1,64,512]{2,1,0:T(8,128)(2,1)S(1)}, bf16[1,64,512]{2,1,0:T(8,128)(2,1)S(1)}, u32[]{:S(2)}, u32[]{:S(2)}) collective-permute-start(bf16[1,64,512]{2,1,0:T(8,128)(2,1)S(1)} %get-tuple-element.8), channel_id=1, source_target_pairs={{0,9},{3,12},{6,15},{9,18},{12,21},{15,0},{18,3},{21,6},{1,10},{4,... | collective-permute-start | bytes 196616 | tf_op jit(solution)/shard_map/ppermute | solution.py:47
  15.8 1.9 %broadcast_in_dim.2 = bf16[32,144,64]{1,2,0:T(8,128)(2,1)} broadcast(bf16[144,64]{0,1:T(8,128)(2,1)} %param.6), dimensions={1,2} | broadcast | bytes 608256 | tf_op jit(solution)/shard_map/broadcast_in_dim | solution.py:27
  17.7 12.7 %all-to-all-start = ((bf16[32,144,64]{1,2,0:T(8,128)(2,1)}), bf16[32,144,64]{1,2,0:T(8,128)(2,1)S(1)}, u32[]{:S(2)}, u32[]{:S(2)}) async-start(bf16[32,144,64]{1,2,0:T(8,128)(2,1)} %broadcast_in_dim.2), calls=%async_computation | async-start | bytes 2097152 | tf_op jit(solution)/shard_map/all_to_all | solution.py:28
  30.6 3.7 %collective-permute-start.1 = (bf16[1,64,512]{2,1,0:T(8,128)(2,1)S(1)}, bf16[1,64,512]{2,1,0:T(8,128)(2,1)S(1)}, u32[]{:S(2)}, u32[]{:S(2)}) collective-permute-start(bf16[1,64,512]{2,1,0:T(8,128)(2,1)S(1)} %get-tuple-element.8), channel_id=1, source_target_pairs={{0,6},{3,9},{6,12},{9,15},{12,18},{15,21},{18,0},{21,3},{1,7},{4,1... | collective-permute-start | bytes 196616 | tf_op jit(solution)/shard_map/ppermute | solution.py:47
  34.3 2.8 %collective-permute-done.1 = bf16[1,64,512]{2,1,0:T(8,128)(2,1)S(1)} collective-permute-done((bf16[1,64,512]{2,1,0:T(8,128)(2,1)S(1)}, bf16[1,64,512]{2,1,0:T(8,128)(2,1)S(1)}, u32[]{:S(2)}, u32[]{:S(2)}) %collective-permute-start.1) | collective-permute-done | bytes 65568 | tf_op jit(solution)/shard_map/ppermute | solution.py:47
  37.7 1.8 %collective-permute-done.6 = bf16[1,64,512]{2,1,0:T(8,128)(2,1)S(1)} collective-permute-done((bf16[1,64,512]{2,1,0:T(8,128)(2,1)S(1)}, bf16[1,64,512]{2,1,0:T(8,128)(2,1)S(1)}, u32[]{:S(2)}, u32[]{:S(2)}) %collective-permute-start.6) | collective-permute-done | bytes 65568 | tf_op jit(solution)/shard_map/ppermute | solution.py:47
  39.4 21.1 %all-to-all-done = bf16[32,144,64]{1,2,0:T(8,128)(2,1)S(1)} async-done(((bf16[32,144,64]{1,2,0:T(8,128)(2,1)}), bf16[32,144,64]{1,2,0:T(8,128)(2,1)S(1)}, u32[]{:S(2)}, u32[]{:S(2)}) %all-to-all-start) | async-done | bytes 589856 | tf_op jit(solution)/shard_map/all_to_all | solution.py:28
  61.1 1.8 %reshape_reshape.4 = bf16[9,512,64]{1,0,2:T(8,128)(2,1)S(1)} reshape(bf16[32,144,64]{1,0,2:T(8,128)(2,1)S(1)} %copy.13) | data formatting | bytes 1179648 | tf_op jit(solution)/shard_map/reshape;reshape | solution.py:81
  64.9 1.1 fusion.13
  66.9 1.6 %fusion = f32[9,512,64]{1,2,0:T(8,128)} fusion(bf16[9,512,64]{1,2,0:T(8,128)(2,1)S(1)} %get-tuple-element.6, bf16[1,9,64,512]{3,2,1,0:T(8,128)(2,1)S(1)} %fusion.61, f32[512,64]{0,1:T(8,128)S(1)} %multiply_multiply_fusion, bf16[512,512]{1,0:T(8,128)(2,1)S(1)} %bitcast_dynamic-update-slice_fusion.1), kind=kOutput, calls=%fused_computation.3 | convolution fusion | flops 302874624 | bytes 3014656 | tf_op jit(solution)/shard_map/nip,nkop->kio/dot_general | solution.py:100
  68.4 1.8 %copy.16 = f32[9,512,64]{2,1,0:T(8,128)S(1)} copy(f32[9,512,64]{1,2,0:T(8,128)} %fusion) | data formatting | bytes 2359296 | tf_op jit(solution)/shard_map/add | solution.py:101
  70.3 2.5 %all_to_all.12 = f32[96,1,3072]{2,1,0:T(1,128)} reshape(f32[9,512,64]{2,1,0:T(8,128)S(1)} %copy.16) | data formatting | bytes 2359296 | tf_op jit(solution)/shard_map/all_to_all | solution.py:37
  72.8 18.5 %all-to-all-start.1 = ((f32[96,1,3072]{2,1,0:T(1,128)}), f32[96,1,3072]{2,1,0:T(1,128)S(1)}, u32[]{:S(2)}, u32[]{:S(2)}) async-start(f32[96,1,3072]{2,1,0:T(1,128)} %all_to_all.12), calls=%async_computation.1 | async-start | bytes 2359296 | tf_op jit(solution)/shard_map/all_to_all | solution.py:37
  91.9 1.9 %collective-permute-start.7 = (f32[1,4,64,512]{3,2,1,0:T(8,128)S(1)}, f32[1,4,64,512]{3,2,1,0:T(8,128)S(1)}, u32[]{:S(2)}, u32[]{:S(2)}) collective-permute-start(f32[1,4,64,512]{3,2,1,0:T(8,128)S(1)} %dynamic-slice_bitcast_fusion), channel_id=1, source_target_pairs={{0,3},{3,0},{1,4},{4,1},{2,5},{5,2},{6,9},{9,6},{7,10},{10,7},{8,1... | collective-permute-start | bytes 1572872 | tf_op jit(solution)/shard_map/ppermute | solution.py:62
  94.0 1.8 %collective-permute-done.7 = f32[1,4,64,512]{3,2,1,0:T(8,128)S(1)} collective-permute-done((f32[1,4,64,512]{3,2,1,0:T(8,128)S(1)}, f32[1,4,64,512]{3,2,1,0:T(8,128)S(1)}, u32[]{:S(2)}, u32[]{:S(2)}) %collective-permute-start.7) | collective-permute-done | bytes 524320 | tf_op jit(solution)/shard_map/ppermute | solution.py:62
  95.9 1.9 %collective-permute-start.8 = (f32[1,64,512]{2,1,0:T(8,128)S(1)}, f32[1,64,512]{2,1,0:T(8,128)S(1)}, u32[]{:S(2)}, u32[]{:S(2)}) collective-permute-start(f32[1,64,512]{2,1,0:T(8,128)S(1)} %get-tuple-element.17), channel_id=1, source_target_pairs={{0,6},{6,12},{12,18},{18,0},{1,7},{7,13},{13,19},{19,1},{2,8},{8,1... | collective-permute-start | bytes 393224 | tf_op jit(solution)/shard_map/ppermute | solution.py:67
  97.8 3.9 %collective-permute-start.10 = (f32[1,64,512]{2,1,0:T(8,128)S(1)}, f32[1,64,512]{2,1,0:T(8,128)S(1)}, u32[]{:S(2)}, u32[]{:S(2)}) collective-permute-start(f32[1,64,512]{2,1,0:T(8,128)S(1)} %get-tuple-element.18), channel_id=1, source_target_pairs={{0,18},{6,0},{12,6},{18,12},{1,19},{7,1},{13,7},{19,13},{2,20},{8,... | collective-permute-start | bytes 393224 | tf_op jit(solution)/shard_map/ppermute | solution.py:67
  101.7 2.8 %collective-permute-start.9 = (f32[1,64,512]{2,1,0:T(8,128)S(1)}, f32[1,64,512]{2,1,0:T(8,128)S(1)}, u32[]{:S(2)}, u32[]{:S(2)}) collective-permute-start(f32[1,64,512]{2,1,0:T(8,128)S(1)} %get-tuple-element.19), channel_id=1, source_target_pairs={{0,12},{6,18},{12,0},{18,6},{1,13},{7,19},{13,1},{19,7},{2,14},{8,... | collective-permute-start | bytes 393224 | tf_op jit(solution)/shard_map/ppermute | solution.py:67
  105.3 4.8 %collective-permute-done.9 = f32[1,64,512]{2,1,0:T(8,128)S(1)} collective-permute-done((f32[1,64,512]{2,1,0:T(8,128)S(1)}, f32[1,64,512]{2,1,0:T(8,128)S(1)}, u32[]{:S(2)}, u32[]{:S(2)}) %collective-permute-start.9) | collective-permute-done | bytes 131104 | tf_op jit(solution)/shard_map/ppermute | solution.py:67
  110.8 27.6 %all-to-all-done.1 = f32[96,1,3072]{2,1,0:T(1,128)S(1)} async-done(((f32[96,1,3072]{2,1,0:T(1,128)}), f32[96,1,3072]{2,1,0:T(1,128)S(1)}, u32[]{:S(2)}, u32[]{:S(2)}) %all-to-all-start.1) | async-done | bytes 1179680 | tf_op jit(solution)/shard_map/all_to_all | solution.py:37
  (61 shorter events, 9.0 us)
Async XLA Ops:
  1.4 1.0 copy-start.5
  2.4 35.3 %collective-permute-start.5 = (bf16[1,64,512]{2,1,0:T(8,128)(2,1)S(1)}, bf16[1,64,512]{2,1,0:T(8,128)(2,1)S(1)}, u32[]{:S(2)}, u32[]{:S(2)}) collective-permute-start(bf16[1,64,512]{2,1,0:T(8,128)(2,1)S(1)} %get-tuple-element.8), channel_id=1, source_target_pairs={{0,18},{3,21},{6,0},{9,3},{12,6},{15,9},{18,12},{21,15},{1,19},{4,... | collective-permute-start | bytes 196616 | tf_op jit(solution)/shard_map/ppermute | solution.py:47
  4.8 32.8 %collective-permute-start.4 = (bf16[1,64,512]{2,1,0:T(8,128)(2,1)S(1)}, bf16[1,64,512]{2,1,0:T(8,128)(2,1)S(1)}, u32[]{:S(2)}, u32[]{:S(2)}) collective-permute-start(bf16[1,64,512]{2,1,0:T(8,128)(2,1)S(1)} %get-tuple-element.8), channel_id=1, source_target_pairs={{0,15},{3,18},{6,21},{9,0},{12,3},{15,6},{18,9},{21,12},{1,16},{4,... | collective-permute-start | bytes 196616 | tf_op jit(solution)/shard_map/ppermute | solution.py:47
  8.3 29.3 %collective-permute-start.3 = (bf16[1,64,512]{2,1,0:T(8,128)(2,1)S(1)}, bf16[1,64,512]{2,1,0:T(8,128)(2,1)S(1)}, u32[]{:S(2)}, u32[]{:S(2)}) collective-permute-start(bf16[1,64,512]{2,1,0:T(8,128)(2,1)S(1)} %get-tuple-element.8), channel_id=1, source_target_pairs={{0,12},{3,15},{6,18},{9,21},{12,0},{15,3},{18,6},{21,9},{1,13},{4,... | collective-permute-start | bytes 196616 | tf_op jit(solution)/shard_map/ppermute | solution.py:47
  11.3 26.2 %collective-permute-start.2 = (bf16[1,64,512]{2,1,0:T(8,128)(2,1)S(1)}, bf16[1,64,512]{2,1,0:T(8,128)(2,1)S(1)}, u32[]{:S(2)}, u32[]{:S(2)}) collective-permute-start(bf16[1,64,512]{2,1,0:T(8,128)(2,1)S(1)} %get-tuple-element.8), channel_id=1, source_target_pairs={{0,9},{3,12},{6,15},{9,18},{12,21},{15,0},{18,3},{21,6},{1,10},{4,... | collective-permute-start | bytes 196616 | tf_op jit(solution)/shard_map/ppermute | solution.py:47
  15.0 15.5 %collective-permute-start = (bf16[1,64,512]{2,1,0:T(8,128)(2,1)S(1)}, bf16[1,64,512]{2,1,0:T(8,128)(2,1)S(1)}, u32[]{:S(2)}, u32[]{:S(2)}) collective-permute-start(bf16[1,64,512]{2,1,0:T(8,128)(2,1)S(1)} %get-tuple-element.8), channel_id=1, source_target_pairs={{0,3},{3,6},{6,9},{9,12},{12,15},{15,18},{18,21},{21,0},{1,4},{4,7... | collective-permute-start | bytes 196616 | tf_op jit(solution)/shard_map/ppermute | solution.py:47
  17.7 12.8 %copy-start.2 = (f32[1,512]{1,0:T(1,128)S(1)}, f32[1,512]{1,0:T(1,128)}, u32[]{:S(2)}) copy-start(f32[1,512]{1,0:T(1,128)} %param.7) | copy-start | bytes 6148
  17.7 42.8 %all-to-all-start = ((bf16[32,144,64]{1,2,0:T(8,128)(2,1)}), bf16[32,144,64]{1,2,0:T(8,128)(2,1)S(1)}, u32[]{:S(2)}, u32[]{:S(2)}) async-start(bf16[32,144,64]{1,2,0:T(8,128)(2,1)} %broadcast_in_dim.2), calls=%async_computation | async-start | bytes 2097152 | tf_op jit(solution)/shard_map/all_to_all | solution.py:28
  30.6 6.5 %collective-permute-start.1 = (bf16[1,64,512]{2,1,0:T(8,128)(2,1)S(1)}, bf16[1,64,512]{2,1,0:T(8,128)(2,1)S(1)}, u32[]{:S(2)}, u32[]{:S(2)}) collective-permute-start(bf16[1,64,512]{2,1,0:T(8,128)(2,1)S(1)} %get-tuple-element.8), channel_id=1, source_target_pairs={{0,6},{3,9},{6,12},{9,15},{12,18},{15,21},{18,0},{21,3},{1,7},{4,1... | collective-permute-start | bytes 196616 | tf_op jit(solution)/shard_map/ppermute | solution.py:47
  37.1 2.4 %collective-permute-start.6 = (bf16[1,64,512]{2,1,0:T(8,128)(2,1)S(1)}, bf16[1,64,512]{2,1,0:T(8,128)(2,1)S(1)}, u32[]{:S(2)}, u32[]{:S(2)}) collective-permute-start(bf16[1,64,512]{2,1,0:T(8,128)(2,1)S(1)} %get-tuple-element.8), channel_id=1, source_target_pairs={{0,21},{3,0},{6,3},{9,6},{12,9},{15,12},{18,15},{21,18},{1,22},{4,... | collective-permute-start | bytes 196616 | tf_op jit(solution)/shard_map/ppermute | solution.py:47
  63.5 2.5 %copy-start.3 = (f32[64]{0:T(128)}, f32[64]{0:T(128)S(1)}, u32[]{:S(2)}) copy-start(f32[64]{0:T(128)S(1)} %fusion.3) | copy-start | bytes 772
  64.0 0.8 copy-start.1
  72.8 65.7 %all-to-all-start.1 = ((f32[96,1,3072]{2,1,0:T(1,128)}), f32[96,1,3072]{2,1,0:T(1,128)S(1)}, u32[]{:S(2)}, u32[]{:S(2)}) async-start(f32[96,1,3072]{2,1,0:T(1,128)} %all_to_all.12), calls=%async_computation.1 | async-start | bytes 2359296 | tf_op jit(solution)/shard_map/all_to_all | solution.py:37
  91.9 3.8 %collective-permute-start.7 = (f32[1,4,64,512]{3,2,1,0:T(8,128)S(1)}, f32[1,4,64,512]{3,2,1,0:T(8,128)S(1)}, u32[]{:S(2)}, u32[]{:S(2)}) collective-permute-start(f32[1,4,64,512]{3,2,1,0:T(8,128)S(1)} %dynamic-slice_bitcast_fusion), channel_id=1, source_target_pairs={{0,3},{3,0},{1,4},{4,1},{2,5},{5,2},{6,9},{9,6},{7,10},{10,7},{8,1... | collective-permute-start | bytes 1572872 | tf_op jit(solution)/shard_map/ppermute | solution.py:62
  93.9 10.6 %copy-start = (f32[1,64,512]{2,1,0:T(8,128)S(1)}, f32[1,64,512]{2,1,0:T(8,128)}, u32[]{:S(2)}) copy-start(f32[1,64,512]{2,1,0:T(8,128)} %get-tuple-element.4) | copy-start | bytes 393220
  93.9 10.6 %copy-start.4 = (f32[64]{0:T(128)S(1)}, f32[64]{0:T(128)}, u32[]{:S(2)}) copy-start(f32[64]{0:T(128)} %copy-done.3) | copy-start | bytes 772
  93.9 10.6 %copy-start.7 = (f32[64]{0:T(128)S(1)}, f32[64]{0:T(128)}, u32[]{:S(2)}) copy-start(f32[64]{0:T(128)} %param.8) | copy-start | bytes 772
  94.0 16.2 %copy-start.6 = (f32[64]{0:T(128)S(1)}, f32[64]{0:T(128)}, u32[]{:S(2)}) copy-start(f32[64]{0:T(128)} %copy-done.5) | copy-start | bytes 772
  95.9 9.4 %collective-permute-start.8 = (f32[1,64,512]{2,1,0:T(8,128)S(1)}, f32[1,64,512]{2,1,0:T(8,128)S(1)}, u32[]{:S(2)}, u32[]{:S(2)}) collective-permute-start(f32[1,64,512]{2,1,0:T(8,128)S(1)} %get-tuple-element.17), channel_id=1, source_target_pairs={{0,6},{6,12},{12,18},{18,0},{1,7},{7,13},{13,19},{19,1},{2,8},{8,1... | collective-permute-start | bytes 393224 | tf_op jit(solution)/shard_map/ppermute | solution.py:67
  97.8 7.5 %collective-permute-start.10 = (f32[1,64,512]{2,1,0:T(8,128)S(1)}, f32[1,64,512]{2,1,0:T(8,128)S(1)}, u32[]{:S(2)}, u32[]{:S(2)}) collective-permute-start(f32[1,64,512]{2,1,0:T(8,128)S(1)} %get-tuple-element.18), channel_id=1, source_target_pairs={{0,18},{6,0},{12,6},{18,12},{1,19},{7,1},{13,7},{19,13},{2,20},{8,... | collective-permute-start | bytes 393224 | tf_op jit(solution)/shard_map/ppermute | solution.py:67
  101.7 8.4 %collective-permute-start.9 = (f32[1,64,512]{2,1,0:T(8,128)S(1)}, f32[1,64,512]{2,1,0:T(8,128)S(1)}, u32[]{:S(2)}, u32[]{:S(2)}) collective-permute-start(f32[1,64,512]{2,1,0:T(8,128)S(1)} %get-tuple-element.19), channel_id=1, source_target_pairs={{0,12},{6,18},{12,0},{18,6},{1,13},{7,19},{13,1},{19,7},{2,14},{8,... | collective-permute-start | bytes 393224 | tf_op jit(solution)/shard_map/ppermute | solution.py:67

commit v8 on v6

--- a/solution.py
+++ b/solution.py
@@ -28,16 +28,6 @@
     return lax.all_to_all(copies, axis, 0, 0, tiled=True)
 
 
-def sum_by_exchange(terms, axes):
-    count = 1
-    for axis in (axes if isinstance(axes, tuple) else (axes,)):
-        count *= lax.axis_size(axis)
-    rows = terms.shape[0] // count
-    flat = terms.reshape(count, rows * terms.shape[1])
-    received = lax.all_to_all(flat, axes, 0, 0, tiled=True)
-    return jnp.sum(received, axis=0).reshape(rows, terms.shape[1])
-
-
 def gather_by_permutes(block, axis, count):
     place = lax.axis_index(axis)
     depth = block.shape[1]
@@ -63,6 +53,15 @@
     return total
 
 
+def sum_along_y_then_z(terms):
+    z_lo, y, dom = (lax.axis_size(axis) for axis in ROWS_AXES)
+    rows, cols = terms.shape[0] // (z_lo * y * dom), terms.shape[1]
+    owners = jnp.swapaxes(terms.reshape(z_lo, y, dom, rows * cols), 0, 1).reshape(y, -1)
+    along_y = jnp.sum(lax.all_to_all(owners, "y", 0, 0, tiled=True), axis=0)
+    along_z = lax.all_to_all(along_y.reshape(z_lo * dom, rows * cols), ("z_lo", "dom"), 0, 0, tiled=True)
+    return jnp.sum(along_z, axis=0).reshape(rows, cols)
+
+
 def layer(features, weight, style, bias, adjoint):
     local_ch = features.shape[1]
     sect_count = lax.axis_size("sect")
@@ -71,8 +70,8 @@
     own_style = lax.dynamic_slice_in_dim(style, sect_place * local_ch, local_ch, 1)
     local_mod = (features.astype(jnp.float32) * own_style[:, :, None]).astype(jnp.bfloat16)
     modulated = gather_by_permutes(local_mod, "sect", sect_count)
-    along_y = gather_by_exchange(weight, "y", lax.axis_size("y"))
-    full_weight = gather_by_exchange(along_y, "z_lo", lax.axis_size("z_lo")).reshape(-1, local_ch)
+    sample_count = lax.axis_size("z_lo") * lax.axis_size("y")
+    full_weight = gather_by_exchange(weight, ("z_lo", "y"), sample_count).reshape(-1, local_ch)
     kernel = full_weight.reshape(9, channels, local_ch)
     kernel_f = kernel.astype(jnp.float32)
     products = jnp.einsum("kio,nip->nkop", kernel, modulated, preferred_element_type=jnp.float32)
@@ -94,7 +93,7 @@
     )
     grad_main = jnp.einsum("nip,nkop->kio", modulated, back_shifts, preferred_element_type=jnp.float32)
     grad_terms = (grad_main + 2.0 * kernel_f * coupling[None]).reshape(-1, local_ch)
-    grad_weight = sum_by_exchange(grad_terms, ROWS_AXES)
+    grad_weight = sum_along_y_then_z(grad_terms)
     back = jnp.einsum("kio,nkop->nip", kernel, back_shifts, preferred_element_type=jnp.float32)
     summed = sum_by_permutes(back, "sect", sect_count)
     grad_features = (summed * own_style[:, :, None]).astype(jnp.bfloat16)

time: 145 us -> 145 us (level)
  the two profiles are of different devices: /device:TPU:50 before, /device:TPU:1 now
where the time goes in v8:
time: 145 us
  starting transfers between devices  79 us (54%)
  waiting for transfers between devices  38.3 us (26%)
  local copies, waits for them, and re-layouts  15.6 us (11%)
  other arithmetic  7.52 us (5%)
  matrix products  2.83 us (2%)
    ppermute x7, starting transfers between devices, sum_by_permutes(): total = total + lax.ppermute(part, axis, pairs)  28.8 us
    ppermute x7, starting transfers between devices, gather_by_permutes(): arrived = lax.ppermute(block, axis, pairs)  26.4 us
    all_to_all x1, waiting for transfers between devices, gather_by_exchange(): return lax.all_to_all(copies, axis, 0, 0, tiled=True)  14.8 us
    all_to_all x1, waiting for transfers between devices, sum_along_y_then_z(): along_y = jnp.sum(lax.all_to_all(owners, 'y', 0, 0, tiled=True), axis=0)  13.5 us
    all_to_all x1, starting transfers between devices, sum_along_y_then_z(): lax.all_to_all(along_y.reshape(z_lo * dom, rows * cols), ('z_lo', 'dom'),...  11.5 us
    all_to_all x1, starting transfers between devices, gather_by_exchange(): return lax.all_to_all(copies, axis, 0, 0, tiled=True)  6.46 us
    all_to_all x1, starting transfers between devices, sum_along_y_then_z(): along_y = jnp.sum(lax.all_to_all(owners, 'y', 0, 0, tiled=True), axis=0)  5.84 us
    ppermute x7, waiting for transfers between devices, gather_by_permutes(): arrived = lax.ppermute(block, axis, pairs)  5.49 us
  transfers between devices with their start and end apart: 17, of which 5 were waited for; matrix products, arithmetic and copies ran while one was open for 5% of the time, Pallas kernels for 0%

profile of v8, /device:TPU:1, one launch (start us, length us, event | category | flops | bytes accessed | tf_op | source)
XLA Modules:
  0.0 144.5 jit_solution(17474449982298139320)
XLA Ops:
  2.3 5.2 %collective-permute-start.5 = (bf16[1,64,512]{2,1,0:T(8,128)(2,1)S(1)}, bf16[1,64,512]{2,1,0:T(8,128)(2,1)S(1)}, u32[]{:S(2)}, u32[]{:S(2)}) collective-permute-start(bf16[1,64,512]{2,1,0:T(8,128)(2,1)S(1)} %get-tuple-element.8), channel_id=1, source_target_pairs={{0,18},{3,21},{6,0},{9,3},{12,6},{15,9},{18,12},{21,15},{1,19},{4,... | collective-permute-start | bytes 196616 | tf_op jit(solution)/shard_map/ppermute | solution.py:38
  7.6 3.3 %collective-permute-start.4 = (bf16[1,64,512]{2,1,0:T(8,128)(2,1)S(1)}, bf16[1,64,512]{2,1,0:T(8,128)(2,1)S(1)}, u32[]{:S(2)}, u32[]{:S(2)}) collective-permute-start(bf16[1,64,512]{2,1,0:T(8,128)(2,1)S(1)} %get-tuple-element.8), channel_id=1, source_target_pairs={{0,15},{3,18},{6,21},{9,0},{12,3},{15,6},{18,9},{21,12},{1,16},{4,... | collective-permute-start | bytes 196616 | tf_op jit(solution)/shard_map/ppermute | solution.py:38
  10.9 11.1 %collective-permute-start.3 = (bf16[1,64,512]{2,1,0:T(8,128)(2,1)S(1)}, bf16[1,64,512]{2,1,0:T(8,128)(2,1)S(1)}, u32[]{:S(2)}, u32[]{:S(2)}) collective-permute-start(bf16[1,64,512]{2,1,0:T(8,128)(2,1)S(1)} %get-tuple-element.8), channel_id=1, source_target_pairs={{0,12},{3,15},{6,18},{9,21},{12,0},{15,3},{18,6},{21,9},{1,13},{4,... | collective-permute-start | bytes 196616 | tf_op jit(solution)/shard_map/ppermute | solution.py:38
  22.0 1.9 %collective-permute-start.2 = (bf16[1,64,512]{2,1,0:T(8,128)(2,1)S(1)}, bf16[1,64,512]{2,1,0:T(8,128)(2,1)S(1)}, u32[]{:S(2)}, u32[]{:S(2)}) collective-permute-start(bf16[1,64,512]{2,1,0:T(8,128)(2,1)S(1)} %get-tuple-element.8), channel_id=1, source_target_pairs={{0,9},{3,12},{6,15},{9,18},{12,21},{15,0},{18,3},{21,6},{1,10},{4,... | collective-permute-start | bytes 196616 | tf_op jit(solution)/shard_map/ppermute | solution.py:38
  23.9 1.9 %broadcast_in_dim.2 = bf16[32,144,64]{1,2,0:T(8,128)(2,1)} broadcast(bf16[144,64]{0,1:T(8,128)(2,1)} %param.6), dimensions={1,2} | broadcast | bytes 608256 | tf_op jit(solution)/shard_map/broadcast_in_dim | solution.py:27
  25.8 6.5 %all-to-all-start = ((bf16[32,144,64]{1,2,0:T(8,128)(2,1)}), bf16[32,144,64]{1,2,0:T(8,128)(2,1)S(1)}, u32[]{:S(2)}, u32[]{:S(2)}) async-start(bf16[32,144,64]{1,2,0:T(8,128)(2,1)} %broadcast_in_dim.2), calls=%async_computation | async-start | bytes 2097152 | tf_op jit(solution)/shard_map/all_to_all | solution.py:28
  32.5 3.4 %collective-permute-start.1 = (bf16[1,64,512]{2,1,0:T(8,128)(2,1)S(1)}, bf16[1,64,512]{2,1,0:T(8,128)(2,1)S(1)}, u32[]{:S(2)}, u32[]{:S(2)}) collective-permute-start(bf16[1,64,512]{2,1,0:T(8,128)(2,1)S(1)} %get-tuple-element.8), channel_id=1, source_target_pairs={{0,6},{3,9},{6,12},{9,15},{12,18},{15,21},{18,0},{21,3},{1,7},{4,1... | collective-permute-start | bytes 196616 | tf_op jit(solution)/shard_map/ppermute | solution.py:38
  35.9 3.1 %collective-permute-done.1 = bf16[1,64,512]{2,1,0:T(8,128)(2,1)S(1)} collective-permute-done((bf16[1,64,512]{2,1,0:T(8,128)(2,1)S(1)}, bf16[1,64,512]{2,1,0:T(8,128)(2,1)S(1)}, u32[]{:S(2)}, u32[]{:S(2)}) %collective-permute-start.1) | collective-permute-done | bytes 65568 | tf_op jit(solution)/shard_map/ppermute | solution.py:38
  40.6 2.4 %collective-permute-done.6 = bf16[1,64,512]{2,1,0:T(8,128)(2,1)S(1)} collective-permute-done((bf16[1,64,512]{2,1,0:T(8,128)(2,1)S(1)}, bf16[1,64,512]{2,1,0:T(8,128)(2,1)S(1)}, u32[]{:S(2)}, u32[]{:S(2)}) %collective-permute-start.6) | collective-permute-done | bytes 65568 | tf_op jit(solution)/shard_map/ppermute | solution.py:38
  43.0 14.8 %all-to-all-done = bf16[32,144,64]{1,2,0:T(8,128)(2,1)S(1)} async-done(((bf16[32,144,64]{1,2,0:T(8,128)(2,1)}), bf16[32,144,64]{1,2,0:T(8,128)(2,1)S(1)}, u32[]{:S(2)}, u32[]{:S(2)}) %all-to-all-start) | async-done | bytes 589856 | tf_op jit(solution)/shard_map/all_to_all | solution.py:28
  58.4 1.8 %reshape_reshape.6 = bf16[9,512,64]{1,0,2:T(8,128)(2,1)S(1)} reshape(bf16[32,144,64]{1,0,2:T(8,128)(2,1)S(1)} %copy.21) | data formatting | bytes 1179648 | tf_op jit(solution)/shard_map/reshape;reshape | solution.py:75
  65.7 1.8 %copy.24 = f32[9,512,64]{2,1,0:T(8,128)S(1)} copy(f32[9,512,64]{1,2,0:T(8,128)} %fusion) | data formatting | bytes 2359296 | tf_op jit(solution)/shard_map/add | solution.py:95
  67.6 2.0 %reshape_reshape.7 = f32[4,8,3,3072]{3,2,1,0:T(4,128)} reshape(f32[9,512,64]{2,1,0:T(8,128)S(1)} %copy.24) | data formatting | bytes 2359296 | tf_op jit(solution)/shard_map/reshape;reshape | solution.py:59
  71.3 2.5 %all_to_all.20 = f32[8,1,36864]{2,1,0:T(1,128)} reshape(f32[8,4,3,3072]{3,2,1,0:T(4,128)S(1)} %copy.25) | data formatting | bytes 2359296 | tf_op jit(solution)/shard_map/all_to_all | solution.py:60
  73.8 5.8 %all-to-all-start.1 = ((f32[8,1,36864]{2,1,0:T(1,128)}), f32[8,1,36864]{2,1,0:T(1,128)S(1)}, u32[]{:S(2)}, u32[]{:S(2)}) async-start(f32[8,1,36864]{2,1,0:T(1,128)} %all_to_all.20), calls=%async_computation.1 | async-start | bytes 2359296 | tf_op jit(solution)/shard_map/all_to_all | solution.py:60
  81.1 7.8 %collective-permute-start.7 = (f32[1,64,512]{2,1,0:T(8,128)}, f32[1,64,512]{2,1,0:T(8,128)S(1)}, u32[]{:S(2)}, u32[]{:S(2)}) collective-permute-start(f32[1,64,512]{2,1,0:T(8,128)} %get-tuple-element.17), channel_id=1, source_target_pairs={{0,3},{3,6},{6,9},{9,12},{12,15},{15,18},{18,21},{21,0},{1,4},{4,7... | collective-permute-start | bytes 393224 | tf_op jit(solution)/shard_map/ppermute | solution.py:52
  88.9 2.0 %collective-permute-start.12 = (f32[1,64,512]{2,1,0:T(8,128)}, f32[1,64,512]{2,1,0:T(8,128)S(1)}, u32[]{:S(2)}, u32[]{:S(2)}) collective-permute-start(f32[1,64,512]{2,1,0:T(8,128)} %get-tuple-element.19), channel_id=1, source_target_pairs={{0,18},{3,21},{6,0},{9,3},{12,6},{15,9},{18,12},{21,15},{1,19},{4,... | collective-permute-start | bytes 393224 | tf_op jit(solution)/shard_map/ppermute | solution.py:52
  90.9 3.8 %collective-permute-start.11 = (f32[1,64,512]{2,1,0:T(8,128)S(1)}, f32[1,64,512]{2,1,0:T(8,128)}, u32[]{:S(2)}, u32[]{:S(2)}) collective-permute-start(f32[1,64,512]{2,1,0:T(8,128)S(1)} %get-tuple-element.20), channel_id=1, source_target_pairs={{0,15},{3,18},{6,21},{9,0},{12,3},{15,6},{18,9},{21,12},{1,16},{4,... | collective-permute-start | bytes 393224 | tf_op jit(solution)/shard_map/ppermute | solution.py:52
  94.7 3.4 %collective-permute-start.10 = (f32[1,64,512]{2,1,0:T(8,128)S(1)}, f32[1,64,512]{2,1,0:T(8,128)}, u32[]{:S(2)}, u32[]{:S(2)}) collective-permute-start(f32[1,64,512]{2,1,0:T(8,128)S(1)} %get-tuple-element.21), channel_id=1, source_target_pairs={{0,12},{3,15},{6,18},{9,21},{12,0},{15,3},{18,6},{21,9},{1,13},{4,... | collective-permute-start | bytes 393224 | tf_op jit(solution)/shard_map/ppermute | solution.py:52
  98.1 13.5 %all-to-all-done.1 = f32[8,1,36864]{2,1,0:T(1,128)S(1)} async-done(((f32[8,1,36864]{2,1,0:T(1,128)}), f32[8,1,36864]{2,1,0:T(1,128)S(1)}, u32[]{:S(2)}, u32[]{:S(2)}) %all-to-all-start.1) | async-done | bytes 1179680 | tf_op jit(solution)/shard_map/all_to_all | solution.py:60
  113.4 11.5 %all-to-all-start.2 = ((f32[12,1,3072]{2,1,0:T(1,128)}), f32[12,1,3072]{2,1,0:T(1,128)S(1)}, u32[]{:S(2)}, u32[]{:S(2)}) async-start(f32[12,1,3072]{2,1,0:T(1,128)} %bitcast.41), calls=%async_computation.2 | async-start | bytes 294912 | tf_op jit(solution)/shard_map/all_to_all | solution.py:61
  124.9 4.7 %collective-permute-start.9 = (f32[1,64,512]{2,1,0:T(8,128)S(1)}, f32[1,64,512]{2,1,0:T(8,128)S(1)}, u32[]{:S(2)}, u32[]{:S(2)}) collective-permute-start(f32[1,64,512]{2,1,0:T(8,128)S(1)} %get-tuple-element.22), channel_id=1, source_target_pairs={{0,9},{3,12},{6,15},{9,18},{12,21},{15,0},{18,3},{21,6},{1,10},{4,... | collective-permute-start | bytes 393224 | tf_op jit(solution)/shard_map/ppermute | solution.py:52
  129.7 7.1 %collective-permute-start.8 = (f32[1,64,512]{2,1,0:T(8,128)S(1)}, f32[1,64,512]{2,1,0:T(8,128)S(1)}, u32[]{:S(2)}, u32[]{:S(2)}) collective-permute-start(f32[1,64,512]{2,1,0:T(8,128)S(1)} %get-tuple-element.23), channel_id=1, source_target_pairs={{0,6},{3,9},{6,12},{9,15},{12,18},{15,21},{18,0},{21,3},{1,7},{4,1... | collective-permute-start | bytes 393224 | tf_op jit(solution)/shard_map/ppermute | solution.py:52
  137.5 4.5 %collective-permute-done.8 = f32[1,64,512]{2,1,0:T(8,128)S(1)} collective-permute-done((f32[1,64,512]{2,1,0:T(8,128)S(1)}, f32[1,64,512]{2,1,0:T(8,128)S(1)}, u32[]{:S(2)}, u32[]{:S(2)}) %collective-permute-start.8) | collective-permute-done | bytes 131104 | tf_op jit(solution)/shard_map/ppermute | solution.py:52
  (70 shorter events, 17.3 us)
Async XLA Ops:
  1.4 1.0 copy-start.5
  2.3 38.2 %collective-permute-start.5 = (bf16[1,64,512]{2,1,0:T(8,128)(2,1)S(1)}, bf16[1,64,512]{2,1,0:T(8,128)(2,1)S(1)}, u32[]{:S(2)}, u32[]{:S(2)}) collective-permute-start(bf16[1,64,512]{2,1,0:T(8,128)(2,1)S(1)} %get-tuple-element.8), channel_id=1, source_target_pairs={{0,18},{3,21},{6,0},{9,3},{12,6},{15,9},{18,12},{21,15},{1,19},{4,... | collective-permute-start | bytes 196616 | tf_op jit(solution)/shard_map/ppermute | solution.py:38
  7.6 32.9 %collective-permute-start.4 = (bf16[1,64,512]{2,1,0:T(8,128)(2,1)S(1)}, bf16[1,64,512]{2,1,0:T(8,128)(2,1)S(1)}, u32[]{:S(2)}, u32[]{:S(2)}) collective-permute-start(bf16[1,64,512]{2,1,0:T(8,128)(2,1)S(1)} %get-tuple-element.8), channel_id=1, source_target_pairs={{0,15},{3,18},{6,21},{9,0},{12,3},{15,6},{18,9},{21,12},{1,16},{4,... | collective-permute-start | bytes 196616 | tf_op jit(solution)/shard_map/ppermute | solution.py:38
  10.9 29.6 %collective-permute-start.3 = (bf16[1,64,512]{2,1,0:T(8,128)(2,1)S(1)}, bf16[1,64,512]{2,1,0:T(8,128)(2,1)S(1)}, u32[]{:S(2)}, u32[]{:S(2)}) collective-permute-start(bf16[1,64,512]{2,1,0:T(8,128)(2,1)S(1)} %get-tuple-element.8), channel_id=1, source_target_pairs={{0,12},{3,15},{6,18},{9,21},{12,0},{15,3},{18,6},{21,9},{1,13},{4,... | collective-permute-start | bytes 196616 | tf_op jit(solution)/shard_map/ppermute | solution.py:38
  22.0 18.4 %collective-permute-start.2 = (bf16[1,64,512]{2,1,0:T(8,128)(2,1)S(1)}, bf16[1,64,512]{2,1,0:T(8,128)(2,1)S(1)}, u32[]{:S(2)}, u32[]{:S(2)}) collective-permute-start(bf16[1,64,512]{2,1,0:T(8,128)(2,1)S(1)} %get-tuple-element.8), channel_id=1, source_target_pairs={{0,9},{3,12},{6,15},{9,18},{12,21},{15,0},{18,3},{21,6},{1,10},{4,... | collective-permute-start | bytes 196616 | tf_op jit(solution)/shard_map/ppermute | solution.py:38
  23.9 8.6 %collective-permute-start = (bf16[1,64,512]{2,1,0:T(8,128)(2,1)S(1)}, bf16[1,64,512]{2,1,0:T(8,128)(2,1)S(1)}, u32[]{:S(2)}, u32[]{:S(2)}) collective-permute-start(bf16[1,64,512]{2,1,0:T(8,128)(2,1)S(1)} %get-tuple-element.8), channel_id=1, source_target_pairs={{0,3},{3,6},{6,9},{9,12},{12,15},{15,18},{18,21},{21,0},{1,4},{4,7... | collective-permute-start | bytes 196616 | tf_op jit(solution)/shard_map/ppermute | solution.py:38
  25.8 6.6 %copy-start.2 = (f32[1,512]{1,0:T(1,128)S(1)}, f32[1,512]{1,0:T(1,128)}, u32[]{:S(2)}) copy-start(f32[1,512]{1,0:T(1,128)} %param.7) | copy-start | bytes 6148
  25.8 32.0 %all-to-all-start = ((bf16[32,144,64]{1,2,0:T(8,128)(2,1)}), bf16[32,144,64]{1,2,0:T(8,128)(2,1)S(1)}, u32[]{:S(2)}, u32[]{:S(2)}) async-start(bf16[32,144,64]{1,2,0:T(8,128)(2,1)} %broadcast_in_dim.2), calls=%async_computation | async-start | bytes 2097152 | tf_op jit(solution)/shard_map/all_to_all | solution.py:28
  32.5 6.5 %collective-permute-start.1 = (bf16[1,64,512]{2,1,0:T(8,128)(2,1)S(1)}, bf16[1,64,512]{2,1,0:T(8,128)(2,1)S(1)}, u32[]{:S(2)}, u32[]{:S(2)}) collective-permute-start(bf16[1,64,512]{2,1,0:T(8,128)(2,1)S(1)} %get-tuple-element.8), channel_id=1, source_target_pairs={{0,6},{3,9},{6,12},{9,15},{12,18},{15,21},{18,0},{21,3},{1,7},{4,1... | collective-permute-start | bytes 196616 | tf_op jit(solution)/shard_map/ppermute | solution.py:38
  39.0 4.0 %collective-permute-start.6 = (bf16[1,64,512]{2,1,0:T(8,128)(2,1)S(1)}, bf16[1,64,512]{2,1,0:T(8,128)(2,1)S(1)}, u32[]{:S(2)}, u32[]{:S(2)}) collective-permute-start(bf16[1,64,512]{2,1,0:T(8,128)(2,1)S(1)} %get-tuple-element.8), channel_id=1, source_target_pairs={{0,21},{3,0},{6,3},{9,6},{12,9},{15,12},{18,15},{21,18},{1,22},{4,... | collective-permute-start | bytes 196616 | tf_op jit(solution)/shard_map/ppermute | solution.py:38
  60.8 2.5 %copy-start.3 = (f32[64]{0:T(128)}, f32[64]{0:T(128)S(1)}, u32[]{:S(2)}) copy-start(f32[64]{0:T(128)S(1)} %fusion.3) | copy-start | bytes 772
  73.8 37.8 %all-to-all-start.1 = ((f32[8,1,36864]{2,1,0:T(1,128)}), f32[8,1,36864]{2,1,0:T(1,128)S(1)}, u32[]{:S(2)}, u32[]{:S(2)}) async-start(f32[8,1,36864]{2,1,0:T(1,128)} %all_to_all.20), calls=%async_computation.1 | async-start | bytes 2359296 | tf_op jit(solution)/shard_map/all_to_all | solution.py:60
  81.1 55.7 %copy-start = (f32[1,64,512]{2,1,0:T(8,128)S(1)}, f32[1,64,512]{2,1,0:T(8,128)}, u32[]{:S(2)}) copy-start(f32[1,64,512]{2,1,0:T(8,128)} %get-tuple-element.4) | copy-start | bytes 393220
  81.1 55.7 %copy-start.4 = (f32[64]{0:T(128)S(1)}, f32[64]{0:T(128)}, u32[]{:S(2)}) copy-start(f32[64]{0:T(128)} %copy-done.3) | copy-start | bytes 772
  81.1 55.7 %copy-start.7 = (f32[64]{0:T(128)S(1)}, f32[64]{0:T(128)}, u32[]{:S(2)}) copy-start(f32[64]{0:T(128)} %param.8) | copy-start | bytes 772
  81.1 60.9 %copy-start.6 = (f32[64]{0:T(128)S(1)}, f32[64]{0:T(128)}, u32[]{:S(2)}) copy-start(f32[64]{0:T(128)} %copy-done.5) | copy-start | bytes 772
  81.1 43.8 %collective-permute-start.7 = (f32[1,64,512]{2,1,0:T(8,128)}, f32[1,64,512]{2,1,0:T(8,128)S(1)}, u32[]{:S(2)}, u32[]{:S(2)}) collective-permute-start(f32[1,64,512]{2,1,0:T(8,128)} %get-tuple-element.17), channel_id=1, source_target_pairs={{0,3},{3,6},{6,9},{9,12},{12,15},{15,18},{18,21},{21,0},{1,4},{4,7... | collective-permute-start | bytes 393224 | tf_op jit(solution)/shard_map/ppermute | solution.py:52
  88.8 40.8 %collective-permute-start.13 = (f32[1,64,512]{2,1,0:T(8,128)}, f32[1,64,512]{2,1,0:T(8,128)S(1)}, u32[]{:S(2)}, u32[]{:S(2)}) collective-permute-start(f32[1,64,512]{2,1,0:T(8,128)} %get-tuple-element.18), channel_id=1, source_target_pairs={{0,21},{3,0},{6,3},{9,6},{12,9},{15,12},{18,15},{21,18},{1,22},{4,... | collective-permute-start | bytes 393224 | tf_op jit(solution)/shard_map/ppermute | solution.py:52
  88.9 48.7 %collective-permute-start.12 = (f32[1,64,512]{2,1,0:T(8,128)}, f32[1,64,512]{2,1,0:T(8,128)S(1)}, u32[]{:S(2)}, u32[]{:S(2)}) collective-permute-start(f32[1,64,512]{2,1,0:T(8,128)} %get-tuple-element.19), channel_id=1, source_target_pairs={{0,18},{3,21},{6,0},{9,3},{12,6},{15,9},{18,12},{21,15},{1,19},{4,... | collective-permute-start | bytes 393224 | tf_op jit(solution)/shard_map/ppermute | solution.py:52
  90.9 46.6 %collective-permute-start.11 = (f32[1,64,512]{2,1,0:T(8,128)S(1)}, f32[1,64,512]{2,1,0:T(8,128)}, u32[]{:S(2)}, u32[]{:S(2)}) collective-permute-start(f32[1,64,512]{2,1,0:T(8,128)S(1)} %get-tuple-element.20), channel_id=1, source_target_pairs={{0,15},{3,18},{6,21},{9,0},{12,3},{15,6},{18,9},{21,12},{1,16},{4,... | collective-permute-start | bytes 393224 | tf_op jit(solution)/shard_map/ppermute | solution.py:52
  94.7 42.8 %collective-permute-start.10 = (f32[1,64,512]{2,1,0:T(8,128)S(1)}, f32[1,64,512]{2,1,0:T(8,128)}, u32[]{:S(2)}, u32[]{:S(2)}) collective-permute-start(f32[1,64,512]{2,1,0:T(8,128)S(1)} %get-tuple-element.21), channel_id=1, source_target_pairs={{0,12},{3,15},{6,18},{9,21},{12,0},{15,3},{18,6},{21,9},{1,13},{4,... | collective-permute-start | bytes 393224 | tf_op jit(solution)/shard_map/ppermute | solution.py:52
  113.4 30.3 %all-to-all-start.2 = ((f32[12,1,3072]{2,1,0:T(1,128)}), f32[12,1,3072]{2,1,0:T(1,128)S(1)}, u32[]{:S(2)}, u32[]{:S(2)}) async-start(f32[12,1,3072]{2,1,0:T(1,128)} %bitcast.41), calls=%async_computation.2 | async-start | bytes 294912 | tf_op jit(solution)/shard_map/all_to_all | solution.py:61
  124.9 12.6 %collective-permute-start.9 = (f32[1,64,512]{2,1,0:T(8,128)S(1)}, f32[1,64,512]{2,1,0:T(8,128)S(1)}, u32[]{:S(2)}, u32[]{:S(2)}) collective-permute-start(f32[1,64,512]{2,1,0:T(8,128)S(1)} %get-tuple-element.22), channel_id=1, source_target_pairs={{0,9},{3,12},{6,15},{9,18},{12,21},{15,0},{18,3},{21,6},{1,10},{4,... | collective-permute-start | bytes 393224 | tf_op jit(solution)/shard_map/ppermute | solution.py:52
  129.7 12.3 %collective-permute-start.8 = (f32[1,64,512]{2,1,0:T(8,128)S(1)}, f32[1,64,512]{2,1,0:T(8,128)S(1)}, u32[]{:S(2)}, u32[]{:S(2)}) collective-permute-start(f32[1,64,512]{2,1,0:T(8,128)S(1)} %get-tuple-element.23), channel_id=1, source_target_pairs={{0,6},{3,9},{6,12},{9,15},{12,18},{15,21},{18,0},{21,3},{1,7},{4,1... | collective-permute-start | bytes 393224 | tf_op jit(solution)/shard_map/ppermute | solution.py:52
  (1 other events, 0.8 us)

commit v9 on v5

--- a/solution.py
+++ b/solution.py
@@ -31,8 +31,10 @@
     count = 1
     for axis in (axes if isinstance(axes, tuple) else (axes,)):
         count *= lax.axis_size(axis)
-    blocks = terms.reshape((count, terms.shape[0] // count) + terms.shape[1:])
-    return jnp.sum(lax.all_to_all(blocks, axes, 0, 0, tiled=True), axis=0)
+    rows = terms.shape[0] // count
+    flat = terms.reshape(count, rows * terms.shape[1])
+    received = lax.all_to_all(flat, axes, 0, 0, tiled=True)
+    return jnp.sum(received, axis=0).reshape(rows, terms.shape[1])
 
 
 def gather_by_permutes(block, axis, count):
@@ -69,7 +71,7 @@
     local_mod = (features.astype(jnp.float32) * own_style[:, :, None]).astype(jnp.bfloat16)
     modulated = gather_by_permutes(local_mod, "sect", sect_count)
     sample_count = lax.axis_size("sample")
-    full_weight = gather_by_exchange(weight, "sample", sample_count).reshape(-1, local_ch)
+    full_weight = gather_by_exchange(weight.reshape(-1), "sample", sample_count).reshape(-1, local_ch)
     kernel = full_weight.reshape(9, channels, local_ch)
     kernel_f = kernel.astype(jnp.float32)
     products = jnp.einsum("kio,nip->nkop", kernel, modulated, preferred_element_type=jnp.float32)

time: 145 us -> 134 us (0.924)
  the two profiles are of different devices: /device:TPU:50 before, /device:TPU:48 now
where the time goes in v9:
time: 134 us; the launch traced here: 133 us
  starting transfers between devices  63.5 us (47%)
  waiting for transfers between devices  40.6 us (30%)
  other arithmetic  12.8 us (10%)
  local copies, waits for them, and re-layouts  12.5 us (9%)
  matrix products  2.81 us (2%)
    all_to_all x1, waiting for transfers between devices, sum_by_exchange(): received = lax.all_to_all(flat, axes, 0, 0, tiled=True)  23.9 us
    ppermute x7, starting transfers between devices, gather_by_permutes(): arrived = lax.ppermute(block, axis, pairs)  18.4 us
    ppermute x7, starting transfers between devices, sum_by_permutes(): total = total + lax.ppermute(part, axis, pairs)  16.3 us
    all_to_all x1, starting transfers between devices, sum_by_exchange(): received = lax.all_to_all(flat, axes, 0, 0, tiled=True)  16.2 us
    all_to_all x1, starting transfers between devices, gather_by_exchange(): return lax.all_to_all(copies, axis, 0, 0, tiled=True)  12.6 us
    all_to_all x1, waiting for transfers between devices, gather_by_exchange(): return lax.all_to_all(copies, axis, 0, 0, tiled=True)  10.1 us
    broadcast_in_dim x1, other arithmetic, gather_by_exchange(): copies = jnp.broadcast_to(block[None], (count,) + block.shape)  4.17 us
    ppermute x7, waiting for transfers between devices, sum_by_permutes(): total = total + lax.ppermute(part, axis, pairs)  4.13 us
  transfers between devices with their start and end apart: 16, of which 5 were waited for; matrix products, arithmetic and copies ran while one was open for 7% of the time, Pallas kernels for 0%

profile of v9, /device:TPU:48, one launch (start us, length us, event | category | flops | bytes accessed | tf_op | source)
XLA Modules:
  0.0 133.5 jit_solution(15637862156911045796)
XLA Ops:
  2.4 3.4 %collective-permute-start.1 = (bf16[1,64,512]{2,1,0:T(8,128)(2,1)S(1)}, bf16[1,64,512]{2,1,0:T(8,128)(2,1)S(1)}, u32[]{:S(2)}, u32[]{:S(2)}) collective-permute-start(bf16[1,64,512]{2,1,0:T(8,128)(2,1)S(1)} %get-tuple-element.6), channel_id=1, source_target_pairs={{0,6},{3,9},{6,12},{9,15},{12,18},{15,21},{18,0},{21,3},{1,7},{4,1... | collective-permute-start | bytes 196616 | tf_op jit(solution)/shard_map/ppermute | solution.py:47
  5.8 4.0 %collective-permute-start.2 = (bf16[1,64,512]{2,1,0:T(8,128)(2,1)S(1)}, bf16[1,64,512]{2,1,0:T(8,128)(2,1)S(1)}, u32[]{:S(2)}, u32[]{:S(2)}) collective-permute-start(bf16[1,64,512]{2,1,0:T(8,128)(2,1)S(1)} %get-tuple-element.6), channel_id=1, source_target_pairs={{0,9},{3,12},{6,15},{9,18},{12,21},{15,0},{18,3},{21,6},{1,10},{4,... | collective-permute-start | bytes 196616 | tf_op jit(solution)/shard_map/ppermute | solution.py:47
  9.8 3.9 %collective-permute-start.3 = (bf16[1,64,512]{2,1,0:T(8,128)(2,1)S(1)}, bf16[1,64,512]{2,1,0:T(8,128)(2,1)S(1)}, u32[]{:S(2)}, u32[]{:S(2)}) collective-permute-start(bf16[1,64,512]{2,1,0:T(8,128)(2,1)S(1)} %get-tuple-element.6), channel_id=1, source_target_pairs={{0,12},{3,15},{6,18},{9,21},{12,0},{15,3},{18,6},{21,9},{1,13},{4,... | collective-permute-start | bytes 196616 | tf_op jit(solution)/shard_map/ppermute | solution.py:47
  13.7 3.5 %collective-permute-start.4 = (bf16[1,64,512]{2,1,0:T(8,128)(2,1)S(1)}, bf16[1,64,512]{2,1,0:T(8,128)(2,1)S(1)}, u32[]{:S(2)}, u32[]{:S(2)}) collective-permute-start(bf16[1,64,512]{2,1,0:T(8,128)(2,1)S(1)} %get-tuple-element.6), channel_id=1, source_target_pairs={{0,15},{3,18},{6,21},{9,0},{12,3},{15,6},{18,9},{21,12},{1,16},{4,... | collective-permute-start | bytes 196616 | tf_op jit(solution)/shard_map/ppermute | solution.py:47
  19.3 4.2 %reduce.3 = bf16[32,9216]{1,0:T(8,128)(2,1)S(1)} reduce(bf16[32,1,9216]{2,1,0:T(2,128)(2,1)S(1)} %broadcast_in_dim.5, bf16[]{:T(256)} %broadcast.519), dimensions={1}, to_apply=%broadcast_in_dim.5.reduce_sub_computation | reduce | bytes 1179650 | tf_op jit(solution)/shard_map/broadcast_in_dim | solution.py:26
  23.5 1.3 reshape.460
  24.8 12.6 %all-to-all-start = ((bf16[32,2,4608]{2,1,0:T(2,128)(2,1)}), bf16[32,2,4608]{2,1,0:T(2,128)(2,1)S(1)}, u32[]{:S(2)}, u32[]{:S(2)}) async-start(bf16[32,2,4608]{2,1,0:T(2,128)(2,1)} %reshape.460), calls=%async_computation | async-start | bytes 1179648 | tf_op jit(solution)/shard_map/all_to_all | solution.py:27
  37.5 3.5 %collective-permute-start.5 = (bf16[1,64,512]{2,1,0:T(8,128)(2,1)S(1)}, bf16[1,64,512]{2,1,0:T(8,128)(2,1)S(1)}, u32[]{:S(2)}, u32[]{:S(2)}) collective-permute-start(bf16[1,64,512]{2,1,0:T(8,128)(2,1)S(1)} %get-tuple-element.6), channel_id=1, source_target_pairs={{0,18},{3,21},{6,0},{9,3},{12,6},{15,9},{18,12},{21,15},{1,19},{4,... | collective-permute-start | bytes 196616 | tf_op jit(solution)/shard_map/ppermute | solution.py:47
  41.2 2.5 %collective-permute-done.5 = bf16[1,64,512]{2,1,0:T(8,128)(2,1)S(1)} collective-permute-done((bf16[1,64,512]{2,1,0:T(8,128)(2,1)S(1)}, bf16[1,64,512]{2,1,0:T(8,128)(2,1)S(1)}, u32[]{:S(2)}, u32[]{:S(2)}) %collective-permute-start.5) | collective-permute-done | bytes 65568 | tf_op jit(solution)/shard_map/ppermute | solution.py:47
  43.7 10.1 %all-to-all-done = bf16[32,2,4608]{2,1,0:T(2,128)(2,1)S(1)} async-done(((bf16[32,2,4608]{2,1,0:T(2,128)(2,1)}), bf16[32,2,4608]{2,1,0:T(2,128)(2,1)S(1)}, u32[]{:S(2)}, u32[]{:S(2)}) %all-to-all-start) | async-done | bytes 589856 | tf_op jit(solution)/shard_map/all_to_all | solution.py:27
  54.3 3.5 %reduce.2 = bf16[32,9216]{1,0:T(8,128)(2,1)S(1)} reduce(bf16[32,1,9216]{2,1,0:T(2,128)(2,1)S(1)} %reshape.461, bf16[]{:T(256)} %constant.215), dimensions={1}, to_apply=%all_to_all.10.reduce_sub_computation | reduce | bytes 1179650 | tf_op jit(solution)/shard_map/all_to_all | solution.py:27
  60.6 1.1 fusion.12
  63.4 1.5 %fusion = f32[9,512,64]{1,2,0:T(8,128)} fusion(bf16[9,512,64]{1,2,0:T(8,128)(2,1)S(1)} %copy.14, bf16[1,9,64,512]{3,2,1,0:T(8,128)(2,1)S(1)} %fusion.64, f32[512,64]{0,1:T(8,128)S(1)} %multiply_multiply_fusion, bf16[512,512]{1,0:T(8,128)(2,1)S(1)} %bitcast_dynamic-update-slice_fusion.1), kind=kOutput, calls=%fused_computation.3 | convolution fusion | flops 302874624 | bytes 3014656 | tf_op jit(solution)/shard_map/nip,nkop->kio/dot_general | solution.py:94
  64.9 1.8 %copy.16 = f32[9,512,64]{2,1,0:T(8,128)S(1)} copy(f32[9,512,64]{1,2,0:T(8,128)} %fusion) | data formatting | bytes 2359296 | tf_op jit(solution)/shard_map/add | solution.py:95
  66.8 2.5 %all_to_all.13 = f32[96,1,3072]{2,1,0:T(1,128)} reshape(f32[9,512,64]{2,1,0:T(8,128)S(1)} %copy.16) | data formatting | bytes 2359296 | tf_op jit(solution)/shard_map/all_to_all | solution.py:36
  69.3 16.2 %all-to-all-start.1 = ((f32[96,1,3072]{2,1,0:T(1,128)}), f32[96,1,3072]{2,1,0:T(1,128)S(1)}, u32[]{:S(2)}, u32[]{:S(2)}) async-start(f32[96,1,3072]{2,1,0:T(1,128)} %all_to_all.13), calls=%async_computation.1 | async-start | bytes 2359296 | tf_op jit(solution)/shard_map/all_to_all | solution.py:36
  86.3 3.7 %collective-permute-start.10 = (f32[1,64,512]{2,1,0:T(8,128)S(1)}, f32[1,64,512]{2,1,0:T(8,128)S(1)}, u32[]{:S(2)}, u32[]{:S(2)}) collective-permute-start(f32[1,64,512]{2,1,0:T(8,128)S(1)} %get-tuple-element.19), channel_id=1, source_target_pairs={{0,12},{3,15},{6,18},{9,21},{12,0},{15,3},{18,6},{21,9},{1,13},{4,... | collective-permute-start | bytes 393224 | tf_op jit(solution)/shard_map/ppermute | solution.py:61
  90.0 1.9 %collective-permute-start.11 = (f32[1,64,512]{2,1,0:T(8,128)S(1)}, f32[1,64,512]{2,1,0:T(8,128)S(1)}, u32[]{:S(2)}, u32[]{:S(2)}) collective-permute-start(f32[1,64,512]{2,1,0:T(8,128)S(1)} %get-tuple-element.18), channel_id=1, source_target_pairs={{0,15},{3,18},{6,21},{9,0},{12,3},{15,6},{18,9},{21,12},{1,16},{4,... | collective-permute-start | bytes 393224 | tf_op jit(solution)/shard_map/ppermute | solution.py:61
  91.9 3.7 %collective-permute-start.12 = (f32[1,64,512]{2,1,0:T(8,128)S(1)}, f32[1,64,512]{2,1,0:T(8,128)S(1)}, u32[]{:S(2)}, u32[]{:S(2)}) collective-permute-start(f32[1,64,512]{2,1,0:T(8,128)S(1)} %get-tuple-element.17), channel_id=1, source_target_pairs={{0,18},{3,21},{6,0},{9,3},{12,6},{15,9},{18,12},{21,15},{1,19},{4,... | collective-permute-start | bytes 393224 | tf_op jit(solution)/shard_map/ppermute | solution.py:61
  96.1 3.4 %collective-permute-start.8 = (f32[1,64,512]{2,1,0:T(8,128)S(1)}, f32[1,64,512]{2,1,0:T(8,128)S(1)}, u32[]{:S(2)}, u32[]{:S(2)}) collective-permute-start(f32[1,64,512]{2,1,0:T(8,128)S(1)} %get-tuple-element.21), channel_id=1, source_target_pairs={{0,6},{3,9},{6,12},{9,15},{12,18},{15,21},{18,0},{21,3},{1,7},{4,1... | collective-permute-start | bytes 393224 | tf_op jit(solution)/shard_map/ppermute | solution.py:61
  99.5 3.1 %collective-permute-start.9 = (f32[1,64,512]{2,1,0:T(8,128)S(1)}, f32[1,64,512]{2,1,0:T(8,128)S(1)}, u32[]{:S(2)}, u32[]{:S(2)}) collective-permute-start(f32[1,64,512]{2,1,0:T(8,128)S(1)} %get-tuple-element.20), channel_id=1, source_target_pairs={{0,9},{3,12},{6,15},{9,18},{12,21},{15,0},{18,3},{21,6},{1,10},{4,... | collective-permute-start | bytes 393224 | tf_op jit(solution)/shard_map/ppermute | solution.py:61
  103.4 1.6 %collective-permute-done.8 = f32[1,64,512]{2,1,0:T(8,128)S(1)} collective-permute-done((f32[1,64,512]{2,1,0:T(8,128)S(1)}, f32[1,64,512]{2,1,0:T(8,128)S(1)}, u32[]{:S(2)}, u32[]{:S(2)}) %collective-permute-start.8) | collective-permute-done | bytes 131104 | tf_op jit(solution)/shard_map/ppermute | solution.py:61
  105.0 2.6 %collective-permute-done.9 = f32[1,64,512]{2,1,0:T(8,128)S(1)} collective-permute-done((f32[1,64,512]{2,1,0:T(8,128)S(1)}, f32[1,64,512]{2,1,0:T(8,128)S(1)}, u32[]{:S(2)}, u32[]{:S(2)}) %collective-permute-start.9) | collective-permute-done | bytes 131104 | tf_op jit(solution)/shard_map/ppermute | solution.py:61
  108.2 23.9 %all-to-all-done.1 = f32[96,1,3072]{2,1,0:T(1,128)S(1)} async-done(((f32[96,1,3072]{2,1,0:T(1,128)}), f32[96,1,3072]{2,1,0:T(1,128)S(1)}, u32[]{:S(2)}, u32[]{:S(2)}) %all-to-all-start.1) | async-done | bytes 1179680 | tf_op jit(solution)/shard_map/all_to_all | solution.py:36
  (68 shorter events, 12.8 us)
Async XLA Ops:
  2.3 35.2 %collective-permute-start = (bf16[1,64,512]{2,1,0:T(8,128)(2,1)S(1)}, bf16[1,64,512]{2,1,0:T(8,128)(2,1)S(1)}, u32[]{:S(2)}, u32[]{:S(2)}) collective-permute-start(bf16[1,64,512]{2,1,0:T(8,128)(2,1)S(1)} %get-tuple-element.6), channel_id=1, source_target_pairs={{0,3},{3,6},{6,9},{9,12},{12,15},{15,18},{18,21},{21,0},{1,4},{4,7... | collective-permute-start | bytes 196616 | tf_op jit(solution)/shard_map/ppermute | solution.py:47
  2.4 38.7 %collective-permute-start.1 = (bf16[1,64,512]{2,1,0:T(8,128)(2,1)S(1)}, bf16[1,64,512]{2,1,0:T(8,128)(2,1)S(1)}, u32[]{:S(2)}, u32[]{:S(2)}) collective-permute-start(bf16[1,64,512]{2,1,0:T(8,128)(2,1)S(1)} %get-tuple-element.6), channel_id=1, source_target_pairs={{0,6},{3,9},{6,12},{9,15},{12,18},{15,21},{18,0},{21,3},{1,7},{4,1... | collective-permute-start | bytes 196616 | tf_op jit(solution)/shard_map/ppermute | solution.py:47
  5.8 35.4 %collective-permute-start.2 = (bf16[1,64,512]{2,1,0:T(8,128)(2,1)S(1)}, bf16[1,64,512]{2,1,0:T(8,128)(2,1)S(1)}, u32[]{:S(2)}, u32[]{:S(2)}) collective-permute-start(bf16[1,64,512]{2,1,0:T(8,128)(2,1)S(1)} %get-tuple-element.6), channel_id=1, source_target_pairs={{0,9},{3,12},{6,15},{9,18},{12,21},{15,0},{18,3},{21,6},{1,10},{4,... | collective-permute-start | bytes 196616 | tf_op jit(solution)/shard_map/ppermute | solution.py:47
  9.8 31.4 %collective-permute-start.3 = (bf16[1,64,512]{2,1,0:T(8,128)(2,1)S(1)}, bf16[1,64,512]{2,1,0:T(8,128)(2,1)S(1)}, u32[]{:S(2)}, u32[]{:S(2)}) collective-permute-start(bf16[1,64,512]{2,1,0:T(8,128)(2,1)S(1)} %get-tuple-element.6), channel_id=1, source_target_pairs={{0,12},{3,15},{6,18},{9,21},{12,0},{15,3},{18,6},{21,9},{1,13},{4,... | collective-permute-start | bytes 196616 | tf_op jit(solution)/shard_map/ppermute | solution.py:47
  13.7 27.5 %collective-permute-start.4 = (bf16[1,64,512]{2,1,0:T(8,128)(2,1)S(1)}, bf16[1,64,512]{2,1,0:T(8,128)(2,1)S(1)}, u32[]{:S(2)}, u32[]{:S(2)}) collective-permute-start(bf16[1,64,512]{2,1,0:T(8,128)(2,1)S(1)} %get-tuple-element.6), channel_id=1, source_target_pairs={{0,15},{3,18},{6,21},{9,0},{12,3},{15,6},{18,9},{21,12},{1,16},{4,... | collective-permute-start | bytes 196616 | tf_op jit(solution)/shard_map/ppermute | solution.py:47
  23.5 13.9 %copy-start.4 = (f32[1,512]{1,0:T(1,128)S(1)}, f32[1,512]{1,0:T(1,128)}, u32[]{:S(2)}) copy-start(f32[1,512]{1,0:T(1,128)} %param.7) | copy-start | bytes 6148
  24.8 29.1 %all-to-all-start = ((bf16[32,2,4608]{2,1,0:T(2,128)(2,1)}), bf16[32,2,4608]{2,1,0:T(2,128)(2,1)S(1)}, u32[]{:S(2)}, u32[]{:S(2)}) async-start(bf16[32,2,4608]{2,1,0:T(2,128)(2,1)} %reshape.460), calls=%async_computation | async-start | bytes 1179648 | tf_op jit(solution)/shard_map/all_to_all | solution.py:27
  37.5 6.2 %collective-permute-start.5 = (bf16[1,64,512]{2,1,0:T(8,128)(2,1)S(1)}, bf16[1,64,512]{2,1,0:T(8,128)(2,1)S(1)}, u32[]{:S(2)}, u32[]{:S(2)}) collective-permute-start(bf16[1,64,512]{2,1,0:T(8,128)(2,1)S(1)} %get-tuple-element.6), channel_id=1, source_target_pairs={{0,18},{3,21},{6,0},{9,3},{12,6},{15,9},{18,12},{21,15},{1,19},{4,... | collective-permute-start | bytes 196616 | tf_op jit(solution)/shard_map/ppermute | solution.py:47
  41.1 2.6 %collective-permute-start.6 = (bf16[1,64,512]{2,1,0:T(8,128)(2,1)S(1)}, bf16[1,64,512]{2,1,0:T(8,128)(2,1)S(1)}, u32[]{:S(2)}, u32[]{:S(2)}) collective-permute-start(bf16[1,64,512]{2,1,0:T(8,128)(2,1)S(1)} %get-tuple-element.6), channel_id=1, source_target_pairs={{0,21},{3,0},{6,3},{9,6},{12,9},{15,12},{18,15},{21,18},{1,22},{4,... | collective-permute-start | bytes 196616 | tf_op jit(solution)/shard_map/ppermute | solution.py:47
  59.8 0.8 copy-start.3
  62.5 0.8 copy-start
  69.3 16.2 %copy-start.1 = (bf16[1,9,64,512]{3,2,1,0:T(8,128)(2,1)S(1)}, bf16[1,9,64,512]{3,2,1,0:T(8,128)(2,1)}, u32[]{:S(2)}) copy-start(bf16[1,9,64,512]{3,2,1,0:T(8,128)(2,1)} %copy-done) | copy-start | bytes 1769476
  69.3 62.8 %all-to-all-start.1 = ((f32[96,1,3072]{2,1,0:T(1,128)}), f32[96,1,3072]{2,1,0:T(1,128)S(1)}, u32[]{:S(2)}, u32[]{:S(2)}) async-start(f32[96,1,3072]{2,1,0:T(1,128)} %all_to_all.13), calls=%async_computation.1 | async-start | bytes 2359296 | tf_op jit(solution)/shard_map/all_to_all | solution.py:36
  86.1 16.5 %copy-start.2 = (f32[1,64,512]{2,1,0:T(8,128)S(1)}, f32[1,64,512]{2,1,0:T(8,128)}, u32[]{:S(2)}) copy-start(f32[1,64,512]{2,1,0:T(8,128)} %get-tuple-element.4) | copy-start | bytes 393220
  86.1 16.5 %copy-start.5 = (f32[64]{0:T(128)S(1)}, f32[64]{0:T(128)}, u32[]{:S(2)}) copy-start(f32[64]{0:T(128)} %param.8) | copy-start | bytes 772
  86.3 9.8 %collective-permute-start.10 = (f32[1,64,512]{2,1,0:T(8,128)S(1)}, f32[1,64,512]{2,1,0:T(8,128)S(1)}, u32[]{:S(2)}, u32[]{:S(2)}) collective-permute-start(f32[1,64,512]{2,1,0:T(8,128)S(1)} %get-tuple-element.19), channel_id=1, source_target_pairs={{0,12},{3,15},{6,18},{9,21},{12,0},{15,3},{18,6},{21,9},{1,13},{4,... | collective-permute-start | bytes 393224 | tf_op jit(solution)/shard_map/ppermute | solution.py:61
  90.0 9.5 %collective-permute-start.11 = (f32[1,64,512]{2,1,0:T(8,128)S(1)}, f32[1,64,512]{2,1,0:T(8,128)S(1)}, u32[]{:S(2)}, u32[]{:S(2)}) collective-permute-start(f32[1,64,512]{2,1,0:T(8,128)S(1)} %get-tuple-element.18), channel_id=1, source_target_pairs={{0,15},{3,18},{6,21},{9,0},{12,3},{15,6},{18,9},{21,12},{1,16},{4,... | collective-permute-start | bytes 393224 | tf_op jit(solution)/shard_map/ppermute | solution.py:61
  91.9 11.5 %collective-permute-start.12 = (f32[1,64,512]{2,1,0:T(8,128)S(1)}, f32[1,64,512]{2,1,0:T(8,128)S(1)}, u32[]{:S(2)}, u32[]{:S(2)}) collective-permute-start(f32[1,64,512]{2,1,0:T(8,128)S(1)} %get-tuple-element.17), channel_id=1, source_target_pairs={{0,18},{3,21},{6,0},{9,3},{12,6},{15,9},{18,12},{21,15},{1,19},{4,... | collective-permute-start | bytes 393224 | tf_op jit(solution)/shard_map/ppermute | solution.py:61
  95.6 7.8 %collective-permute-start.13 = (f32[1,64,512]{2,1,0:T(8,128)S(1)}, f32[1,64,512]{2,1,0:T(8,128)S(1)}, u32[]{:S(2)}, u32[]{:S(2)}) collective-permute-start(f32[1,64,512]{2,1,0:T(8,128)S(1)} %get-tuple-element.16), channel_id=1, source_target_pairs={{0,21},{3,0},{6,3},{9,6},{12,9},{15,12},{18,15},{21,18},{1,22},{4,... | collective-permute-start | bytes 393224 | tf_op jit(solution)/shard_map/ppermute | solution.py:61
  95.9 7.5 %collective-permute-start.7 = (f32[1,64,512]{2,1,0:T(8,128)S(1)}, f32[1,64,512]{2,1,0:T(8,128)S(1)}, u32[]{:S(2)}, u32[]{:S(2)}) collective-permute-start(f32[1,64,512]{2,1,0:T(8,128)S(1)} %get-tuple-element.15), channel_id=1, source_target_pairs={{0,3},{3,6},{6,9},{9,12},{12,15},{15,18},{18,21},{21,0},{1,4},{4,7... | collective-permute-start | bytes 393224 | tf_op jit(solution)/shard_map/ppermute | solution.py:61
  96.1 8.8 %collective-permute-start.8 = (f32[1,64,512]{2,1,0:T(8,128)S(1)}, f32[1,64,512]{2,1,0:T(8,128)S(1)}, u32[]{:S(2)}, u32[]{:S(2)}) collective-permute-start(f32[1,64,512]{2,1,0:T(8,128)S(1)} %get-tuple-element.21), channel_id=1, source_target_pairs={{0,6},{3,9},{6,12},{9,15},{12,18},{15,21},{18,0},{21,3},{1,7},{4,1... | collective-permute-start | bytes 393224 | tf_op jit(solution)/shard_map/ppermute | solution.py:61
  99.5 8.0 %collective-permute-start.9 = (f32[1,64,512]{2,1,0:T(8,128)S(1)}, f32[1,64,512]{2,1,0:T(8,128)S(1)}, u32[]{:S(2)}, u32[]{:S(2)}) collective-permute-start(f32[1,64,512]{2,1,0:T(8,128)S(1)} %get-tuple-element.20), channel_id=1, source_target_pairs={{0,9},{3,12},{6,15},{9,18},{12,21},{15,0},{18,3},{21,6},{1,10},{4,... | collective-permute-start | bytes 393224 | tf_op jit(solution)/shard_map/ppermute | solution.py:61
